TPU v7x, 128 devices: a whole 4x4x4 slice. The times are simulated.
128 devices in a mesh: row: 8 (over x, core), col: 16 (over z, y).
Axes of the slice: x: 4, y: 4, z: 4, core: 2. Of those that a mesh axis runs over, the one named last changes fastest.
Arguments:
- basis: bfloat16 [32768, 256], P(('row', 'col')), may hold values from -6 to 6
- degree_scale: float32 [32768], P(('row', 'col')), may hold values from 0.5 to 3
- tile_data: bfloat16 [256, 16, 8, 128, 128], P('row', 'col'), may hold values from -0.09375 to 0.09375
- tile_index: int32 [256, 16, 8], P('row', 'col'), may hold values from 0 to 15, as said below
- tile_count: int32 [256, 16], P('row', 'col'), may hold values from 1 to 8, as said below
Outputs:
- embedding: float32 [32768, 256], P(('row', 'col'))
- factor: float32 [256, 256], replicated
Inputs may be any that keep to these rules, and one draw needn't show every extreme that they name: `tile_index`: all 8 entries of one tile row in one column block are distinct. `tile_count`: some tile row has 8 live slots in every draw; loads differ widely between devices.
All inputs are finite; a program needn't handle non-finite values.
Results may differ from a plain program's by a relative error of at most 0.034.
Values may be sent and summed in bfloat16 or wider, within the bound.
No kernel may reach another device: no remote copies, remote signals or barrier semaphores. Data moves between devices by JAX's collectives and lax.ppermute only.
A program may use at most 128 MiB of HBM per device.

v0:
```python
import jax
import jax.numpy as jnp
from jax import lax
from jax.sharding import PartitionSpec as P

ITERS = 4


def gram_of(image, nodes):
    return (
        lax.dot_general(
            image,
            image,
            (((0,), (0,)), ((), ())),
            precision=lax.Precision.HIGHEST,
            preferred_element_type=jnp.float32,
        )
        / nodes
    )


def normalize(image, gram):
    lower = jnp.linalg.cholesky(gram)
    solved = jax.scipy.linalg.solve_triangular(lower, image.T, lower=True).T
    return (solved, lower.T)


def body(basis, degree_scale, tile_data, tile_index, tile_count):
    tiles = tile_data[:, 0]
    index = tile_index[:, 0]
    counts = tile_count[:, 0]
    rows_dev, width = basis.shape
    tile = tiles.shape[-1]
    slots = tiles.shape[1]
    nodes = rows_dev * lax.axis_size("row") * lax.axis_size("col")
    live = jnp.arange(slots)[None, :] < counts[:, None]
    scale = degree_scale[:, None]
    probe = (basis.astype(jnp.float32) * scale).astype(jnp.bfloat16)
    current = probe
    embedding = None
    factor = None
    for step in range(ITERS):
        block_basis = lax.all_gather(current, "row", axis=0, tiled=True)
        tiled = block_basis.reshape(-1, tile, width)
        number = lax.axis_size("col") * rows_dev // tile
        chosen = jnp.where(live[:, :, None, None], tiled[index], jnp.zeros((), jnp.bfloat16))
        result = lax.dot_general(
            tiles, chosen, (((1, 3), (1, 2)), ((0,), (0,))), preferred_element_type=jnp.float32
        )
        summed = lax.psum_scatter(
            result.reshape(number * tile, width).astype(jnp.bfloat16),
            "col",
            scatter_dimension=0,
            tiled=True,
        ).astype(jnp.float32)
        image = summed * scale
        gram = lax.psum(gram_of(image, nodes), ("row", "col"))
        embedding, factor = normalize(image, gram)
        current = (embedding * scale).astype(jnp.bfloat16)
    return (embedding, factor)


def solution(mesh):
    placed = (
        P(("row", "col"), None),
        P(("row", "col")),
        P("row", "col", None, None, None),
        P("row", "col", None),
        P("row", "col"),
    )
    return jax.shard_map(
        body, mesh=mesh, in_specs=placed, out_specs=(P(("row", "col"), None), P()), check_vma=False
    )
```

profile of v0, /device:TPU:1, one launch (start us, length us, event | category | flops | bytes accessed | tf_op | source)
XLA Modules:
  0.0 1355.3 jit_solution(647993125058810786)
XLA Ops:
  10.6 26.5 %all-gather.5.cloned.1.call-done = bf16[2048,256]{1,0:T(8,128)(2,1)} async-done(((bf16[256,256]{1,0:T(8,128)(2,1)}), bf16[2048,256]{1,0:T(8,128)(2,1)}) %all-gather.5.cloned.1.call-update) | async-done | bytes 1048592 | tf_op jit(solution)/shard_map/all_gather | solution.py:43
  48.0 12.7 bitcast_convert_fusion.3
  60.8 73.4 %reduce-scatter.5.cloned.1.call-done = bf16[256,256]{1,0:T(8,128)(2,1)} async-done(((bf16[4096,256]{1,0:T(8,128)(2,1)}), bf16[256,256]{1,0:T(8,128)(2,1)}) %reduce-scatter.5.cloned.1.call-update) | async-done | bytes 131088 | tf_op jit(solution)/shard_map/reduce_scatter | solution.py:50
  138.1 145.3 %all-reduce.6.cloned.1.call-done = f32[256,256]{0,1:T(8,128)} async-done(((f32[256,256]{0,1:T(8,128)}), f32[256,256]{0,1:T(8,128)}) %all-reduce.6.cloned.1.call-update) | async-done | bytes 262160 | tf_op jit(solution)/shard_map/psum | solution.py:57
  307.6 11.7 cholesky.231
  325.9 19.7 %custom-call.18 = f32[2,128,128]{1,2,0:T(8,128)S(1)} custom-call(f32[2,128,128]{2,1,0:T(8,128)S(1)} %get-tuple-element.30), custom_call_target="InvertDiagBlocksLowerTriangular" | custom-call | tf_op jit(solution)/shard_map/jit(_solve_triangular)/triangular_solve | solution.py:24
  347.3 21.1 %all-gather.7.cloned.1.call-done = bf16[2048,256]{0,1:T(8,128)(2,1)} async-done(((bf16[256,256]{0,1:T(8,128)(2,1)}), bf16[2048,256]{0,1:T(8,128)(2,1)}) %all-gather.7.cloned.1.call-update) | async-done | bytes 1048592 | tf_op jit(solution)/shard_map/all_gather | solution.py:43
  379.7 12.6 bitcast_convert_fusion.2
  392.4 74.5 %reduce-scatter.7.cloned.1.call-done = bf16[256,256]{1,0:T(8,128)(2,1)} async-done(((bf16[4096,256]{1,0:T(8,128)(2,1)}), bf16[256,256]{1,0:T(8,128)(2,1)}) %reduce-scatter.7.cloned.1.call-update) | async-done | bytes 131088 | tf_op jit(solution)/shard_map/reduce_scatter | solution.py:50
  470.5 145.5 %all-reduce.8.cloned.1.call-done = f32[256,256]{0,1:T(8,128)} async-done(((f32[256,256]{0,1:T(8,128)}), f32[256,256]{0,1:T(8,128)}) %all-reduce.8.cloned.1.call-update) | async-done | bytes 262160 | tf_op jit(solution)/shard_map/psum | solution.py:57
  640.2 11.7 cholesky.265
  659.2 19.7 %custom-call.20 = f32[2,128,128]{1,2,0:T(8,128)S(1)} custom-call(f32[2,128,128]{2,1,0:T(8,128)S(1)} %get-tuple-element.31), custom_call_target="InvertDiagBlocksLowerTriangular" | custom-call | tf_op jit(solution)/shard_map/jit(_solve_triangular)/triangular_solve | solution.py:24
  680.7 21.1 %all-gather.9.cloned.1.call-done = bf16[2048,256]{0,1:T(8,128)(2,1)} async-done(((bf16[256,256]{0,1:T(8,128)(2,1)}), bf16[2048,256]{0,1:T(8,128)(2,1)}) %all-gather.9.cloned.1.call-update) | async-done | bytes 1048592 | tf_op jit(solution)/shard_map/all_gather | solution.py:43
  713.0 12.6 bitcast_convert_fusion.1
  725.7 74.3 %reduce-scatter.9.cloned.1.call-done = bf16[256,256]{1,0:T(8,128)(2,1)} async-done(((bf16[4096,256]{1,0:T(8,128)(2,1)}), bf16[256,256]{1,0:T(8,128)(2,1)}) %reduce-scatter.9.cloned.1.call-update) | async-done | bytes 131088 | tf_op jit(solution)/shard_map/reduce_scatter | solution.py:50
  803.7 145.7 %all-reduce.10.cloned.1.call-done = f32[256,256]{0,1:T(8,128)} async-done(((f32[256,256]{0,1:T(8,128)}), f32[256,256]{0,1:T(8,128)}) %all-reduce.10.cloned.1.call-update) | async-done | bytes 262160 | tf_op jit(solution)/shard_map/psum | solution.py:57
  973.6 11.7 cholesky.299
  992.4 19.7 %custom-call.22 = f32[2,128,128]{1,2,0:T(8,128)S(1)} custom-call(f32[2,128,128]{2,1,0:T(8,128)S(1)} %get-tuple-element.32), custom_call_target="InvertDiagBlocksLowerTriangular" | custom-call | tf_op jit(solution)/shard_map/jit(_solve_triangular)/triangular_solve | solution.py:24
  1013.9 21.1 %all-gather.11.cloned.1.call-done = bf16[2048,256]{0,1:T(8,128)(2,1)} async-done(((bf16[256,256]{0,1:T(8,128)(2,1)}), bf16[2048,256]{0,1:T(8,128)(2,1)}) %all-gather.11.cloned.1.call-update) | async-done | bytes 1048592 | tf_op jit(solution)/shard_map/all_gather | solution.py:43
  1046.2 12.6 bitcast_convert_fusion
  1059.2 74.1 %reduce-scatter.11.cloned.1.call-done = bf16[256,256]{1,0:T(8,128)(2,1)} async-done(((bf16[4096,256]{1,0:T(8,128)(2,1)}), bf16[256,256]{1,0:T(8,128)(2,1)}) %reduce-scatter.11.cloned.1.call-update) | async-done | bytes 131088 | tf_op jit(solution)/shard_map/reduce_scatter | solution.py:50
  1136.7 145.8 %all-reduce.12.cloned.1.call-done = f32[256,256]{0,1:T(8,128)} async-done(((f32[256,256]{0,1:T(8,128)}), f32[256,256]{0,1:T(8,128)}) %all-reduce.12.cloned.1.call-update) | async-done | bytes 262160 | tf_op jit(solution)/shard_map/psum | solution.py:57
  1306.7 11.7 cholesky.333
  1325.6 19.7 %custom-call.24 = f32[2,128,128]{1,2,0:T(8,128)S(1)} custom-call(f32[2,128,128]{2,1,0:T(8,128)S(1)} %get-tuple-element.33), custom_call_target="InvertDiagBlocksLowerTriangular" | custom-call | tf_op jit(solution)/shard_map/jit(_solve_triangular)/triangular_solve | solution.py:24
  (150 shorter events, 206.3 us)
Async XLA Ops:
  7.2 29.9 %all-gather.5.cloned.1.call-start = ((), (), s32[]{:S(2)}) async-start(), calls=%async_computation.4 | async-start | bytes 1179648 | tf_op jit(solution)/shard_map/all_gather | solution.py:43
  8.9 125.2 %reduce-scatter.5.cloned.1.call-start = ((), (), s32[]{:S(2)}) async-start(), calls=%async_computation.5 | async-start | bytes 2228224 | tf_op jit(solution)/shard_map/reduce_scatter | solution.py:50
  48.0 86.1 %copy-start = (f32[256]{0:T(256)S(1)}, f32[256]{0:T(256)}, u32[]{:S(2)}) copy-start(f32[256]{0:T(256)} %param.9) | copy-start | bytes 3076
  60.7 222.8 %all-reduce.6.cloned.1.call-start = ((), (), s32[]{:S(2)}) async-start(), calls=%async_computation.6 | async-start | bytes 524288 | tf_op jit(solution)/shard_map/psum | solution.py:57
  136.5 231.9 %all-gather.7.cloned.1.call-start = ((), (), s32[]{:S(2)}) async-start(), calls=%async_computation.7 | async-start | bytes 1179648 | tf_op jit(solution)/shard_map/all_gather | solution.py:43
  347.3 119.6 %reduce-scatter.7.cloned.1.call-start = ((), (), s32[]{:S(2)}) async-start(), calls=%async_computation.8 | async-start | bytes 2228224 | tf_op jit(solution)/shard_map/reduce_scatter | solution.py:50
  392.3 223.7 %all-reduce.8.cloned.1.call-start = ((), (), s32[]{:S(2)}) async-start(), calls=%async_computation.9 | async-start | bytes 524288 | tf_op jit(solution)/shard_map/psum | solution.py:57
  469.3 232.6 %all-gather.9.cloned.1.call-start = ((), (), s32[]{:S(2)}) async-start(), calls=%async_computation.10 | async-start | bytes 1179648 | tf_op jit(solution)/shard_map/all_gather | solution.py:43
  680.6 119.5 %reduce-scatter.9.cloned.1.call-start = ((), (), s32[]{:S(2)}) async-start(), calls=%async_computation.11 | async-start | bytes 2228224 | tf_op jit(solution)/shard_map/reduce_scatter | solution.py:50
  725.7 223.8 %all-reduce.10.cloned.1.call-start = ((), (), s32[]{:S(2)}) async-start(), calls=%async_computation.12 | async-start | bytes 524288 | tf_op jit(solution)/shard_map/psum | solution.py:57
  802.5 232.5 %all-gather.11.cloned.1.call-start = ((), (), s32[]{:S(2)}) async-start(), calls=%async_computation.13 | async-start | bytes 1179648 | tf_op jit(solution)/shard_map/all_gather | solution.py:43
  1013.8 119.5 %reduce-scatter.11.cloned.1.call-start = ((), (), s32[]{:S(2)}) async-start(), calls=%async_computation.14 | async-start | bytes 2228224 | tf_op jit(solution)/shard_map/reduce_scatter | solution.py:50
  1058.9 223.6 %all-reduce.12.cloned.1.call-start = ((), (), s32[]{:S(2)}) async-start(), calls=%async_computation.15 | async-start | bytes 524288 | tf_op jit(solution)/shard_map/psum | solution.py:57
Sparse Core Ops, SparseCore 0:
  10.3 26.7 all-gather.4
  60.8 73.2 reduce-scatter.4
  139.5 143.9 all-reduce.5
  347.4 21.0 all-gather.6
  392.5 74.3 reduce-scatter.6
  472.0 143.9 all-reduce.7
  680.8 21.0 all-gather.8
  725.8 74.2 reduce-scatter.8
  805.4 143.9 all-reduce.9
  1014.0 21.0 all-gather.10
  1059.0 74.2 reduce-scatter.10
  1138.5 143.9 all-reduce.11
where the time goes:
time: 1360 us
  waiting for transfers between devices  969 us (71%)
  other arithmetic  230 us (17%)
  local copies, waits for them, and re-layouts  67.1 us (5%)
  matrix products  66.1 us (5%)
  between operations  20.5 us (2%)
    psum x4, waiting for transfers between devices, body(): gram = lax.psum(gram_of(image, nodes), ('row', 'col'))  582 us
    reduce_scatter x4, waiting for transfers between devices, body(): lax.psum_scatter(result.reshape(number * tile, width).astype(jnp.bfloat16...  296 us
    another operation x27, other arithmetic, normalize(): lower = jnp.linalg.cholesky(gram)  138 us
    all_gather x4, waiting for transfers between devices, body(): block_basis = lax.all_gather(current, 'row', axis=0, tiled=True)  90 us
    another operation x8, other arithmetic, normalize(): solved = jax.scipy.linalg.solve_triangular(lower, image.T, lower=True).T  78.8 us
    dot_general x4, matrix products, body(): lax.dot_general(tiles, chosen, (((1, 3), (1, 2)), ((0,), (0,))), preferre...  50.6 us
    gather x4, local copies, waits for them, and re-layouts, body(): tiled[index]  40.1 us
  transfers between devices with their start and end apart: 12, of which 12 were waited for; matrix products, arithmetic and copies ran while one was open for 0% of the time, Pallas kernels for 0%

commit v1 on v0

--- a/solution.py
+++ b/solution.py
@@ -25,6 +25,27 @@
     return (solved, lower.T)
 
 
+def gather_rows(x, axis):
+    n = lax.axis_size(axis)
+    got = lax.all_to_all(jnp.broadcast_to(x, (n,) + x.shape), axis, 0, 0, tiled=False)
+    return got.reshape((-1,) + x.shape[1:])
+
+
+def sum_scatter_rows(x, axis):
+    n = lax.axis_size(axis)
+    got = lax.all_to_all(x.reshape((n, -1) + x.shape[1:]), axis, 0, 0, tiled=False)
+    return jnp.sum(got.astype(jnp.float32), axis=0)
+
+
+def sum_all(x, axes):
+    n = 1
+    for a in axes:
+        n *= lax.axis_size(a)
+    piece = jnp.sum(lax.all_to_all(x.reshape(n, -1), axes, 0, 0, tiled=False), axis=0)
+    full = lax.all_to_all(jnp.broadcast_to(piece, (n,) + piece.shape), axes, 0, 0, tiled=False)
+    return full.reshape(x.shape)
+
+
 def body(basis, degree_scale, tile_data, tile_index, tile_count):
     tiles = tile_data[:, 0]
     index = tile_index[:, 0]
@@ -40,21 +61,16 @@
     embedding = None
     factor = None
     for step in range(ITERS):
-        block_basis = lax.all_gather(current, "row", axis=0, tiled=True)
+        block_basis = gather_rows(current, "row")
         tiled = block_basis.reshape(-1, tile, width)
         number = lax.axis_size("col") * rows_dev // tile
         chosen = jnp.where(live[:, :, None, None], tiled[index], jnp.zeros((), jnp.bfloat16))
         result = lax.dot_general(
             tiles, chosen, (((1, 3), (1, 2)), ((0,), (0,))), preferred_element_type=jnp.float32
         )
-        summed = lax.psum_scatter(
-            result.reshape(number * tile, width).astype(jnp.bfloat16),
-            "col",
-            scatter_dimension=0,
-            tiled=True,
-        ).astype(jnp.float32)
+        summed = sum_scatter_rows(result.reshape(number * tile, width).astype(jnp.bfloat16), "col")
         image = summed * scale
-        gram = lax.psum(gram_of(image, nodes), ("row", "col"))
+        gram = sum_all(gram_of(image, nodes), ("row", "col"))
         embedding, factor = normalize(image, gram)
         current = (embedding * scale).astype(jnp.bfloat16)
     return (embedding, factor)

time: 1360 us -> 682 us (0.50)
  waiting for transfers between devices: 969 us -> 70.2 us
  blocking collectives: 0 us -> 228 us
  starting transfers between devices: 1.66 us -> 28.9 us
  matrix products: 66.1 us -> 52.3 us
  between operations: 20.5 us -> 6.9 us
    psum x4 -> x0, waiting for transfers between devices: 582 us -> none  [body(): gram = lax.psum(gram_of(image, nodes), ('row', 'col'))]
    reduce_scatter x4 -> x0, waiting for transfers between devices: 296 us -> none  [body(): lax.psum_scatter(result.reshape(number * tile, width).astype(jnp.bfloat16...]
    all_to_all x0 -> x10, blocking collectives: none -> 228 us  [the longest x4 124 us: sum_scatter_rows(): lax.all_to_all(x.reshape((n, -1) + x.shape[1:]), axis, 0, 0, tiled=False)]
    all_gather x4 -> x0, waiting for transfers between devices: 90 us -> none  [body(): block_basis = lax.all_gather(current, 'row', axis=0, tiled=True)]
    all_to_all x0 -> x6, waiting for transfers between devices: none -> 70.2 us  [the longest x4 45.3 us: sum_all(): lax.all_to_all(jnp.broadcast_to(piece, (n,) + piece.shape), axes, 0, 0, t...]
    all_to_all x0 -> x6, starting transfers between devices: none -> 28.9 us  [the longest x4 17.6 us: sum_all(): lax.all_to_all(jnp.broadcast_to(piece, (n,) + piece.shape), axes, 0, 0, t...]
  transfers between devices with their start and end apart: 12 -> 6, of which waited for: 12 -> 6; matrix products, arithmetic and copies ran while one was open for 0% -> 0% of each run, Pallas kernels for 0% -> 0%
where the time goes in v1:
time: 682 us; the launch traced here: 676 us
  blocking collectives  228 us (33%)
  other arithmetic  225 us (33%)
  waiting for transfers between devices  70.2 us (10%)
  local copies, waits for them, and re-layouts  65.2 us (10%)
  matrix products  52.3 us (8%)
  starting transfers between devices  28.9 us (4%)
  between operations  6.9 us (1%)
    another operation x27, other arithmetic, normalize(): lower = jnp.linalg.cholesky(gram)  138 us
    all_to_all x4, blocking collectives, sum_scatter_rows(): lax.all_to_all(x.reshape((n, -1) + x.shape[1:]), axis, 0, 0, tiled=False)  124 us
    another operation x8, other arithmetic, normalize(): solved = jax.scipy.linalg.solve_triangular(lower, image.T, lower=True).T  79.9 us
    all_to_all x3, blocking collectives, gather_rows(): lax.all_to_all(jnp.broadcast_to(x, (n,) + x.shape), axis, 0, 0, tiled=False)  53.6 us
    all_to_all x3, blocking collectives, sum_all(): lax.all_to_all(x.reshape(n, -1), axes, 0, 0, tiled=False)  50 us
    all_to_all x4, waiting for transfers between devices, sum_all(): lax.all_to_all(jnp.broadcast_to(piece, (n,) + piece.shape), axes, 0, 0, t...  45.3 us
    dot_general x4, matrix products, body(): lax.dot_general(tiles, chosen, (((1, 3), (1, 2)), ((0,), (0,))), preferre...  45.3 us
    gather x4, local copies, waits for them, and re-layouts, body(): tiled[index]  38.7 us
  transfers between devices with their start and end apart: 6, of which 6 were waited for; matrix products, arithmetic and copies ran while one was open for 0% of the time, Pallas kernels for 0%

profile of v1, /device:TPU:1, one launch (start us, length us, event | category | flops | bytes accessed | tf_op | source)
XLA Modules:
  0.0 676.3 jit_solution(10934031457987659948)
XLA Ops:
  10.9 13.4 %all-to-all-done = bf16[8,256,256]{2,1,0:T(8,128)(2,1)S(1)} async-done(((bf16[8,256,256]{2,1,0:T(8,128)(2,1)}), bf16[8,256,256]{2,1,0:T(8,128)(2,1)S(1)}, u32[]{:S(2)}, u32[]{:S(2)}) %all-to-all-start) | async-done | bytes 1048608 | tf_op jit(solution)/shard_map/all_to_all | solution.py:30
  45.3 34.8 %all_to_all.104 = bf16[16,256,256]{2,1,0:T(8,128)(2,1)S(1)} all-to-all(bf16[16,256,256]{2,1,0:T(8,128)(2,1)S(1)} %bitcast.205), channel_id=1, replica_groups=mesh['row'=8,'col'=16] {'col'}, dimensions={0} | all-to-all | bytes 4194304 | tf_op jit(solution)/shard_map/all_to_all | solution.py:36
  87.4 11.6 %all-to-all-done.2 = f32[128,1,512]{2,1,0:T(1,128)S(1)} async-done(((f32[128,1,512]{2,1,0:T(1,128)}), f32[128,1,512]{2,1,0:T(1,128)S(1)}, u32[]{:S(2)}, u32[]{:S(2)}) %all-to-all-start.2) | async-done | bytes 262176 | tf_op jit(solution)/shard_map/all_to_all | solution.py:44
  116.9 11.7 %cholesky.214 = f32[128,128]{1,0:T(8,128)S(1)} custom-call(f32[128,128]{1,0:T(8,128)S(1)} %cholesky.346), custom_call_target="Cholesky" | custom-call | tf_op jit(solution)/shard_map/jit(cholesky)/cholesky | solution.py:23
  139.0 11.7 %cholesky.231 = f32[128,128]{1,0:T(8,128)S(1)} custom-call(f32[128,128]{1,0:T(8,128)S(1)} %convolution_subtract_fusion.7), custom_call_target="Cholesky" | custom-call | tf_op jit(solution)/shard_map/jit(cholesky)/cholesky | solution.py:23
  156.6 19.8 %custom-call.18 = f32[2,128,128]{1,2,0:T(8,128)S(1)} custom-call(f32[2,128,128]{2,1,0:T(8,128)S(1)} %get-tuple-element.30), custom_call_target="InvertDiagBlocksLowerTriangular" | custom-call | tf_op jit(solution)/shard_map/jit(_solve_triangular)/triangular_solve | solution.py:24
  177.5 17.9 %all_to_all.105 = bf16[8,256,256]{2,1,0:T(8,128)(2,1)S(1)} all-to-all(bf16[8,256,256]{2,1,0:T(8,128)(2,1)S(1)} %broadcast_in_dim.63), channel_id=1, replica_groups=mesh['row'=8,'col'=16] {'row'}, dimensions={0} | all-to-all | bytes 2097152 | tf_op jit(solution)/shard_map/all_to_all | solution.py:30
  216.4 29.8 %all_to_all.106 = bf16[16,256,256]{2,1,0:T(8,128)(2,1)S(1)} all-to-all(bf16[16,256,256]{2,1,0:T(8,128)(2,1)S(1)} %bitcast.206), channel_id=1, replica_groups=mesh['row'=8,'col'=16] {'col'}, dimensions={0} | all-to-all | bytes 4194304 | tf_op jit(solution)/shard_map/all_to_all | solution.py:36
  247.4 16.7 %all_to_all.111 = f32[128,1,512]{2,1,0:T(1,128)S(1)} all-to-all(f32[128,1,512]{2,1,0:T(1,128)S(1)} %all_to_all.85), channel_id=1, replica_groups=mesh['row'=8,'col'=16] {'row','col'}, dimensions={0} | all-to-all | bytes 524288 | tf_op jit(solution)/shard_map/all_to_all | solution.py:44
  281.7 11.7 %cholesky.248 = f32[128,128]{1,0:T(8,128)S(1)} custom-call(f32[128,128]{1,0:T(8,128)S(1)} %cholesky.349), custom_call_target="Cholesky" | custom-call | tf_op jit(solution)/shard_map/jit(cholesky)/cholesky | solution.py:23
  303.7 11.7 %cholesky.265 = f32[128,128]{1,0:T(8,128)S(1)} custom-call(f32[128,128]{1,0:T(8,128)S(1)} %convolution_subtract_fusion.6), custom_call_target="Cholesky" | custom-call | tf_op jit(solution)/shard_map/jit(cholesky)/cholesky | solution.py:23
  321.8 20.1 %custom-call.20 = f32[2,128,128]{1,2,0:T(8,128)S(1)} custom-call(f32[2,128,128]{2,1,0:T(8,128)S(1)} %get-tuple-element.31), custom_call_target="InvertDiagBlocksLowerTriangular" | custom-call | tf_op jit(solution)/shard_map/jit(_solve_triangular)/triangular_solve | solution.py:24
  343.0 17.9 %all_to_all.107 = bf16[8,256,256]{2,1,0:T(8,128)(2,1)S(1)} all-to-all(bf16[8,256,256]{2,1,0:T(8,128)(2,1)S(1)} %broadcast_in_dim.65), channel_id=1, replica_groups=mesh['row'=8,'col'=16] {'row'}, dimensions={0} | all-to-all | bytes 2097152 | tf_op jit(solution)/shard_map/all_to_all | solution.py:30
  381.9 29.9 %all_to_all.108 = bf16[16,256,256]{2,1,0:T(8,128)(2,1)S(1)} all-to-all(bf16[16,256,256]{2,1,0:T(8,128)(2,1)S(1)} %bitcast.207), channel_id=1, replica_groups=mesh['row'=8,'col'=16] {'col'}, dimensions={0} | all-to-all | bytes 4194304 | tf_op jit(solution)/shard_map/all_to_all | solution.py:36
  412.9 16.6 %all_to_all.112 = f32[128,1,512]{2,1,0:T(1,128)S(1)} all-to-all(f32[128,1,512]{2,1,0:T(1,128)S(1)} %all_to_all.86), channel_id=1, replica_groups=mesh['row'=8,'col'=16] {'row','col'}, dimensions={0} | all-to-all | bytes 524288 | tf_op jit(solution)/shard_map/all_to_all | solution.py:44
  447.1 11.7 %cholesky.282 = f32[128,128]{1,0:T(8,128)S(1)} custom-call(f32[128,128]{1,0:T(8,128)S(1)} %cholesky.352), custom_call_target="Cholesky" | custom-call | tf_op jit(solution)/shard_map/jit(cholesky)/cholesky | solution.py:23
  469.2 11.7 %cholesky.299 = f32[128,128]{1,0:T(8,128)S(1)} custom-call(f32[128,128]{1,0:T(8,128)S(1)} %convolution_subtract_fusion.5), custom_call_target="Cholesky" | custom-call | tf_op jit(solution)/shard_map/jit(cholesky)/cholesky | solution.py:23
  487.3 19.9 %custom-call.22 = f32[2,128,128]{1,2,0:T(8,128)S(1)} custom-call(f32[2,128,128]{2,1,0:T(8,128)S(1)} %get-tuple-element.32), custom_call_target="InvertDiagBlocksLowerTriangular" | custom-call | tf_op jit(solution)/shard_map/jit(_solve_triangular)/triangular_solve | solution.py:24
  508.3 17.9 %all_to_all.109 = bf16[8,256,256]{2,1,0:T(8,128)(2,1)S(1)} all-to-all(bf16[8,256,256]{2,1,0:T(8,128)(2,1)S(1)} %broadcast_in_dim.67), channel_id=1, replica_groups=mesh['row'=8,'col'=16] {'row'}, dimensions={0} | all-to-all | bytes 2097152 | tf_op jit(solution)/shard_map/all_to_all | solution.py:30
  547.2 29.9 %all_to_all.110 = bf16[16,256,256]{2,1,0:T(8,128)(2,1)S(1)} all-to-all(bf16[16,256,256]{2,1,0:T(8,128)(2,1)S(1)} %bitcast.204), channel_id=1, replica_groups=mesh['row'=8,'col'=16] {'col'}, dimensions={0} | all-to-all | bytes 4194304 | tf_op jit(solution)/shard_map/all_to_all | solution.py:36
  578.2 16.7 %all_to_all.113 = f32[128,1,512]{2,1,0:T(1,128)S(1)} all-to-all(f32[128,1,512]{2,1,0:T(1,128)S(1)} %all_to_all.87), channel_id=1, replica_groups=mesh['row'=8,'col'=16] {'row','col'}, dimensions={0} | all-to-all | bytes 524288 | tf_op jit(solution)/shard_map/all_to_all | solution.py:44
  612.5 11.7 %cholesky.316 = f32[128,128]{1,0:T(8,128)S(1)} custom-call(f32[128,128]{1,0:T(8,128)S(1)} %cholesky.355), custom_call_target="Cholesky" | custom-call | tf_op jit(solution)/shard_map/jit(cholesky)/cholesky | solution.py:23
  634.6 11.7 %cholesky.333 = f32[128,128]{1,0:T(8,128)S(1)} custom-call(f32[128,128]{1,0:T(8,128)S(1)} %convolution_subtract_fusion.4), custom_call_target="Cholesky" | custom-call | tf_op jit(solution)/shard_map/jit(cholesky)/cholesky | solution.py:23
  653.2 20.0 %custom-call.24 = f32[2,128,128]{1,2,0:T(8,128)S(1)} custom-call(f32[2,128,128]{2,1,0:T(8,128)S(1)} %get-tuple-element.33), custom_call_target="InvertDiagBlocksLowerTriangular" | custom-call | tf_op jit(solution)/shard_map/jit(_solve_triangular)/triangular_solve | solution.py:24
  (170 shorter events, 258.3 us)
Async XLA Ops:
  3.5 20.8 %all-to-all-start = ((bf16[8,256,256]{2,1,0:T(8,128)(2,1)}), bf16[8,256,256]{2,1,0:T(8,128)(2,1)S(1)}, u32[]{:S(2)}, u32[]{:S(2)}) async-start(bf16[8,256,256]{2,1,0:T(8,128)(2,1)} %broadcast_in_dim.60), calls=%async_computation | async-start | bytes 2097152 | tf_op jit(solution)/shard_map/all_to_all | solution.py:30
  34.0 46.6 %copy-start = (f32[256]{0:T(256)S(1)}, f32[256]{0:T(256)}, u32[]{:S(2)}) copy-start(f32[256]{0:T(256)} %param.9) | copy-start | bytes 3076
  81.9 17.1 %all-to-all-start.2 = ((f32[128,1,512]{2,1,0:T(1,128)}), f32[128,1,512]{2,1,0:T(1,128)S(1)}, u32[]{:S(2)}, u32[]{:S(2)}) async-start(f32[128,1,512]{2,1,0:T(1,128)} %all_to_all.84), calls=%async_computation.2 | async-start | bytes 524288 | tf_op jit(solution)/shard_map/all_to_all | solution.py:44
  100.1 16.0 %all-to-all-start.3 = ((f32[128,1,512]{2,1,0:T(1,128)}), f32[128,1,512]{2,1,0:T(1,128)S(1)}, u32[]{:S(2)}, u32[]{:S(2)}) async-start(f32[128,1,512]{2,1,0:T(1,128)} %broadcast_in_dim.62), calls=%async_computation.3 | async-start | bytes 524288 | tf_op jit(solution)/shard_map/all_to_all | solution.py:45
  265.1 15.7 %all-to-all-start.7 = ((f32[128,1,512]{2,1,0:T(1,128)}), f32[128,1,512]{2,1,0:T(1,128)S(1)}, u32[]{:S(2)}, u32[]{:S(2)}) async-start(f32[128,1,512]{2,1,0:T(1,128)} %broadcast_in_dim.64), calls=%async_computation.7 | async-start | bytes 524288 | tf_op jit(solution)/shard_map/all_to_all | solution.py:45
  430.6 15.6 %all-to-all-start.11 = ((f32[128,1,512]{2,1,0:T(1,128)}), f32[128,1,512]{2,1,0:T(1,128)S(1)}, u32[]{:S(2)}, u32[]{:S(2)}) async-start(f32[128,1,512]{2,1,0:T(1,128)} %broadcast_in_dim.66), calls=%async_computation.11 | async-start | bytes 524288 | tf_op jit(solution)/shard_map/all_to_all | solution.py:45
  595.9 15.7 %all-to-all-start.15 = ((f32[128,1,512]{2,1,0:T(1,128)}), f32[128,1,512]{2,1,0:T(1,128)S(1)}, u32[]{:S(2)}, u32[]{:S(2)}) async-start(f32[128,1,512]{2,1,0:T(1,128)} %broadcast_in_dim.68), calls=%async_computation.15 | async-start | bytes 524288 | tf_op jit(solution)/shard_map/all_to_all | solution.py:45

commit v2 on v1

--- a/solution.py
+++ b/solution.py
@@ -19,10 +19,31 @@
     )
 
 
+def dot_hi(a, b):
+    return jnp.dot(a, b, precision=lax.Precision.HIGHEST, preferred_element_type=jnp.float32)
+
+
+def cholesky_and_inverse(g, leaf=128):
+    n = g.shape[0]
+    if n <= leaf:
+        lower = jnp.linalg.cholesky(g)
+        eye = jnp.eye(n, dtype=jnp.float32)
+        return lower, jax.scipy.linalg.solve_triangular(lower, eye, lower=True)
+    h = n // 2
+    l11, i11 = cholesky_and_inverse(g[:h, :h], leaf)
+    l21 = dot_hi(g[h:, :h], i11.T)
+    l22, i22 = cholesky_and_inverse(g[h:, h:] - dot_hi(l21, l21.T), leaf)
+    i21 = -dot_hi(i22, dot_hi(l21, i11))
+    zero = jnp.zeros((h, n - h), jnp.float32)
+    lower = jnp.block([[l11, zero], [l21, l22]])
+    inverse = jnp.block([[i11, zero], [i21, i22]])
+    return lower, inverse
+
+
 def normalize(image, gram):
-    lower = jnp.linalg.cholesky(gram)
-    solved = jax.scipy.linalg.solve_triangular(lower, image.T, lower=True).T
-    return (solved, lower.T)
+    gram = (gram + gram.T) * 0.5
+    lower, inverse = cholesky_and_inverse(gram)
+    return (dot_hi(image, inverse.T), lower.T)
 
 
 def gather_rows(x, axis):
@@ -57,13 +78,11 @@
     live = jnp.arange(slots)[None, :] < counts[:, None]
     scale = degree_scale[:, None]
     probe = (basis.astype(jnp.float32) * scale).astype(jnp.bfloat16)
-    current = probe
-    embedding = None
-    factor = None
-    for step in range(ITERS):
+    number = lax.axis_size("col") * rows_dev // tile
+
+    def one_step(current):
         block_basis = gather_rows(current, "row")
         tiled = block_basis.reshape(-1, tile, width)
-        number = lax.axis_size("col") * rows_dev // tile
         chosen = jnp.where(live[:, :, None, None], tiled[index], jnp.zeros((), jnp.bfloat16))
         result = lax.dot_general(
             tiles, chosen, (((1, 3), (1, 2)), ((0,), (0,))), preferred_element_type=jnp.float32
@@ -71,8 +90,18 @@
         summed = sum_scatter_rows(result.reshape(number * tile, width).astype(jnp.bfloat16), "col")
         image = summed * scale
         gram = sum_all(gram_of(image, nodes), ("row", "col"))
-        embedding, factor = normalize(image, gram)
-        current = (embedding * scale).astype(jnp.bfloat16)
+        return normalize(image, gram)
+
+    def loop_step(i, carry):
+        embedding, factor = one_step(carry[0])
+        return ((embedding * scale).astype(jnp.bfloat16), embedding, factor)
+
+    start = (probe, jnp.zeros(basis.shape, jnp.float32), jnp.zeros((width, width), jnp.float32))
+    _, embedding, factor = lax.fori_loop(0, ITERS, loop_step, start)
+    return (embedding, factor)
+
+    embedding, factor = one_step(probe)
+    embedding, factor = lax.fori_loop(1, ITERS, loop_step, (embedding, factor))
     return (embedding, factor)
 
 

time: 682 us -> 635 us (0.931)
  blocking collectives: 228 us -> 191 us
  waiting for transfers between devices: 70.2 us -> 103 us
  other arithmetic: 225 us -> 194 us
  local copies, waits for them, and re-layouts: 65.2 us -> 52.4 us
    all_to_all x3 -> x0, blocking collectives: 53.6 us -> none  [gather_rows(): lax.all_to_all(jnp.broadcast_to(x, (n,) + x.shape), axis, 0, 0, tiled=False)]
    all_to_all x1 -> x4, waiting for transfers between devices: 13.4 us -> 56.6 us  [gather_rows(): lax.all_to_all(jnp.broadcast_to(x, (n,) + x.shape), axis, 0, 0, tiled=False)]
    another operation x35 -> x42, other arithmetic: 218 us -> 183 us  [the longest x24 99.1 us: cholesky_and_inverse(): lower = jnp.linalg.cholesky(g)]
    all_to_all x3 -> x4, blocking collectives: 50 us -> 66.1 us  [sum_all(): lax.all_to_all(x.reshape(n, -1), axes, 0, 0, tiled=False)]
    another operation x37 -> x4, local copies, waits for them, and re-layouts: 15.6 us -> 0.35 us  [cholesky_and_inverse(): return (lower, jax.scipy.linalg.solve_triangular(lower, eye, lower=True))]
    all_to_all x1 -> x4, starting transfers between devices: 5.79 us -> 17.7 us  [gather_rows(): lax.all_to_all(jnp.broadcast_to(x, (n,) + x.shape), axis, 0, 0, tiled=False)]
    all_to_all x1 -> x0, waiting for transfers between devices: 11.6 us -> none  [sum_all(): lax.all_to_all(x.reshape(n, -1), axes, 0, 0, tiled=False)]
    dot_general x4 -> x24, matrix products: 45.3 us -> 54 us  [the longest x4 45.2 us: one_step(): lax.dot_general(tiles, chosen, (((1, 3), (1, 2)), ((0,), (0,))), preferre...]
  transfers between devices with their start and end apart: 6 -> 8, of which waited for: 6 -> 8; matrix products, arithmetic and copies ran while one was open for 0% -> 1% of each run, Pallas kernels for 0% -> 0%
where the time goes in v2:
time: 635 us; the launch traced here: 634 us
  other arithmetic  194 us (31%)
  blocking collectives  191 us (30%)
  waiting for transfers between devices  103 us (16%)
  matrix products  58.9 us (9%)
  local copies, waits for them, and re-layouts  52.4 us (8%)
  starting transfers between devices  33.7 us (5%)
    all_to_all x4, blocking collectives, sum_scatter_rows(): lax.all_to_all(x.reshape((n, -1) + x.shape[1:]), axis, 0, 0, tiled=False)  125 us
    another operation x24, other arithmetic, cholesky_and_inverse(): lower = jnp.linalg.cholesky(g)  99.1 us
    another operation x16, other arithmetic, cholesky_and_inverse(): return (lower, jax.scipy.linalg.solve_triangular(lower, eye, lower=True))  83.7 us
    all_to_all x4, blocking collectives, sum_all(): lax.all_to_all(x.reshape(n, -1), axes, 0, 0, tiled=False)  66.1 us
    all_to_all x4, waiting for transfers between devices, gather_rows(): lax.all_to_all(jnp.broadcast_to(x, (n,) + x.shape), axis, 0, 0, tiled=False)  56.6 us
    all_to_all x4, waiting for transfers between devices, sum_all(): lax.all_to_all(jnp.broadcast_to(piece, (n,) + piece.shape), axes, 0, 0, t...  45.9 us
    dot_general x4, matrix products, one_step(): lax.dot_general(tiles, chosen, (((1, 3), (1, 2)), ((0,), (0,))), preferre...  45.2 us
    gather x4, local copies, waits for them, and re-layouts, one_step(): tiled[index]  38.7 us
  transfers between devices with their start and end apart: 8, of which 8 were waited for; matrix products, arithmetic and copies ran while one was open for 1% of the time, Pallas kernels for 0%

profile of v2, /device:TPU:1, one launch (start us, length us, event | category | flops | bytes accessed | tf_op | source)
XLA Modules:
  0.0 634.2 jit_solution(12319939992281817614)
XLA Ops:
  2.4 630.0 %while.15 = (s32[]{:T(128)}, bf16[256,256]{1,0:T(8,128)(2,1)S(1)}, f32[256,256]{1,0:T(8,128)}, f32[256,256]{0,1:T(8,128)}, s32[32,8]{1,0:T(8,128)S(1)}, /*index=...) while((s32[]{:T(128)}, bf16[256,256]{1,0:T(8,128)(2,1)S(1)}, ...), condition=%wide.region_5.8_spmd.clone, body=%wide.region_0.0_spmd.clone.sunk | while | flops 2714044160 | bytes 80960336 | solution.py:100
  10.1 14.1 %all-to-all-done = bf16[8,256,256]{2,1,0:T(8,128)(2,1)S(1)} async-done(((bf16[8,256,256]{2,1,0:T(8,128)(2,1)}), bf16[8,256,256]{2,1,0:T(8,128)(2,1)S(1)}, u32[]{:S(2)}, u32[]{:S(2)}) %all-to-all-start) | async-done | bytes 1048608 | tf_op jit(solution)/shard_map/while/body/eval_jaxpr/all_to_all | solution.py:51
  45.3 34.9 %all_to_all.36 = bf16[16,256,256]{2,1,0:T(8,128)(2,1)S(1)} all-to-all(bf16[16,256,256]{2,1,0:T(8,128)(2,1)S(1)} %bitcast.95), channel_id=1, replica_groups=mesh['row'=8,'col'=16] {'col'}, dimensions={0} | all-to-all | bytes 4194304 | tf_op jit(solution)/shard_map/while/body/eval_jaxpr/all_to_all | solution.py:57
  81.5 16.5 %all_to_all.37 = f32[128,1,512]{2,1,0:T(1,128)S(1)} all-to-all(f32[128,1,512]{2,1,0:T(1,128)S(1)} %all_to_all.29), channel_id=1, replica_groups=mesh['row'=8,'col'=16] {'row','col'}, dimensions={0} | all-to-all | bytes 524288 | tf_op jit(solution)/shard_map/while/body/eval_jaxpr/all_to_all | solution.py:65
  103.0 11.5 %all-to-all-done.3 = f32[128,1,512]{2,1,0:T(1,128)S(1)} async-done(((f32[128,1,512]{2,1,0:T(1,128)}), f32[128,1,512]{2,1,0:T(1,128)S(1)}, u32[]{:S(2)}, u32[]{:S(2)}) %all-to-all-start.3) | async-done | bytes 262176 | tf_op jit(solution)/shard_map/while/body/eval_jaxpr/all_to_all | solution.py:66
  115.4 11.7 %cholesky.152 = f32[128,128]{1,0:T(8,128)S(1)} custom-call(f32[128,128]{1,0:T(8,128)S(1)} %fusion.85), custom_call_target="Cholesky" | custom-call | tf_op jit(solution)/shard_map/while/body/eval_jaxpr/jit(cholesky)/cholesky | solution.py:29
  139.6 11.7 %cholesky.153 = f32[128,128]{1,0:T(8,128)S(1)} custom-call(f32[128,128]{1,0:T(8,128)S(1)} %fusion.88), custom_call_target="Cholesky" | custom-call | tf_op jit(solution)/shard_map/while/body/eval_jaxpr/jit(cholesky)/cholesky | solution.py:29
  170.8 14.2 %all-to-all-done = bf16[8,256,256]{2,1,0:T(8,128)(2,1)S(1)} async-done(((bf16[8,256,256]{2,1,0:T(8,128)(2,1)}), bf16[8,256,256]{2,1,0:T(8,128)(2,1)S(1)}, u32[]{:S(2)}, u32[]{:S(2)}) %all-to-all-start) | async-done | bytes 1048608 | tf_op jit(solution)/shard_map/while/body/eval_jaxpr/all_to_all | solution.py:51
  206.0 29.9 %all_to_all.36 = bf16[16,256,256]{2,1,0:T(8,128)(2,1)S(1)} all-to-all(bf16[16,256,256]{2,1,0:T(8,128)(2,1)S(1)} %bitcast.95), channel_id=1, replica_groups=mesh['row'=8,'col'=16] {'col'}, dimensions={0} | all-to-all | bytes 4194304 | tf_op jit(solution)/shard_map/while/body/eval_jaxpr/all_to_all | solution.py:57
  237.2 16.6 %all_to_all.37 = f32[128,1,512]{2,1,0:T(1,128)S(1)} all-to-all(f32[128,1,512]{2,1,0:T(1,128)S(1)} %all_to_all.29), channel_id=1, replica_groups=mesh['row'=8,'col'=16] {'row','col'}, dimensions={0} | all-to-all | bytes 524288 | tf_op jit(solution)/shard_map/while/body/eval_jaxpr/all_to_all | solution.py:65
  258.8 11.5 %all-to-all-done.3 = f32[128,1,512]{2,1,0:T(1,128)S(1)} async-done(((f32[128,1,512]{2,1,0:T(1,128)}), f32[128,1,512]{2,1,0:T(1,128)S(1)}, u32[]{:S(2)}, u32[]{:S(2)}) %all-to-all-start.3) | async-done | bytes 262176 | tf_op jit(solution)/shard_map/while/body/eval_jaxpr/all_to_all | solution.py:66
  271.3 11.7 %cholesky.152 = f32[128,128]{1,0:T(8,128)S(1)} custom-call(f32[128,128]{1,0:T(8,128)S(1)} %fusion.85), custom_call_target="Cholesky" | custom-call | tf_op jit(solution)/shard_map/while/body/eval_jaxpr/jit(cholesky)/cholesky | solution.py:29
  295.4 11.7 %cholesky.153 = f32[128,128]{1,0:T(8,128)S(1)} custom-call(f32[128,128]{1,0:T(8,128)S(1)} %fusion.88), custom_call_target="Cholesky" | custom-call | tf_op jit(solution)/shard_map/while/body/eval_jaxpr/jit(cholesky)/cholesky | solution.py:29
  326.7 14.2 %all-to-all-done = bf16[8,256,256]{2,1,0:T(8,128)(2,1)S(1)} async-done(((bf16[8,256,256]{2,1,0:T(8,128)(2,1)}), bf16[8,256,256]{2,1,0:T(8,128)(2,1)S(1)}, u32[]{:S(2)}, u32[]{:S(2)}) %all-to-all-start) | async-done | bytes 1048608 | tf_op jit(solution)/shard_map/while/body/eval_jaxpr/all_to_all | solution.py:51
  361.8 29.9 %all_to_all.36 = bf16[16,256,256]{2,1,0:T(8,128)(2,1)S(1)} all-to-all(bf16[16,256,256]{2,1,0:T(8,128)(2,1)S(1)} %bitcast.95), channel_id=1, replica_groups=mesh['row'=8,'col'=16] {'col'}, dimensions={0} | all-to-all | bytes 4194304 | tf_op jit(solution)/shard_map/while/body/eval_jaxpr/all_to_all | solution.py:57
  393.0 16.5 %all_to_all.37 = f32[128,1,512]{2,1,0:T(1,128)S(1)} all-to-all(f32[128,1,512]{2,1,0:T(1,128)S(1)} %all_to_all.29), channel_id=1, replica_groups=mesh['row'=8,'col'=16] {'row','col'}, dimensions={0} | all-to-all | bytes 524288 | tf_op jit(solution)/shard_map/while/body/eval_jaxpr/all_to_all | solution.py:65
  414.6 11.5 %all-to-all-done.3 = f32[128,1,512]{2,1,0:T(1,128)S(1)} async-done(((f32[128,1,512]{2,1,0:T(1,128)}), f32[128,1,512]{2,1,0:T(1,128)S(1)}, u32[]{:S(2)}, u32[]{:S(2)}) %all-to-all-start.3) | async-done | bytes 262176 | tf_op jit(solution)/shard_map/while/body/eval_jaxpr/all_to_all | solution.py:66
  427.1 11.7 %cholesky.152 = f32[128,128]{1,0:T(8,128)S(1)} custom-call(f32[128,128]{1,0:T(8,128)S(1)} %fusion.85), custom_call_target="Cholesky" | custom-call | tf_op jit(solution)/shard_map/while/body/eval_jaxpr/jit(cholesky)/cholesky | solution.py:29
  451.2 11.7 %cholesky.153 = f32[128,128]{1,0:T(8,128)S(1)} custom-call(f32[128,128]{1,0:T(8,128)S(1)} %fusion.88), custom_call_target="Cholesky" | custom-call | tf_op jit(solution)/shard_map/while/body/eval_jaxpr/jit(cholesky)/cholesky | solution.py:29
  482.5 14.2 %all-to-all-done = bf16[8,256,256]{2,1,0:T(8,128)(2,1)S(1)} async-done(((bf16[8,256,256]{2,1,0:T(8,128)(2,1)}), bf16[8,256,256]{2,1,0:T(8,128)(2,1)S(1)}, u32[]{:S(2)}, u32[]{:S(2)}) %all-to-all-start) | async-done | bytes 1048608 | tf_op jit(solution)/shard_map/while/body/eval_jaxpr/all_to_all | solution.py:51
  517.6 29.9 %all_to_all.36 = bf16[16,256,256]{2,1,0:T(8,128)(2,1)S(1)} all-to-all(bf16[16,256,256]{2,1,0:T(8,128)(2,1)S(1)} %bitcast.95), channel_id=1, replica_groups=mesh['row'=8,'col'=16] {'col'}, dimensions={0} | all-to-all | bytes 4194304 | tf_op jit(solution)/shard_map/while/body/eval_jaxpr/all_to_all | solution.py:57
  548.8 16.5 %all_to_all.37 = f32[128,1,512]{2,1,0:T(1,128)S(1)} all-to-all(f32[128,1,512]{2,1,0:T(1,128)S(1)} %all_to_all.29), channel_id=1, replica_groups=mesh['row'=8,'col'=16] {'row','col'}, dimensions={0} | all-to-all | bytes 524288 | tf_op jit(solution)/shard_map/while/body/eval_jaxpr/all_to_all | solution.py:65
  582.8 11.7 %cholesky.152 = f32[128,128]{1,0:T(8,128)S(1)} custom-call(f32[128,128]{1,0:T(8,128)S(1)} %fusion.85), custom_call_target="Cholesky" | custom-call | tf_op jit(solution)/shard_map/while/body/eval_jaxpr/jit(cholesky)/cholesky | solution.py:29
  607.0 11.7 %cholesky.153 = f32[128,128]{1,0:T(8,128)S(1)} custom-call(f32[128,128]{1,0:T(8,128)S(1)} %fusion.88), custom_call_target="Cholesky" | custom-call | tf_op jit(solution)/shard_map/while/body/eval_jaxpr/jit(cholesky)/cholesky | solution.py:29
  (178 shorter events, 257.2 us)
Async XLA Ops:
  3.5 20.8 %all-to-all-start = ((bf16[8,256,256]{2,1,0:T(8,128)(2,1)}), bf16[8,256,256]{2,1,0:T(8,128)(2,1)S(1)}, u32[]{:S(2)}, u32[]{:S(2)}) async-start(bf16[8,256,256]{2,1,0:T(8,128)(2,1)} %broadcast_in_dim.48), calls=%async_computation | async-start | bytes 2097152 | tf_op jit(solution)/shard_map/while/body/eval_jaxpr/all_to_all | solution.py:51
  33.9 46.6 %copy-start = (f32[256,1]{0,1:T(1,128)S(1)}, f32[256,1]{0,1:T(1,128)}, u32[]{:S(2)}) copy-start(f32[256,1]{0,1:T(1,128)} %get-tuple-element.201) | copy-start | bytes 3076 | tf_op jit(solution)/shard_map/while
  99.0 15.5 %all-to-all-start.3 = ((f32[128,1,512]{2,1,0:T(1,128)}), f32[128,1,512]{2,1,0:T(1,128)S(1)}, u32[]{:S(2)}, u32[]{:S(2)}) async-start(f32[128,1,512]{2,1,0:T(1,128)} %broadcast_in_dim.49), calls=%async_computation.3 | async-start | bytes 524288 | tf_op jit(solution)/shard_map/while/body/eval_jaxpr/all_to_all | solution.py:66
  166.0 19.0 %all-to-all-start = ((bf16[8,256,256]{2,1,0:T(8,128)(2,1)}), bf16[8,256,256]{2,1,0:T(8,128)(2,1)S(1)}, u32[]{:S(2)}, u32[]{:S(2)}) async-start(bf16[8,256,256]{2,1,0:T(8,128)(2,1)} %broadcast_in_dim.48), calls=%async_computation | async-start | bytes 2097152 | tf_op jit(solution)/shard_map/while/body/eval_jaxpr/all_to_all | solution.py:51
  194.7 41.5 %copy-start = (f32[256,1]{0,1:T(1,128)S(1)}, f32[256,1]{0,1:T(1,128)}, u32[]{:S(2)}) copy-start(f32[256,1]{0,1:T(1,128)} %get-tuple-element.201) | copy-start | bytes 3076 | tf_op jit(solution)/shard_map/while
  254.8 15.5 %all-to-all-start.3 = ((f32[128,1,512]{2,1,0:T(1,128)}), f32[128,1,512]{2,1,0:T(1,128)S(1)}, u32[]{:S(2)}, u32[]{:S(2)}) async-start(f32[128,1,512]{2,1,0:T(1,128)} %broadcast_in_dim.49), calls=%async_computation.3 | async-start | bytes 524288 | tf_op jit(solution)/shard_map/while/body/eval_jaxpr/all_to_all | solution.py:66
  321.9 19.0 %all-to-all-start = ((bf16[8,256,256]{2,1,0:T(8,128)(2,1)}), bf16[8,256,256]{2,1,0:T(8,128)(2,1)S(1)}, u32[]{:S(2)}, u32[]{:S(2)}) async-start(bf16[8,256,256]{2,1,0:T(8,128)(2,1)} %broadcast_in_dim.48), calls=%async_computation | async-start | bytes 2097152 | tf_op jit(solution)/shard_map/while/body/eval_jaxpr/all_to_all | solution.py:51
  350.5 41.5 %copy-start = (f32[256,1]{0,1:T(1,128)S(1)}, f32[256,1]{0,1:T(1,128)}, u32[]{:S(2)}) copy-start(f32[256,1]{0,1:T(1,128)} %get-tuple-element.201) | copy-start | bytes 3076 | tf_op jit(solution)/shard_map/while
  410.6 15.5 %all-to-all-start.3 = ((f32[128,1,512]{2,1,0:T(1,128)}), f32[128,1,512]{2,1,0:T(1,128)S(1)}, u32[]{:S(2)}, u32[]{:S(2)}) async-start(f32[128,1,512]{2,1,0:T(1,128)} %broadcast_in_dim.49), calls=%async_computation.3 | async-start | bytes 524288 | tf_op jit(solution)/shard_map/while/body/eval_jaxpr/all_to_all | solution.py:66
  477.7 19.0 %all-to-all-start = ((bf16[8,256,256]{2,1,0:T(8,128)(2,1)}), bf16[8,256,256]{2,1,0:T(8,128)(2,1)S(1)}, u32[]{:S(2)}, u32[]{:S(2)}) async-start(bf16[8,256,256]{2,1,0:T(8,128)(2,1)} %broadcast_in_dim.48), calls=%async_computation | async-start | bytes 2097152 | tf_op jit(solution)/shard_map/while/body/eval_jaxpr/all_to_all | solution.py:51
  506.3 41.5 %copy-start = (f32[256,1]{0,1:T(1,128)S(1)}, f32[256,1]{0,1:T(1,128)}, u32[]{:S(2)}) copy-start(f32[256,1]{0,1:T(1,128)} %get-tuple-element.201) | copy-start | bytes 3076 | tf_op jit(solution)/shard_map/while
  566.4 15.5 %all-to-all-start.3 = ((f32[128,1,512]{2,1,0:T(1,128)}), f32[128,1,512]{2,1,0:T(1,128)S(1)}, u32[]{:S(2)}, u32[]{:S(2)}) async-start(f32[128,1,512]{2,1,0:T(1,128)} %broadcast_in_dim.49), calls=%async_computation.3 | async-start | bytes 524288 | tf_op jit(solution)/shard_map/while/body/eval_jaxpr/all_to_all | solution.py:66

commit v3 on v2

--- a/solution.py
+++ b/solution.py
@@ -1,6 +1,10 @@
+import functools
+
 import jax
 import jax.numpy as jnp
 from jax import lax
+from jax.experimental import pallas as pl
+from jax.experimental.pallas import tpu as pltpu
 from jax.sharding import PartitionSpec as P
 
 ITERS = 4
@@ -46,6 +50,40 @@
     return (dot_hi(image, inverse.T), lower.T)
 
 
+def _apply_kernel(index_ref, count_ref, tiles_ref, basis_ref, out_ref, gat_ref, *, rows_per_block, slots, tile):
+    block = pl.program_id(0)
+    for r in range(rows_per_block):
+        t = block * rows_per_block + r
+        live = count_ref[t]
+        for s in range(slots):
+            start = pl.multiple_of(index_ref[t * slots + s] * tile, tile)
+            rows = basis_ref[pl.ds(start, tile), :]
+            gat_ref[s * tile:(s + 1) * tile, :] = jnp.where(s < live, rows, jnp.zeros_like(rows))
+        lhs = jnp.concatenate([tiles_ref[r, s] for s in range(slots)], axis=1)
+        out_ref[r] = jnp.dot(lhs, gat_ref[...], preferred_element_type=jnp.float32).astype(out_ref.dtype)
+
+
+def apply_tiles(tiles, basis, index, counts, rows_per_block=8):
+    trows, slots, tile, _ = tiles.shape
+    width = basis.shape[-1]
+    kernel = functools.partial(_apply_kernel, rows_per_block=rows_per_block, slots=slots, tile=tile)
+    spec = pltpu.PrefetchScalarGridSpec(
+        num_scalar_prefetch=2,
+        grid=(trows // rows_per_block,),
+        in_specs=[
+            pl.BlockSpec((rows_per_block, slots, tile, tile), lambda i, idx, cnt: (i, 0, 0, 0)),
+            pl.BlockSpec(basis.shape, lambda i, idx, cnt: (0, 0)),
+        ],
+        out_specs=pl.BlockSpec((rows_per_block, tile, width), lambda i, idx, cnt: (i, 0, 0)),
+        scratch_shapes=[pltpu.VMEM((slots * tile, width), basis.dtype)],
+    )
+    return pl.pallas_call(
+        kernel,
+        grid_spec=spec,
+        out_shape=jax.ShapeDtypeStruct((trows, tile, width), jnp.bfloat16),
+    )(index.reshape(-1), counts, tiles, basis)
+
+
 def gather_rows(x, axis):
     n = lax.axis_size(axis)
     got = lax.all_to_all(jnp.broadcast_to(x, (n,) + x.shape), axis, 0, 0, tiled=False)
@@ -73,21 +111,15 @@
     counts = tile_count[:, 0]
     rows_dev, width = basis.shape
     tile = tiles.shape[-1]
-    slots = tiles.shape[1]
     nodes = rows_dev * lax.axis_size("row") * lax.axis_size("col")
-    live = jnp.arange(slots)[None, :] < counts[:, None]
     scale = degree_scale[:, None]
     probe = (basis.astype(jnp.float32) * scale).astype(jnp.bfloat16)
     number = lax.axis_size("col") * rows_dev // tile
 
     def one_step(current):
         block_basis = gather_rows(current, "row")
-        tiled = block_basis.reshape(-1, tile, width)
-        chosen = jnp.where(live[:, :, None, None], tiled[index], jnp.zeros((), jnp.bfloat16))
-        result = lax.dot_general(
-            tiles, chosen, (((1, 3), (1, 2)), ((0,), (0,))), preferred_element_type=jnp.float32
-        )
-        summed = sum_scatter_rows(result.reshape(number * tile, width).astype(jnp.bfloat16), "col")
+        result = apply_tiles(tiles, block_basis, index, counts)
+        summed = sum_scatter_rows(result.reshape(number * tile, width), "col")
         image = summed * scale
         gram = sum_all(gram_of(image, nodes), ("row", "col"))
         return normalize(image, gram)
@@ -98,10 +130,6 @@
 
     start = (probe, jnp.zeros(basis.shape, jnp.float32), jnp.zeros((width, width), jnp.float32))
     _, embedding, factor = lax.fori_loop(0, ITERS, loop_step, start)
-    return (embedding, factor)
-
-    embedding, factor = one_step(probe)
-    embedding, factor = lax.fori_loop(1, ITERS, loop_step, (embedding, factor))
     return (embedding, factor)
 
 

time: 635 us -> 581 us (0.915)
  blocking collectives: 191 us -> 270 us
  waiting for transfers between devices: 103 us -> 45.9 us
  matrix products: 58.9 us -> 13.7 us
  local copies, waits for them, and re-layouts: 52.4 us -> 11 us
  Pallas kernels: 0 us -> 30.4 us
  starting transfers between devices: 33.7 us -> 16 us
    all_to_all x0 -> x4, blocking collectives: none -> 76.3 us  [gather_rows(): lax.all_to_all(jnp.broadcast_to(x, (n,) + x.shape), axis, 0, 0, tiled=False)]
    all_to_all x4 -> x0, waiting for transfers between devices: 56.6 us -> none  [gather_rows(): lax.all_to_all(jnp.broadcast_to(x, (n,) + x.shape), axis, 0, 0, tiled=False)]
    dot_general x4 -> x0, matrix products: 45.2 us -> none  [one_step(): lax.dot_general(tiles, chosen, (((1, 3), (1, 2)), ((0,), (0,))), preferre...]
    gather x4 -> x0, local copies, waits for them, and re-layouts: 38.7 us -> none  [one_step(): tiled[index]]
    pallas_call x0 -> x4, Pallas kernels: none -> 30.4 us  [apply_tiles(): pl.pallas_call(kernel, grid_spec=spec, out_shape=jax.ShapeDtypeStruct((tr...]
    all_to_all x4 -> x0, starting transfers between devices: 17.7 us -> none  [gather_rows(): lax.all_to_all(jnp.broadcast_to(x, (n,) + x.shape), axis, 0, 0, tiled=False)]
  transfers between devices with their start and end apart: 8 -> 4, of which waited for: 8 -> 4; matrix products, arithmetic and copies ran while one was open for 1% -> 0% of each run, Pallas kernels for 0% -> 0%
where the time goes in v3:
time: 581 us; the launch traced here: 580 us
  blocking collectives  270 us (46%)
  other arithmetic  191 us (33%)
  waiting for transfers between devices  45.9 us (8%)
  Pallas kernels  30.4 us (5%)
  starting transfers between devices  16 us (3%)
  matrix products  13.7 us (2%)
  local copies, waits for them, and re-layouts  11 us (2%)
    all_to_all x4, blocking collectives, sum_scatter_rows(): lax.all_to_all(x.reshape((n, -1) + x.shape[1:]), axis, 0, 0, tiled=False)  128 us
    another operation x24, other arithmetic, cholesky_and_inverse(): lower = jnp.linalg.cholesky(g)  99.1 us
    another operation x16, other arithmetic, cholesky_and_inverse(): return (lower, jax.scipy.linalg.solve_triangular(lower, eye, lower=True))  83.7 us
    all_to_all x4, blocking collectives, gather_rows(): lax.all_to_all(jnp.broadcast_to(x, (n,) + x.shape), axis, 0, 0, tiled=False)  76.3 us
    all_to_all x4, blocking collectives, sum_all(): lax.all_to_all(x.reshape(n, -1), axes, 0, 0, tiled=False)  65.7 us
    all_to_all x4, waiting for transfers between devices, sum_all(): lax.all_to_all(jnp.broadcast_to(piece, (n,) + piece.shape), axes, 0, 0, t...  45.9 us
    pallas_call x4, Pallas kernels, apply_tiles(): pl.pallas_call(kernel, grid_spec=spec, out_shape=jax.ShapeDtypeStruct((tr...  30.4 us
    all_to_all x4, starting transfers between devices, sum_all(): lax.all_to_all(jnp.broadcast_to(piece, (n,) + piece.shape), axes, 0, 0, t...  16 us
  transfers between devices with their start and end apart: 4, of which 4 were waited for; matrix products, arithmetic and copies ran while one was open for 0% of the time, Pallas kernels for 0%

profile of v3, /device:TPU:1, one launch (start us, length us, event | category | flops | bytes accessed | tf_op | source)
XLA Modules:
  0.0 580.1 jit_solution(13931602234933428898)
XLA Ops:
  2.5 575.8 %while.15 = (s32[]{:T(128)}, bf16[256,256]{1,0:T(8,128)(2,1)S(1)}, f32[256,256]{1,0:T(8,128)}, f32[256,256]{0,1:T(8,128)}, s32[32,1,8]{2,0,1:T(8,128)}, /*index=...) while((s32[]{:T(128)}, bf16[256,256]{1,0:T(8,128)(2,1)S(1)}, ...), condition=%wide.wide.region_5.8_spmd, body=%wide.wide.region_0.7_spmd.sunk | while | flops 557121280 | bytes 19083992 | solution.py:132
  2.6 20.6 %all_to_all.36 = bf16[8,256,256]{2,1,0:T(8,128)(2,1)} all-to-all(bf16[8,256,256]{2,1,0:T(8,128)(2,1)S(1)} %broadcast_in_dim.15), channel_id=1, replica_groups=mesh['row'=8,'col'=16] {'row'}, dimensions={0} | all-to-all | bytes 2097152 | tf_op jit(solution)/shard_map/while/body/eval_jaxpr/all_to_all | solution.py:89
  30.9 35.0 %all_to_all.37 = bf16[16,256,256]{2,1,0:T(8,128)(2,1)S(1)} all-to-all(bf16[16,256,256]{2,1,0:T(8,128)(2,1)} %bitcast.94), channel_id=1, replica_groups=mesh['row'=8,'col'=16] {'col'}, dimensions={0} | all-to-all | bytes 4194304 | tf_op jit(solution)/shard_map/while/body/eval_jaxpr/all_to_all | solution.py:95
  67.5 16.6 %all_to_all.38 = f32[128,1,512]{2,1,0:T(1,128)S(1)} all-to-all(f32[128,1,512]{2,1,0:T(1,128)S(1)} %all_to_all.29), channel_id=1, replica_groups=mesh['row'=8,'col'=16] {'row','col'}, dimensions={0} | all-to-all | bytes 524288 | tf_op jit(solution)/shard_map/while/body/eval_jaxpr/all_to_all | solution.py:103
  89.1 11.5 %all-to-all-done.3 = f32[128,1,512]{2,1,0:T(1,128)S(1)} async-done(((f32[128,1,512]{2,1,0:T(1,128)}), f32[128,1,512]{2,1,0:T(1,128)S(1)}, u32[]{:S(2)}, u32[]{:S(2)}) %all-to-all-start.3) | async-done | bytes 262176 | tf_op jit(solution)/shard_map/while/body/eval_jaxpr/all_to_all | solution.py:104
  101.6 11.7 %cholesky.172 = f32[128,128]{1,0:T(8,128)S(1)} custom-call(f32[128,128]{1,0:T(8,128)S(1)} %fusion.92), custom_call_target="Cholesky" | custom-call | tf_op jit(solution)/shard_map/while/body/eval_jaxpr/jit(cholesky)/cholesky | solution.py:33
  125.8 11.7 %cholesky.173 = f32[128,128]{1,0:T(8,128)S(1)} custom-call(f32[128,128]{1,0:T(8,128)S(1)} %fusion.95), custom_call_target="Cholesky" | custom-call | tf_op jit(solution)/shard_map/while/body/eval_jaxpr/jit(cholesky)/cholesky | solution.py:33
  151.2 18.6 %all_to_all.36 = bf16[8,256,256]{2,1,0:T(8,128)(2,1)} all-to-all(bf16[8,256,256]{2,1,0:T(8,128)(2,1)S(1)} %broadcast_in_dim.15), channel_id=1, replica_groups=mesh['row'=8,'col'=16] {'row'}, dimensions={0} | all-to-all | bytes 2097152 | tf_op jit(solution)/shard_map/while/body/eval_jaxpr/all_to_all | solution.py:89
  177.4 31.1 %all_to_all.37 = bf16[16,256,256]{2,1,0:T(8,128)(2,1)S(1)} all-to-all(bf16[16,256,256]{2,1,0:T(8,128)(2,1)} %bitcast.94), channel_id=1, replica_groups=mesh['row'=8,'col'=16] {'col'}, dimensions={0} | all-to-all | bytes 4194304 | tf_op jit(solution)/shard_map/while/body/eval_jaxpr/all_to_all | solution.py:95
  210.1 16.4 %all_to_all.38 = f32[128,1,512]{2,1,0:T(1,128)S(1)} all-to-all(f32[128,1,512]{2,1,0:T(1,128)S(1)} %all_to_all.29), channel_id=1, replica_groups=mesh['row'=8,'col'=16] {'row','col'}, dimensions={0} | all-to-all | bytes 524288 | tf_op jit(solution)/shard_map/while/body/eval_jaxpr/all_to_all | solution.py:103
  231.5 11.5 %all-to-all-done.3 = f32[128,1,512]{2,1,0:T(1,128)S(1)} async-done(((f32[128,1,512]{2,1,0:T(1,128)}), f32[128,1,512]{2,1,0:T(1,128)S(1)}, u32[]{:S(2)}, u32[]{:S(2)}) %all-to-all-start.3) | async-done | bytes 262176 | tf_op jit(solution)/shard_map/while/body/eval_jaxpr/all_to_all | solution.py:104
  244.0 11.7 %cholesky.172 = f32[128,128]{1,0:T(8,128)S(1)} custom-call(f32[128,128]{1,0:T(8,128)S(1)} %fusion.92), custom_call_target="Cholesky" | custom-call | tf_op jit(solution)/shard_map/while/body/eval_jaxpr/jit(cholesky)/cholesky | solution.py:33
  268.2 11.7 %cholesky.173 = f32[128,128]{1,0:T(8,128)S(1)} custom-call(f32[128,128]{1,0:T(8,128)S(1)} %fusion.95), custom_call_target="Cholesky" | custom-call | tf_op jit(solution)/shard_map/while/body/eval_jaxpr/jit(cholesky)/cholesky | solution.py:33
  293.6 18.6 %all_to_all.36 = bf16[8,256,256]{2,1,0:T(8,128)(2,1)} all-to-all(bf16[8,256,256]{2,1,0:T(8,128)(2,1)S(1)} %broadcast_in_dim.15), channel_id=1, replica_groups=mesh['row'=8,'col'=16] {'row'}, dimensions={0} | all-to-all | bytes 2097152 | tf_op jit(solution)/shard_map/while/body/eval_jaxpr/all_to_all | solution.py:89
  319.8 31.1 %all_to_all.37 = bf16[16,256,256]{2,1,0:T(8,128)(2,1)S(1)} all-to-all(bf16[16,256,256]{2,1,0:T(8,128)(2,1)} %bitcast.94), channel_id=1, replica_groups=mesh['row'=8,'col'=16] {'col'}, dimensions={0} | all-to-all | bytes 4194304 | tf_op jit(solution)/shard_map/while/body/eval_jaxpr/all_to_all | solution.py:95
  352.5 16.4 %all_to_all.38 = f32[128,1,512]{2,1,0:T(1,128)S(1)} all-to-all(f32[128,1,512]{2,1,0:T(1,128)S(1)} %all_to_all.29), channel_id=1, replica_groups=mesh['row'=8,'col'=16] {'row','col'}, dimensions={0} | all-to-all | bytes 524288 | tf_op jit(solution)/shard_map/while/body/eval_jaxpr/all_to_all | solution.py:103
  373.9 11.5 %all-to-all-done.3 = f32[128,1,512]{2,1,0:T(1,128)S(1)} async-done(((f32[128,1,512]{2,1,0:T(1,128)}), f32[128,1,512]{2,1,0:T(1,128)S(1)}, u32[]{:S(2)}, u32[]{:S(2)}) %all-to-all-start.3) | async-done | bytes 262176 | tf_op jit(solution)/shard_map/while/body/eval_jaxpr/all_to_all | solution.py:104
  386.4 11.7 %cholesky.172 = f32[128,128]{1,0:T(8,128)S(1)} custom-call(f32[128,128]{1,0:T(8,128)S(1)} %fusion.92), custom_call_target="Cholesky" | custom-call | tf_op jit(solution)/shard_map/while/body/eval_jaxpr/jit(cholesky)/cholesky | solution.py:33
  410.6 11.7 %cholesky.173 = f32[128,128]{1,0:T(8,128)S(1)} custom-call(f32[128,128]{1,0:T(8,128)S(1)} %fusion.95), custom_call_target="Cholesky" | custom-call | tf_op jit(solution)/shard_map/while/body/eval_jaxpr/jit(cholesky)/cholesky | solution.py:33
  436.0 18.6 %all_to_all.36 = bf16[8,256,256]{2,1,0:T(8,128)(2,1)} all-to-all(bf16[8,256,256]{2,1,0:T(8,128)(2,1)S(1)} %broadcast_in_dim.15), channel_id=1, replica_groups=mesh['row'=8,'col'=16] {'row'}, dimensions={0} | all-to-all | bytes 2097152 | tf_op jit(solution)/shard_map/while/body/eval_jaxpr/all_to_all | solution.py:89
  462.2 31.1 %all_to_all.37 = bf16[16,256,256]{2,1,0:T(8,128)(2,1)S(1)} all-to-all(bf16[16,256,256]{2,1,0:T(8,128)(2,1)} %bitcast.94), channel_id=1, replica_groups=mesh['row'=8,'col'=16] {'col'}, dimensions={0} | all-to-all | bytes 4194304 | tf_op jit(solution)/shard_map/while/body/eval_jaxpr/all_to_all | solution.py:95
  494.9 16.4 %all_to_all.38 = f32[128,1,512]{2,1,0:T(1,128)S(1)} all-to-all(f32[128,1,512]{2,1,0:T(1,128)S(1)} %all_to_all.29), channel_id=1, replica_groups=mesh['row'=8,'col'=16] {'row','col'}, dimensions={0} | all-to-all | bytes 524288 | tf_op jit(solution)/shard_map/while/body/eval_jaxpr/all_to_all | solution.py:103
  528.8 11.7 %cholesky.172 = f32[128,128]{1,0:T(8,128)S(1)} custom-call(f32[128,128]{1,0:T(8,128)S(1)} %fusion.92), custom_call_target="Cholesky" | custom-call | tf_op jit(solution)/shard_map/while/body/eval_jaxpr/jit(cholesky)/cholesky | solution.py:33
  552.9 11.7 %cholesky.173 = f32[128,128]{1,0:T(8,128)S(1)} custom-call(f32[128,128]{1,0:T(8,128)S(1)} %fusion.95), custom_call_target="Cholesky" | custom-call | tf_op jit(solution)/shard_map/while/body/eval_jaxpr/jit(cholesky)/cholesky | solution.py:33
  (165 shorter events, 180.2 us)
Async XLA Ops:
  1.4 1.1 copy-start.1
  2.5 20.7 %copy-start.2 = (s32[32]{0:T(128)S(1)}, s32[32]{0:T(128)}, u32[]{:S(2)}) copy-start(s32[32]{0:T(128)} %get-tuple-element.227.count_ref) | copy-start | bytes 388 | tf_op jit(solution)/shard_map/while
  65.8 0.7 copy-start
  85.1 15.5 %all-to-all-start.3 = ((f32[128,1,512]{2,1,0:T(1,128)}), f32[128,1,512]{2,1,0:T(1,128)S(1)}, u32[]{:S(2)}, u32[]{:S(2)}) async-start(f32[128,1,512]{2,1,0:T(1,128)} %broadcast_in_dim.16), calls=%async_computation.3 | async-start | bytes 524288 | tf_op jit(solution)/shard_map/while/body/eval_jaxpr/all_to_all | solution.py:104
  151.1 18.6 %copy-start.2 = (s32[32]{0:T(128)S(1)}, s32[32]{0:T(128)}, u32[]{:S(2)}) copy-start(s32[32]{0:T(128)} %get-tuple-element.227.count_ref) | copy-start | bytes 388 | tf_op jit(solution)/shard_map/while
  208.4 0.7 copy-start
  227.5 15.5 %all-to-all-start.3 = ((f32[128,1,512]{2,1,0:T(1,128)}), f32[128,1,512]{2,1,0:T(1,128)S(1)}, u32[]{:S(2)}, u32[]{:S(2)}) async-start(f32[128,1,512]{2,1,0:T(1,128)} %broadcast_in_dim.16), calls=%async_computation.3 | async-start | bytes 524288 | tf_op jit(solution)/shard_map/while/body/eval_jaxpr/all_to_all | solution.py:104
  293.5 18.6 %copy-start.2 = (s32[32]{0:T(128)S(1)}, s32[32]{0:T(128)}, u32[]{:S(2)}) copy-start(s32[32]{0:T(128)} %get-tuple-element.227.count_ref) | copy-start | bytes 388 | tf_op jit(solution)/shard_map/while
  350.8 0.7 copy-start
  369.9 15.5 %all-to-all-start.3 = ((f32[128,1,512]{2,1,0:T(1,128)}), f32[128,1,512]{2,1,0:T(1,128)S(1)}, u32[]{:S(2)}, u32[]{:S(2)}) async-start(f32[128,1,512]{2,1,0:T(1,128)} %broadcast_in_dim.16), calls=%async_computation.3 | async-start | bytes 524288 | tf_op jit(solution)/shard_map/while/body/eval_jaxpr/all_to_all | solution.py:104
  435.9 18.6 %copy-start.2 = (s32[32]{0:T(128)S(1)}, s32[32]{0:T(128)}, u32[]{:S(2)}) copy-start(s32[32]{0:T(128)} %get-tuple-element.227.count_ref) | copy-start | bytes 388 | tf_op jit(solution)/shard_map/while
  493.2 0.7 copy-start
  512.3 15.5 %all-to-all-start.3 = ((f32[128,1,512]{2,1,0:T(1,128)}), f32[128,1,512]{2,1,0:T(1,128)S(1)}, u32[]{:S(2)}, u32[]{:S(2)}) async-start(f32[128,1,512]{2,1,0:T(1,128)} %broadcast_in_dim.16), calls=%async_computation.3 | async-start | bytes 524288 | tf_op jit(solution)/shard_map/while/body/eval_jaxpr/all_to_all | solution.py:104

commit v4 on v3

--- a/solution.py
+++ b/solution.py
@@ -44,12 +44,6 @@
     return lower, inverse
 
 
-def normalize(image, gram):
-    gram = (gram + gram.T) * 0.5
-    lower, inverse = cholesky_and_inverse(gram)
-    return (dot_hi(image, inverse.T), lower.T)
-
-
 def _apply_kernel(index_ref, count_ref, tiles_ref, basis_ref, out_ref, gat_ref, *, rows_per_block, slots, tile):
     block = pl.program_id(0)
     for r in range(rows_per_block):
@@ -84,10 +78,12 @@
     )(index.reshape(-1), counts, tiles, basis)
 
 
-def gather_rows(x, axis):
+def shift_gather(x, axis):
     n = lax.axis_size(axis)
-    got = lax.all_to_all(jnp.broadcast_to(x, (n,) + x.shape), axis, 0, 0, tiled=False)
-    return got.reshape((-1,) + x.shape[1:])
+    blocks = [x]
+    for d in range(1, n):
+        blocks.append(lax.ppermute(x, axis, [(i, (i + d) % n) for i in range(n)]))
+    return jnp.concatenate(blocks, axis=0)
 
 
 def sum_scatter_rows(x, axis):
@@ -115,20 +111,26 @@
     scale = degree_scale[:, None]
     probe = (basis.astype(jnp.float32) * scale).astype(jnp.bfloat16)
     number = lax.axis_size("col") * rows_dev // tile
+    n_row = lax.axis_size("row")
+    per_peer = rows_dev // tile
+    me = lax.axis_index("row")
+    index = ((me - index // per_peer) % n_row) * per_peer + index % per_peer
+    scale_block = shift_gather(scale, "row")
 
-    def one_step(current):
-        block_basis = gather_rows(current, "row")
-        result = apply_tiles(tiles, block_basis, index, counts)
+    def loop_step(i, carry):
+        block_probe = carry[0]
+        result = apply_tiles(tiles, block_probe, index, counts)
         summed = sum_scatter_rows(result.reshape(number * tile, width), "col")
         image = summed * scale
+        image_block = shift_gather(image, "row")
         gram = sum_all(gram_of(image, nodes), ("row", "col"))
-        return normalize(image, gram)
+        gram = (gram + gram.T) * 0.5
+        lower, inverse = cholesky_and_inverse(gram)
+        embedding = dot_hi(image, inverse.T)
+        next_probe = (dot_hi(image_block, inverse.T) * scale_block).astype(jnp.bfloat16)
+        return (next_probe, embedding, lower.T)
 
-    def loop_step(i, carry):
-        embedding, factor = one_step(carry[0])
-        return ((embedding * scale).astype(jnp.bfloat16), embedding, factor)
-
-    start = (probe, jnp.zeros(basis.shape, jnp.float32), jnp.zeros((width, width), jnp.float32))
+    start = (shift_gather(probe, "row"), jnp.zeros(basis.shape, jnp.float32), jnp.zeros((width, width), jnp.float32))
     _, embedding, factor = lax.fori_loop(0, ITERS, loop_step, start)
     return (embedding, factor)
 

time: 581 us -> 589 us (1.014)
  blocking collectives: 270 us -> 130 us
  starting transfers between devices: 16 us -> 104 us
  waiting for transfers between devices: 45.9 us -> 79 us
  local copies, waits for them, and re-layouts: 11 us -> 25.5 us
  matrix products: 13.7 us -> 24.6 us
    all_to_all x8 -> x0, blocking collectives: 142 us -> none  [the longest x4 76.3 us: gather_rows(): lax.all_to_all(jnp.broadcast_to(x, (n,) + x.shape), axis, 0, 0, tiled=False)]
    ppermute x0 -> x42, starting transfers between devices: none -> 60.7 us  [shift_gather(): blocks.append(lax.ppermute(x, axis, [(i, (i + d) % n) for i in range(n)]))]
    ppermute x0 -> x42, waiting for transfers between devices: none -> 46.4 us  [shift_gather(): blocks.append(lax.ppermute(x, axis, [(i, (i + d) % n) for i in range(n)]))]
    all_to_all x4, waiting for transfers between devices: 45.9 us -> 11.2 us  [sum_all(): lax.all_to_all(jnp.broadcast_to(piece, (n,) + piece.shape), axes, 0, 0, t...]
    all_to_all x0 -> x4, starting transfers between devices: none -> 27.4 us  [sum_all(): lax.all_to_all(x.reshape(n, -1), axes, 0, 0, tiled=False)]
    all_to_all x0 -> x4, waiting for transfers between devices: none -> 21.4 us  [sum_all(): lax.all_to_all(x.reshape(n, -1), axes, 0, 0, tiled=False)]
    dot_general x20 -> x24, matrix products: 8.75 us -> 20 us  [dot_hi(): jnp.dot(a, b, precision=lax.Precision.HIGHEST, preferred_element_type=jnp...]
  transfers between devices with their start and end apart: 4 -> 50, of which waited for: 4 -> 31; matrix products, arithmetic and copies ran while one was open for 0% -> 3% of each run, Pallas kernels for 0% -> 0%
where the time goes in v4:
time: 589 us; the launch traced here: 588 us
  other arithmetic  193 us (33%)
  blocking collectives  130 us (22%)
  starting transfers between devices  104 us (18%)
  waiting for transfers between devices  79 us (13%)
  Pallas kernels  30.4 us (5%)
  local copies, waits for them, and re-layouts  25.5 us (4%)
  matrix products  24.6 us (4%)
    all_to_all x4, blocking collectives, sum_scatter_rows(): lax.all_to_all(x.reshape((n, -1) + x.shape[1:]), axis, 0, 0, tiled=False)  130 us
    another operation x24, other arithmetic, cholesky_and_inverse(): lower = jnp.linalg.cholesky(g)  99.1 us
    another operation x16, other arithmetic, cholesky_and_inverse(): return (lower, jax.scipy.linalg.solve_triangular(lower, eye, lower=True))  83.7 us
    ppermute x42, starting transfers between devices, shift_gather(): blocks.append(lax.ppermute(x, axis, [(i, (i + d) % n) for i in range(n)]))  60.7 us
    ppermute x42, waiting for transfers between devices, shift_gather(): blocks.append(lax.ppermute(x, axis, [(i, (i + d) % n) for i in range(n)]))  46.4 us
    pallas_call x4, Pallas kernels, apply_tiles(): pl.pallas_call(kernel, grid_spec=spec, out_shape=jax.ShapeDtypeStruct((tr...  30.4 us
    all_to_all x4, starting transfers between devices, sum_all(): lax.all_to_all(x.reshape(n, -1), axes, 0, 0, tiled=False)  27.4 us
    all_to_all x4, waiting for transfers between devices, sum_all(): lax.all_to_all(x.reshape(n, -1), axes, 0, 0, tiled=False)  21.4 us
  transfers between devices with their start and end apart: 50, of which 31 were waited for; matrix products, arithmetic and copies ran while one was open for 3% of the time, Pallas kernels for 0%

profile of v4, /device:TPU:1, one launch (start us, length us, event | category | flops | bytes accessed | tf_op | source)
XLA Modules:
  0.0 588.0 jit_solution(3324857197614115889)
XLA Ops:
  37.5 548.7 %while.15 = (s32[]{:T(128)}, bf16[2048,256]{1,0:T(8,128)(2,1)}, f32[256,256]{1,0:T(8,128)}, f32[256,256]{0,1:T(8,128)}, s32[32,8]{1,0:T(8,128)}, /*index=5*/s32[...) while((s32[]{:T(128)}, bf16[2048,256]{1,0:T(8,128)(2,1)}, ...), condition=%wide.wide.region_5.8_spmd, body=%wide.wide.region_0.7_spmd.sunk | while | flops 2168848128 | bytes 31079900 | solution.py:134
  37.7 7.6 %eval_jaxpr.1 = bf16[32,128,256]{2,1,0:T(8,128)(2,1)} custom-call(s32[256]{0:T(256)S(1)} %get-tuple-element.255.index_ref, s32[32]{0:T(128)S(1)} %get-tuple-element.251.count_ref, bf16[32,8,128,128]{3,2,1,0:T(8,128)(2,1)} %get-tuple-element.252.tiles_ref, bf16[2048,256]{1,0:T(8,128)(2,1)} %get-tuple-element.234.basis_ref), custom_call_target="tpu_custom_call" | custom-call | tf_op jit(solution)/shard_map/while/body/eval_jaxpr/pallas_call | solution.py:74
  45.3 35.8 %all_to_all.29 = bf16[16,256,256]{2,1,0:T(8,128)(2,1)S(1)} all-to-all(bf16[16,256,256]{2,1,0:T(8,128)(2,1)} %bitcast.126), channel_id=1, replica_groups=mesh['row'=8,'col'=16] {'col'}, dimensions={0} | all-to-all | bytes 4194304 | tf_op jit(solution)/shard_map/while/body/eval_jaxpr/all_to_all | solution.py:91
  125.3 11.7 %cholesky.172 = f32[128,128]{1,0:T(8,128)S(1)} custom-call(f32[128,128]{1,0:T(8,128)S(1)} %fusion.113), custom_call_target="Cholesky" | custom-call | tf_op jit(solution)/shard_map/while/body/eval_jaxpr/jit(cholesky)/cholesky | solution.py:33
  138.3 9.8 %custom-call.23 = f32[1,128,128]{1,2,0:T(8,128)S(1)} custom-call(f32[1,128,128]{2,1,0:T(8,128)S(1)} %get-tuple-element.216), custom_call_target="InvertDiagBlocksLowerTriangular" | custom-call | tf_op jit(solution)/shard_map/while/body/eval_jaxpr/jit(_solve_triangular)/triangular_solve | solution.py:35
  149.4 11.7 %cholesky.173 = f32[128,128]{1,0:T(8,128)S(1)} custom-call(f32[128,128]{1,0:T(8,128)S(1)} %fusion.116), custom_call_target="Cholesky" | custom-call | tf_op jit(solution)/shard_map/while/body/eval_jaxpr/jit(cholesky)/cholesky | solution.py:33
  162.5 9.8 %custom-call.24 = f32[1,128,128]{1,2,0:T(8,128)S(1)} custom-call(f32[1,128,128]{2,1,0:T(8,128)S(1)} %get-tuple-element.217), custom_call_target="InvertDiagBlocksLowerTriangular" | custom-call | tf_op jit(solution)/shard_map/while/body/eval_jaxpr/jit(_solve_triangular)/triangular_solve | solution.py:35
  177.6 7.6 %eval_jaxpr.1 = bf16[32,128,256]{2,1,0:T(8,128)(2,1)} custom-call(s32[256]{0:T(256)S(1)} %get-tuple-element.255.index_ref, s32[32]{0:T(128)S(1)} %get-tuple-element.251.count_ref, bf16[32,8,128,128]{3,2,1,0:T(8,128)(2,1)} %get-tuple-element.252.tiles_ref, bf16[2048,256]{1,0:T(8,128)(2,1)} %get-tuple-element.234.basis_ref), custom_call_target="tpu_custom_call" | custom-call | tf_op jit(solution)/shard_map/while/body/eval_jaxpr/pallas_call | solution.py:74
  185.2 31.4 %all_to_all.29 = bf16[16,256,256]{2,1,0:T(8,128)(2,1)S(1)} all-to-all(bf16[16,256,256]{2,1,0:T(8,128)(2,1)} %bitcast.126), channel_id=1, replica_groups=mesh['row'=8,'col'=16] {'col'}, dimensions={0} | all-to-all | bytes 4194304 | tf_op jit(solution)/shard_map/while/body/eval_jaxpr/all_to_all | solution.py:91
  261.5 11.7 %cholesky.172 = f32[128,128]{1,0:T(8,128)S(1)} custom-call(f32[128,128]{1,0:T(8,128)S(1)} %fusion.113), custom_call_target="Cholesky" | custom-call | tf_op jit(solution)/shard_map/while/body/eval_jaxpr/jit(cholesky)/cholesky | solution.py:33
  274.5 9.8 %custom-call.23 = f32[1,128,128]{1,2,0:T(8,128)S(1)} custom-call(f32[1,128,128]{2,1,0:T(8,128)S(1)} %get-tuple-element.216), custom_call_target="InvertDiagBlocksLowerTriangular" | custom-call | tf_op jit(solution)/shard_map/while/body/eval_jaxpr/jit(_solve_triangular)/triangular_solve | solution.py:35
  285.7 11.7 %cholesky.173 = f32[128,128]{1,0:T(8,128)S(1)} custom-call(f32[128,128]{1,0:T(8,128)S(1)} %fusion.116), custom_call_target="Cholesky" | custom-call | tf_op jit(solution)/shard_map/while/body/eval_jaxpr/jit(cholesky)/cholesky | solution.py:33
  298.7 9.8 %custom-call.24 = f32[1,128,128]{1,2,0:T(8,128)S(1)} custom-call(f32[1,128,128]{2,1,0:T(8,128)S(1)} %get-tuple-element.217), custom_call_target="InvertDiagBlocksLowerTriangular" | custom-call | tf_op jit(solution)/shard_map/while/body/eval_jaxpr/jit(_solve_triangular)/triangular_solve | solution.py:35
  321.5 31.4 %all_to_all.29 = bf16[16,256,256]{2,1,0:T(8,128)(2,1)S(1)} all-to-all(bf16[16,256,256]{2,1,0:T(8,128)(2,1)} %bitcast.126), channel_id=1, replica_groups=mesh['row'=8,'col'=16] {'col'}, dimensions={0} | all-to-all | bytes 4194304 | tf_op jit(solution)/shard_map/while/body/eval_jaxpr/all_to_all | solution.py:91
  397.7 11.7 %cholesky.172 = f32[128,128]{1,0:T(8,128)S(1)} custom-call(f32[128,128]{1,0:T(8,128)S(1)} %fusion.113), custom_call_target="Cholesky" | custom-call | tf_op jit(solution)/shard_map/while/body/eval_jaxpr/jit(cholesky)/cholesky | solution.py:33
  410.7 9.8 %custom-call.23 = f32[1,128,128]{1,2,0:T(8,128)S(1)} custom-call(f32[1,128,128]{2,1,0:T(8,128)S(1)} %get-tuple-element.216), custom_call_target="InvertDiagBlocksLowerTriangular" | custom-call | tf_op jit(solution)/shard_map/while/body/eval_jaxpr/jit(_solve_triangular)/triangular_solve | solution.py:35
  421.8 11.7 %cholesky.173 = f32[128,128]{1,0:T(8,128)S(1)} custom-call(f32[128,128]{1,0:T(8,128)S(1)} %fusion.116), custom_call_target="Cholesky" | custom-call | tf_op jit(solution)/shard_map/while/body/eval_jaxpr/jit(cholesky)/cholesky | solution.py:33
  434.9 9.8 %custom-call.24 = f32[1,128,128]{1,2,0:T(8,128)S(1)} custom-call(f32[1,128,128]{2,1,0:T(8,128)S(1)} %get-tuple-element.217), custom_call_target="InvertDiagBlocksLowerTriangular" | custom-call | tf_op jit(solution)/shard_map/while/body/eval_jaxpr/jit(_solve_triangular)/triangular_solve | solution.py:35
  450.0 7.6 %eval_jaxpr.1 = bf16[32,128,256]{2,1,0:T(8,128)(2,1)} custom-call(s32[256]{0:T(256)S(1)} %get-tuple-element.255.index_ref, s32[32]{0:T(128)S(1)} %get-tuple-element.251.count_ref, bf16[32,8,128,128]{3,2,1,0:T(8,128)(2,1)} %get-tuple-element.252.tiles_ref, bf16[2048,256]{1,0:T(8,128)(2,1)} %get-tuple-element.234.basis_ref), custom_call_target="tpu_custom_call" | custom-call | tf_op jit(solution)/shard_map/while/body/eval_jaxpr/pallas_call | solution.py:74
  457.6 31.4 %all_to_all.29 = bf16[16,256,256]{2,1,0:T(8,128)(2,1)S(1)} all-to-all(bf16[16,256,256]{2,1,0:T(8,128)(2,1)} %bitcast.126), channel_id=1, replica_groups=mesh['row'=8,'col'=16] {'col'}, dimensions={0} | all-to-all | bytes 4194304 | tf_op jit(solution)/shard_map/while/body/eval_jaxpr/all_to_all | solution.py:91
  533.9 11.7 %cholesky.172 = f32[128,128]{1,0:T(8,128)S(1)} custom-call(f32[128,128]{1,0:T(8,128)S(1)} %fusion.113), custom_call_target="Cholesky" | custom-call | tf_op jit(solution)/shard_map/while/body/eval_jaxpr/jit(cholesky)/cholesky | solution.py:33
  546.9 9.8 %custom-call.23 = f32[1,128,128]{1,2,0:T(8,128)S(1)} custom-call(f32[1,128,128]{2,1,0:T(8,128)S(1)} %get-tuple-element.216), custom_call_target="InvertDiagBlocksLowerTriangular" | custom-call | tf_op jit(solution)/shard_map/while/body/eval_jaxpr/jit(_solve_triangular)/triangular_solve | solution.py:35
  558.1 11.7 %cholesky.173 = f32[128,128]{1,0:T(8,128)S(1)} custom-call(f32[128,128]{1,0:T(8,128)S(1)} %fusion.116), custom_call_target="Cholesky" | custom-call | tf_op jit(solution)/shard_map/while/body/eval_jaxpr/jit(cholesky)/cholesky | solution.py:33
  571.1 9.8 %custom-call.24 = f32[1,128,128]{1,2,0:T(8,128)S(1)} custom-call(f32[1,128,128]{2,1,0:T(8,128)S(1)} %get-tuple-element.217), custom_call_target="InvertDiagBlocksLowerTriangular" | custom-call | tf_op jit(solution)/shard_map/while/body/eval_jaxpr/jit(_solve_triangular)/triangular_solve | solution.py:35
  (285 shorter events, 261.3 us)
Async XLA Ops:
  2.3 24.6 %collective-permute-start.7 = (bf16[256,256]{1,0:T(8,128)(2,1)S(1)}, bf16[256,256]{1,0:T(8,128)(2,1)S(1)}, u32[]{:S(2)}, u32[]{:S(2)}) collective-permute-start(bf16[256,256]{1,0:T(8,128)(2,1)S(1)} %get-tuple-element.110), channel_id=1, source_target_pairs={{0,16},{16,32},{32,48},{48,64},{64,80},{80,96},{96,112},{112,0},{1... | collective-permute-start | bytes 393224 | tf_op jit(solution)/shard_map/ppermute | solution.py:85
  4.9 24.1 %collective-permute-start.8 = (bf16[256,256]{1,0:T(8,128)(2,1)S(1)}, bf16[256,256]{1,0:T(8,128)(2,1)S(1)}, u32[]{:S(2)}, u32[]{:S(2)}) collective-permute-start(bf16[256,256]{1,0:T(8,128)(2,1)S(1)} %get-tuple-element.110), channel_id=1, source_target_pairs={{0,32},{16,48},{32,64},{48,80},{64,96},{80,112},{96,0},{112,16},{1... | collective-permute-start | bytes 393224 | tf_op jit(solution)/shard_map/ppermute | solution.py:85
  6.1 24.5 %collective-permute-start.9 = (bf16[256,256]{1,0:T(8,128)(2,1)S(1)}, bf16[256,256]{1,0:T(8,128)(2,1)S(1)}, u32[]{:S(2)}, u32[]{:S(2)}) collective-permute-start(bf16[256,256]{1,0:T(8,128)(2,1)S(1)} %get-tuple-element.110), channel_id=1, source_target_pairs={{0,48},{16,64},{32,80},{48,96},{64,112},{80,0},{96,16},{112,32},{1... | collective-permute-start | bytes 393224 | tf_op jit(solution)/shard_map/ppermute | solution.py:85
  81.6 25.7 %collective-permute-start = (f32[256,256]{1,0:T(8,128)S(1)}, f32[256,256]{1,0:T(8,128)S(1)}, u32[]{:S(2)}, u32[]{:S(2)}) collective-permute-start(f32[256,256]{1,0:T(8,128)S(1)} %get-tuple-element.215), channel_id=1, source_target_pairs={{0,16},{16,32},{32,48},{48,64},{64,80},{80,96},{96,112},{112,0},{1... | collective-permute-start | bytes 786440 | tf_op jit(solution)/shard_map/while/body/eval_jaxpr/ppermute | solution.py:85
  90.4 19.6 %collective-permute-start.1 = (f32[256,256]{1,0:T(8,128)S(1)}, f32[256,256]{1,0:T(8,128)}, u32[]{:S(2)}, u32[]{:S(2)}) collective-permute-start(f32[256,256]{1,0:T(8,128)S(1)} %get-tuple-element.215), channel_id=1, source_target_pairs={{0,32},{16,48},{32,64},{48,80},{64,96},{80,112},{96,0},{112,16},{1... | collective-permute-start | bytes 786440 | tf_op jit(solution)/shard_map/while/body/eval_jaxpr/ppermute | solution.py:85
  91.8 19.8 %collective-permute-start.2 = (f32[256,256]{1,0:T(8,128)S(1)}, f32[256,256]{1,0:T(8,128)S(1)}, u32[]{:S(2)}, u32[]{:S(2)}) collective-permute-start(f32[256,256]{1,0:T(8,128)S(1)} %get-tuple-element.215), channel_id=1, source_target_pairs={{0,48},{16,64},{32,80},{48,96},{64,112},{80,0},{96,16},{112,32},{1... | collective-permute-start | bytes 786440 | tf_op jit(solution)/shard_map/while/body/eval_jaxpr/ppermute | solution.py:85
  95.3 22.4 %collective-permute-start.4 = (f32[256,256]{1,0:T(8,128)S(1)}, f32[256,256]{1,0:T(8,128)S(1)}, u32[]{:S(2)}, u32[]{:S(2)}) collective-permute-start(f32[256,256]{1,0:T(8,128)S(1)} %get-tuple-element.215), channel_id=1, source_target_pairs={{0,80},{16,96},{32,112},{48,0},{64,16},{80,32},{96,48},{112,64},{1... | collective-permute-start | bytes 786440 | tf_op jit(solution)/shard_map/while/body/eval_jaxpr/ppermute | solution.py:85
  103.2 21.1 %all-to-all-start.2 = ((f32[128,1,512]{2,1,0:T(1,128)}), f32[128,1,512]{2,1,0:T(1,128)S(1)}, u32[]{:S(2)}, u32[]{:S(2)}) async-start(f32[128,1,512]{2,1,0:T(1,128)} %broadcast_in_dim.10), calls=%async_computation.2 | async-start | bytes 524288 | tf_op jit(solution)/shard_map/while/body/eval_jaxpr/all_to_all | solution.py:100
  217.0 26.5 %collective-permute-start = (f32[256,256]{1,0:T(8,128)S(1)}, f32[256,256]{1,0:T(8,128)S(1)}, u32[]{:S(2)}, u32[]{:S(2)}) collective-permute-start(f32[256,256]{1,0:T(8,128)S(1)} %get-tuple-element.215), channel_id=1, source_target_pairs={{0,16},{16,32},{32,48},{48,64},{64,80},{80,96},{96,112},{112,0},{1... | collective-permute-start | bytes 786440 | tf_op jit(solution)/shard_map/while/body/eval_jaxpr/ppermute | solution.py:85
  226.6 19.6 %collective-permute-start.1 = (f32[256,256]{1,0:T(8,128)S(1)}, f32[256,256]{1,0:T(8,128)}, u32[]{:S(2)}, u32[]{:S(2)}) collective-permute-start(f32[256,256]{1,0:T(8,128)S(1)} %get-tuple-element.215), channel_id=1, source_target_pairs={{0,32},{16,48},{32,64},{48,80},{64,96},{80,112},{96,0},{112,16},{1... | collective-permute-start | bytes 786440 | tf_op jit(solution)/shard_map/while/body/eval_jaxpr/ppermute | solution.py:85
  228.0 19.8 %collective-permute-start.2 = (f32[256,256]{1,0:T(8,128)S(1)}, f32[256,256]{1,0:T(8,128)S(1)}, u32[]{:S(2)}, u32[]{:S(2)}) collective-permute-start(f32[256,256]{1,0:T(8,128)S(1)} %get-tuple-element.215), channel_id=1, source_target_pairs={{0,48},{16,64},{32,80},{48,96},{64,112},{80,0},{96,16},{112,32},{1... | collective-permute-start | bytes 786440 | tf_op jit(solution)/shard_map/while/body/eval_jaxpr/ppermute | solution.py:85
  231.5 22.4 %collective-permute-start.4 = (f32[256,256]{1,0:T(8,128)S(1)}, f32[256,256]{1,0:T(8,128)S(1)}, u32[]{:S(2)}, u32[]{:S(2)}) collective-permute-start(f32[256,256]{1,0:T(8,128)S(1)} %get-tuple-element.215), channel_id=1, source_target_pairs={{0,80},{16,96},{32,112},{48,0},{64,16},{80,32},{96,48},{112,64},{1... | collective-permute-start | bytes 786440 | tf_op jit(solution)/shard_map/while/body/eval_jaxpr/ppermute | solution.py:85
  239.4 21.1 %all-to-all-start.2 = ((f32[128,1,512]{2,1,0:T(1,128)}), f32[128,1,512]{2,1,0:T(1,128)S(1)}, u32[]{:S(2)}, u32[]{:S(2)}) async-start(f32[128,1,512]{2,1,0:T(1,128)} %broadcast_in_dim.10), calls=%async_computation.2 | async-start | bytes 524288 | tf_op jit(solution)/shard_map/while/body/eval_jaxpr/all_to_all | solution.py:100
  353.2 26.4 %collective-permute-start = (f32[256,256]{1,0:T(8,128)S(1)}, f32[256,256]{1,0:T(8,128)S(1)}, u32[]{:S(2)}, u32[]{:S(2)}) collective-permute-start(f32[256,256]{1,0:T(8,128)S(1)} %get-tuple-element.215), channel_id=1, source_target_pairs={{0,16},{16,32},{32,48},{48,64},{64,80},{80,96},{96,112},{112,0},{1... | collective-permute-start | bytes 786440 | tf_op jit(solution)/shard_map/while/body/eval_jaxpr/ppermute | solution.py:85
  362.8 19.6 %collective-permute-start.1 = (f32[256,256]{1,0:T(8,128)S(1)}, f32[256,256]{1,0:T(8,128)}, u32[]{:S(2)}, u32[]{:S(2)}) collective-permute-start(f32[256,256]{1,0:T(8,128)S(1)} %get-tuple-element.215), channel_id=1, source_target_pairs={{0,32},{16,48},{32,64},{48,80},{64,96},{80,112},{96,0},{112,16},{1... | collective-permute-start | bytes 786440 | tf_op jit(solution)/shard_map/while/body/eval_jaxpr/ppermute | solution.py:85
  364.2 19.8 %collective-permute-start.2 = (f32[256,256]{1,0:T(8,128)S(1)}, f32[256,256]{1,0:T(8,128)S(1)}, u32[]{:S(2)}, u32[]{:S(2)}) collective-permute-start(f32[256,256]{1,0:T(8,128)S(1)} %get-tuple-element.215), channel_id=1, source_target_pairs={{0,48},{16,64},{32,80},{48,96},{64,112},{80,0},{96,16},{112,32},{1... | collective-permute-start | bytes 786440 | tf_op jit(solution)/shard_map/while/body/eval_jaxpr/ppermute | solution.py:85
  367.7 22.4 %collective-permute-start.4 = (f32[256,256]{1,0:T(8,128)S(1)}, f32[256,256]{1,0:T(8,128)S(1)}, u32[]{:S(2)}, u32[]{:S(2)}) collective-permute-start(f32[256,256]{1,0:T(8,128)S(1)} %get-tuple-element.215), channel_id=1, source_target_pairs={{0,80},{16,96},{32,112},{48,0},{64,16},{80,32},{96,48},{112,64},{1... | collective-permute-start | bytes 786440 | tf_op jit(solution)/shard_map/while/body/eval_jaxpr/ppermute | solution.py:85
  375.6 21.1 %all-to-all-start.2 = ((f32[128,1,512]{2,1,0:T(1,128)}), f32[128,1,512]{2,1,0:T(1,128)S(1)}, u32[]{:S(2)}, u32[]{:S(2)}) async-start(f32[128,1,512]{2,1,0:T(1,128)} %broadcast_in_dim.10), calls=%async_computation.2 | async-start | bytes 524288 | tf_op jit(solution)/shard_map/while/body/eval_jaxpr/all_to_all | solution.py:100
  489.4 26.5 %collective-permute-start = (f32[256,256]{1,0:T(8,128)S(1)}, f32[256,256]{1,0:T(8,128)S(1)}, u32[]{:S(2)}, u32[]{:S(2)}) collective-permute-start(f32[256,256]{1,0:T(8,128)S(1)} %get-tuple-element.215), channel_id=1, source_target_pairs={{0,16},{16,32},{32,48},{48,64},{64,80},{80,96},{96,112},{112,0},{1... | collective-permute-start | bytes 786440 | tf_op jit(solution)/shard_map/while/body/eval_jaxpr/ppermute | solution.py:85
  491.5 19.3 %all-to-all-start.1 = ((f32[128,1,512]{2,1,0:T(1,128)}), f32[128,1,512]{2,1,0:T(1,128)S(1)}, u32[]{:S(2)}, u32[]{:S(2)}) async-start(f32[128,1,512]{2,1,0:T(1,128)} %all_to_all.23), calls=%async_computation.1 | async-start | bytes 524288 | tf_op jit(solution)/shard_map/while/body/eval_jaxpr/all_to_all | solution.py:99
  499.0 19.6 %collective-permute-start.1 = (f32[256,256]{1,0:T(8,128)S(1)}, f32[256,256]{1,0:T(8,128)}, u32[]{:S(2)}, u32[]{:S(2)}) collective-permute-start(f32[256,256]{1,0:T(8,128)S(1)} %get-tuple-element.215), channel_id=1, source_target_pairs={{0,32},{16,48},{32,64},{48,80},{64,96},{80,112},{96,0},{112,16},{1... | collective-permute-start | bytes 786440 | tf_op jit(solution)/shard_map/while/body/eval_jaxpr/ppermute | solution.py:85
  500.4 19.8 %collective-permute-start.2 = (f32[256,256]{1,0:T(8,128)S(1)}, f32[256,256]{1,0:T(8,128)S(1)}, u32[]{:S(2)}, u32[]{:S(2)}) collective-permute-start(f32[256,256]{1,0:T(8,128)S(1)} %get-tuple-element.215), channel_id=1, source_target_pairs={{0,48},{16,64},{32,80},{48,96},{64,112},{80,0},{96,16},{112,32},{1... | collective-permute-start | bytes 786440 | tf_op jit(solution)/shard_map/while/body/eval_jaxpr/ppermute | solution.py:85
  503.9 22.4 %collective-permute-start.4 = (f32[256,256]{1,0:T(8,128)S(1)}, f32[256,256]{1,0:T(8,128)S(1)}, u32[]{:S(2)}, u32[]{:S(2)}) collective-permute-start(f32[256,256]{1,0:T(8,128)S(1)} %get-tuple-element.215), channel_id=1, source_target_pairs={{0,80},{16,96},{32,112},{48,0},{64,16},{80,32},{96,48},{112,64},{1... | collective-permute-start | bytes 786440 | tf_op jit(solution)/shard_map/while/body/eval_jaxpr/ppermute | solution.py:85
  511.8 21.1 %all-to-all-start.2 = ((f32[128,1,512]{2,1,0:T(1,128)}), f32[128,1,512]{2,1,0:T(1,128)S(1)}, u32[]{:S(2)}, u32[]{:S(2)}) async-start(f32[128,1,512]{2,1,0:T(1,128)} %broadcast_in_dim.10), calls=%async_computation.2 | async-start | bytes 524288 | tf_op jit(solution)/shard_map/while/body/eval_jaxpr/all_to_all | solution.py:100
  (29 other events, 385.5 us)

commit v5 on v4

--- a/solution.py
+++ b/solution.py
@@ -6,6 +6,7 @@
 from jax.experimental import pallas as pl
 from jax.experimental.pallas import tpu as pltpu
 from jax.sharding import PartitionSpec as P
+
 
 ITERS = 4
 
@@ -78,14 +79,6 @@
     )(index.reshape(-1), counts, tiles, basis)
 
 
-def shift_gather(x, axis):
-    n = lax.axis_size(axis)
-    blocks = [x]
-    for d in range(1, n):
-        blocks.append(lax.ppermute(x, axis, [(i, (i + d) % n) for i in range(n)]))
-    return jnp.concatenate(blocks, axis=0)
-
-
 def sum_scatter_rows(x, axis):
     n = lax.axis_size(axis)
     got = lax.all_to_all(x.reshape((n, -1) + x.shape[1:]), axis, 0, 0, tiled=False)
@@ -111,18 +104,14 @@
     scale = degree_scale[:, None]
     probe = (basis.astype(jnp.float32) * scale).astype(jnp.bfloat16)
     number = lax.axis_size("col") * rows_dev // tile
-    n_row = lax.axis_size("row")
-    per_peer = rows_dev // tile
-    me = lax.axis_index("row")
-    index = ((me - index // per_peer) % n_row) * per_peer + index % per_peer
-    scale_block = shift_gather(scale, "row")
+    scale_block = lax.all_gather(scale, "row", axis=0, tiled=True)
 
     def loop_step(i, carry):
         block_probe = carry[0]
         result = apply_tiles(tiles, block_probe, index, counts)
         summed = sum_scatter_rows(result.reshape(number * tile, width), "col")
         image = summed * scale
-        image_block = shift_gather(image, "row")
+        image_block = lax.all_gather(image, "row", axis=0, tiled=True)
         gram = sum_all(gram_of(image, nodes), ("row", "col"))
         gram = (gram + gram.T) * 0.5
         lower, inverse = cholesky_and_inverse(gram)
@@ -130,7 +119,7 @@
         next_probe = (dot_hi(image_block, inverse.T) * scale_block).astype(jnp.bfloat16)
         return (next_probe, embedding, lower.T)
 
-    start = (shift_gather(probe, "row"), jnp.zeros(basis.shape, jnp.float32), jnp.zeros((width, width), jnp.float32))
+    start = (lax.all_gather(probe, "row", axis=0, tiled=True), jnp.zeros(basis.shape, jnp.float32), jnp.zeros((width, width), jnp.float32))
     _, embedding, factor = lax.fori_loop(0, ITERS, loop_step, start)
     return (embedding, factor)
 

time: 589 us -> 580 us (0.985)
  starting transfers between devices: 104 us -> 37.1 us
  waiting for transfers between devices: 79 us -> 118 us
  between operations: 0.68 us -> 13.7 us
  local copies, waits for them, and re-layouts: 25.5 us -> 13.6 us
  blocking collectives: 130 us -> 140 us
  matrix products: 24.6 us -> 31 us
    ppermute x42 -> x0, starting transfers between devices: 60.7 us -> none  [shift_gather(): blocks.append(lax.ppermute(x, axis, [(i, (i + d) % n) for i in range(n)]))]
    ppermute x42 -> x0, waiting for transfers between devices: 46.4 us -> none  [shift_gather(): blocks.append(lax.ppermute(x, axis, [(i, (i + d) % n) for i in range(n)]))]
    all_to_all x4, waiting for transfers between devices: 11.2 us -> 57.3 us  [sum_all(): lax.all_to_all(jnp.broadcast_to(piece, (n,) + piece.shape), axes, 0, 0, t...]
    all_to_all x4, waiting for transfers between devices: 21.4 us -> 43.4 us  [sum_all(): lax.all_to_all(x.reshape(n, -1), axes, 0, 0, tiled=False)]
    all_gather x0 -> x5, waiting for transfers between devices: none -> 15.2 us  [the longest x1 15.2 us: body(): lax.all_gather(probe, 'row', axis=0, tiled=True)]
    all_gather x0 -> x1, blocking collectives: none -> 12.1 us  [body(): scale_block = lax.all_gather(scale, 'row', axis=0, tiled=True)]
    all_to_all x4, starting transfers between devices: 27.4 us -> 20.9 us  [sum_all(): lax.all_to_all(x.reshape(n, -1), axes, 0, 0, tiled=False)]
    dot_general x24, matrix products: 20 us -> 26.4 us  [dot_hi(): jnp.dot(a, b, precision=lax.Precision.HIGHEST, preferred_element_type=jnp...]
  transfers between devices with their start and end apart: 50 -> 13, of which waited for: 31 -> 9; matrix products, arithmetic and copies ran while one was open for 3% -> 36% of each run, Pallas kernels for 0% -> 0%
where the time goes in v5:
time: 580 us; the launch traced here: 578 us
  other arithmetic  193 us (33%)
  blocking collectives  140 us (24%)
  waiting for transfers between devices  118 us (20%)
  starting transfers between devices  37.1 us (6%)
  matrix products  31 us (5%)
  Pallas kernels  30.9 us (5%)
  between operations  13.7 us (2%)
  local copies, waits for them, and re-layouts  13.6 us (2%)
    all_to_all x4, blocking collectives, sum_scatter_rows(): lax.all_to_all(x.reshape((n, -1) + x.shape[1:]), axis, 0, 0, tiled=False)  128 us
    another operation x24, other arithmetic, cholesky_and_inverse(): lower = jnp.linalg.cholesky(g)  99.1 us
    another operation x16, other arithmetic, cholesky_and_inverse(): return (lower, jax.scipy.linalg.solve_triangular(lower, eye, lower=True))  83.7 us
    all_to_all x4, waiting for transfers between devices, sum_all(): lax.all_to_all(jnp.broadcast_to(piece, (n,) + piece.shape), axes, 0, 0, t...  57.3 us
    all_to_all x4, waiting for transfers between devices, sum_all(): lax.all_to_all(x.reshape(n, -1), axes, 0, 0, tiled=False)  43.4 us
    pallas_call x4, Pallas kernels, apply_tiles(): pl.pallas_call(kernel, grid_spec=spec, out_shape=jax.ShapeDtypeStruct((tr...  30.9 us
    dot_general x24, matrix products, dot_hi(): jnp.dot(a, b, precision=lax.Precision.HIGHEST, preferred_element_type=jnp...  26.4 us
    all_to_all x4, starting transfers between devices, sum_all(): lax.all_to_all(x.reshape(n, -1), axes, 0, 0, tiled=False)  20.9 us
  transfers between devices with their start and end apart: 13, of which 9 were waited for; matrix products, arithmetic and copies ran while one was open for 36% of the time, Pallas kernels for 0%

profile of v5, /device:TPU:1, one launch (start us, length us, event | category | flops | bytes accessed | tf_op | source)
XLA Modules:
  0.0 578.3 jit_solution(15745962435012806006)
XLA Ops:
  9.8 12.1 %all-gather.1 = f32[8,1,256]{2,1,0:T(1,128)S(1)} all-gather(f32[1,1,256]{2,1,0:T(1,128)} %bitcast.115), channel_id=2, replica_groups=mesh['row'=8,'col'=16] {'row'}, dimensions={0}, use_global_device_ids=true | all-gather | bytes 9216 | tf_op jit(solution)/shard_map/all_gather | solution.py:107
  21.9 15.2 %all-gather.5.cloned.1.call-done = bf16[2048,256]{1,0:T(8,128)(2,1)} async-done(((bf16[256,256]{1,0:T(8,128)(2,1)}), bf16[2048,256]{1,0:T(8,128)(2,1)}) %all-gather.5.cloned.1.call-update) | async-done | bytes 1048592 | tf_op jit(solution)/shard_map/all_gather | solution.py:122
  37.1 532.9 %while.15 = (s32[]{:T(128)}, bf16[2048,256]{1,0:T(8,128)(2,1)}, f32[256,256]{1,0:T(8,128)}, f32[256,256]{0,1:T(8,128)}, s32[32,1,8]{2,0,1:T(8,128)}, /*index=5*/...) while((s32[]{:T(128)}, bf16[2048,256]{1,0:T(8,128)(2,1)}, ...), condition=%wide.wide.region_5.8_spmd, body=%wide.wide.region_0.7_spmd.sunk | while | flops 2168848128 | bytes 28986688 | solution.py:123
  44.8 34.4 %all_to_all.29 = bf16[16,256,256]{2,1,0:T(8,128)(2,1)S(1)} all-to-all(bf16[16,256,256]{2,1,0:T(8,128)(2,1)} %bitcast.112), channel_id=1, replica_groups=mesh['row'=8,'col'=16] {'col'}, dimensions={0} | all-to-all | bytes 4194304 | tf_op jit(solution)/shard_map/while/body/eval_jaxpr/all_to_all | solution.py:84
  87.6 10.7 %all-to-all-done.1 = f32[128,1,512]{2,1,0:T(1,128)S(1)} async-done(((f32[128,1,512]{2,1,0:T(1,128)}), f32[128,1,512]{2,1,0:T(1,128)S(1)}, u32[]{:S(2)}, u32[]{:S(2)}) %all-to-all-start.1) | async-done | bytes 262176 | tf_op jit(solution)/shard_map/while/body/eval_jaxpr/all_to_all | solution.py:92
  103.3 14.3 %all-to-all-done.2 = f32[128,1,512]{2,1,0:T(1,128)S(1)} async-done(((f32[128,1,512]{2,1,0:T(1,128)}), f32[128,1,512]{2,1,0:T(1,128)S(1)}, u32[]{:S(2)}, u32[]{:S(2)}) %all-to-all-start.2) | async-done | bytes 262176 | tf_op jit(solution)/shard_map/while/body/eval_jaxpr/all_to_all | solution.py:93
  118.6 11.7 %cholesky.172 = f32[128,128]{1,0:T(8,128)S(1)} custom-call(f32[128,128]{1,0:T(8,128)S(1)} %fusion.107), custom_call_target="Cholesky" | custom-call | tf_op jit(solution)/shard_map/while/body/eval_jaxpr/jit(cholesky)/cholesky | solution.py:34
  142.5 11.7 %cholesky.173 = f32[128,128]{1,0:T(8,128)S(1)} custom-call(f32[128,128]{1,0:T(8,128)S(1)} %fusion.110), custom_call_target="Cholesky" | custom-call | tf_op jit(solution)/shard_map/while/body/eval_jaxpr/jit(cholesky)/cholesky | solution.py:34
  155.6 9.8 %custom-call.15 = f32[1,128,128]{1,2,0:T(8,128)S(1)} custom-call(f32[1,128,128]{2,1,0:T(8,128)S(1)} %get-tuple-element.207), custom_call_target="InvertDiagBlocksLowerTriangular" | custom-call | tf_op jit(solution)/shard_map/while/body/eval_jaxpr/jit(_solve_triangular)/triangular_solve | solution.py:36
  180.4 31.2 %all_to_all.29 = bf16[16,256,256]{2,1,0:T(8,128)(2,1)S(1)} all-to-all(bf16[16,256,256]{2,1,0:T(8,128)(2,1)} %bitcast.112), channel_id=1, replica_groups=mesh['row'=8,'col'=16] {'col'}, dimensions={0} | all-to-all | bytes 4194304 | tf_op jit(solution)/shard_map/while/body/eval_jaxpr/all_to_all | solution.py:84
  219.9 10.8 %all-to-all-done.1 = f32[128,1,512]{2,1,0:T(1,128)S(1)} async-done(((f32[128,1,512]{2,1,0:T(1,128)}), f32[128,1,512]{2,1,0:T(1,128)S(1)}, u32[]{:S(2)}, u32[]{:S(2)}) %all-to-all-start.1) | async-done | bytes 262176 | tf_op jit(solution)/shard_map/while/body/eval_jaxpr/all_to_all | solution.py:92
  235.8 14.3 %all-to-all-done.2 = f32[128,1,512]{2,1,0:T(1,128)S(1)} async-done(((f32[128,1,512]{2,1,0:T(1,128)}), f32[128,1,512]{2,1,0:T(1,128)S(1)}, u32[]{:S(2)}, u32[]{:S(2)}) %all-to-all-start.2) | async-done | bytes 262176 | tf_op jit(solution)/shard_map/while/body/eval_jaxpr/all_to_all | solution.py:93
  251.1 11.7 %cholesky.172 = f32[128,128]{1,0:T(8,128)S(1)} custom-call(f32[128,128]{1,0:T(8,128)S(1)} %fusion.107), custom_call_target="Cholesky" | custom-call | tf_op jit(solution)/shard_map/while/body/eval_jaxpr/jit(cholesky)/cholesky | solution.py:34
  275.0 11.7 %cholesky.173 = f32[128,128]{1,0:T(8,128)S(1)} custom-call(f32[128,128]{1,0:T(8,128)S(1)} %fusion.110), custom_call_target="Cholesky" | custom-call | tf_op jit(solution)/shard_map/while/body/eval_jaxpr/jit(cholesky)/cholesky | solution.py:34
  312.8 31.2 %all_to_all.29 = bf16[16,256,256]{2,1,0:T(8,128)(2,1)S(1)} all-to-all(bf16[16,256,256]{2,1,0:T(8,128)(2,1)} %bitcast.112), channel_id=1, replica_groups=mesh['row'=8,'col'=16] {'col'}, dimensions={0} | all-to-all | bytes 4194304 | tf_op jit(solution)/shard_map/while/body/eval_jaxpr/all_to_all | solution.py:84
  352.2 11.0 %all-to-all-done.1 = f32[128,1,512]{2,1,0:T(1,128)S(1)} async-done(((f32[128,1,512]{2,1,0:T(1,128)}), f32[128,1,512]{2,1,0:T(1,128)S(1)}, u32[]{:S(2)}, u32[]{:S(2)}) %all-to-all-start.1) | async-done | bytes 262176 | tf_op jit(solution)/shard_map/while/body/eval_jaxpr/all_to_all | solution.py:92
  368.2 14.3 %all-to-all-done.2 = f32[128,1,512]{2,1,0:T(1,128)S(1)} async-done(((f32[128,1,512]{2,1,0:T(1,128)}), f32[128,1,512]{2,1,0:T(1,128)S(1)}, u32[]{:S(2)}, u32[]{:S(2)}) %all-to-all-start.2) | async-done | bytes 262176 | tf_op jit(solution)/shard_map/while/body/eval_jaxpr/all_to_all | solution.py:93
  383.6 11.7 %cholesky.172 = f32[128,128]{1,0:T(8,128)S(1)} custom-call(f32[128,128]{1,0:T(8,128)S(1)} %fusion.107), custom_call_target="Cholesky" | custom-call | tf_op jit(solution)/shard_map/while/body/eval_jaxpr/jit(cholesky)/cholesky | solution.py:34
  407.4 11.7 %cholesky.173 = f32[128,128]{1,0:T(8,128)S(1)} custom-call(f32[128,128]{1,0:T(8,128)S(1)} %fusion.110), custom_call_target="Cholesky" | custom-call | tf_op jit(solution)/shard_map/while/body/eval_jaxpr/jit(cholesky)/cholesky | solution.py:34
  445.3 31.2 %all_to_all.29 = bf16[16,256,256]{2,1,0:T(8,128)(2,1)S(1)} all-to-all(bf16[16,256,256]{2,1,0:T(8,128)(2,1)} %bitcast.112), channel_id=1, replica_groups=mesh['row'=8,'col'=16] {'col'}, dimensions={0} | all-to-all | bytes 4194304 | tf_op jit(solution)/shard_map/while/body/eval_jaxpr/all_to_all | solution.py:84
  484.7 11.0 %all-to-all-done.1 = f32[128,1,512]{2,1,0:T(1,128)S(1)} async-done(((f32[128,1,512]{2,1,0:T(1,128)}), f32[128,1,512]{2,1,0:T(1,128)S(1)}, u32[]{:S(2)}, u32[]{:S(2)}) %all-to-all-start.1) | async-done | bytes 262176 | tf_op jit(solution)/shard_map/while/body/eval_jaxpr/all_to_all | solution.py:92
  500.7 14.3 %all-to-all-done.2 = f32[128,1,512]{2,1,0:T(1,128)S(1)} async-done(((f32[128,1,512]{2,1,0:T(1,128)}), f32[128,1,512]{2,1,0:T(1,128)S(1)}, u32[]{:S(2)}, u32[]{:S(2)}) %all-to-all-start.2) | async-done | bytes 262176 | tf_op jit(solution)/shard_map/while/body/eval_jaxpr/all_to_all | solution.py:93
  516.0 11.7 %cholesky.172 = f32[128,128]{1,0:T(8,128)S(1)} custom-call(f32[128,128]{1,0:T(8,128)S(1)} %fusion.107), custom_call_target="Cholesky" | custom-call | tf_op jit(solution)/shard_map/while/body/eval_jaxpr/jit(cholesky)/cholesky | solution.py:34
  539.9 11.7 %cholesky.173 = f32[128,128]{1,0:T(8,128)S(1)} custom-call(f32[128,128]{1,0:T(8,128)S(1)} %fusion.110), custom_call_target="Cholesky" | custom-call | tf_op jit(solution)/shard_map/while/body/eval_jaxpr/jit(cholesky)/cholesky | solution.py:34
  (193 shorter events, 204.0 us)
Async XLA Ops:
  7.2 29.9 %all-gather.5.cloned.1.call-start = ((), (), s32[]{:S(2)}) async-start(), calls=%async_computation.3 | async-start | bytes 1179648 | tf_op jit(solution)/shard_map/all_gather | solution.py:122
  9.7 27.4 %copy-start.2 = (s32[32,1,8]{2,0,1:T(8,128)}, s32[32,1,8]{2,0,1:T(8,128)S(1)}, u32[]{:S(2)}) copy-start(s32[32,1,8]{2,0,1:T(8,128)S(1)} %copy.35) | copy-start | bytes 3076
  80.0 6.9 %copy-start = (f32[256,256]{1,0:T(8,128)}, f32[256,256]{1,0:T(8,128)S(1)}, u32[]{:S(2)}) copy-start(f32[256,256]{1,0:T(8,128)S(1)} %broadcast_multiply_fusion.3) | copy-start | bytes 786436 | tf_op jit(solution)/shard_map/while
  81.6 16.7 %all-to-all-start.1 = ((f32[128,1,512]{2,1,0:T(1,128)}), f32[128,1,512]{2,1,0:T(1,128)S(1)}, u32[]{:S(2)}, u32[]{:S(2)}) async-start(f32[128,1,512]{2,1,0:T(1,128)} %all_to_all.23), calls=%async_computation.1 | async-start | bytes 524288 | tf_op jit(solution)/shard_map/while/body/eval_jaxpr/all_to_all | solution.py:92
  86.8 81.4 %all-gather.7.cloned.1.call-start = ((), (), s32[]{:S(2)}) async-start(), calls=%async_computation.4 | async-start | bytes 2359296 | tf_op jit(solution)/shard_map/while/body/eval_jaxpr/all_gather | solution.py:114
  99.3 18.3 %all-to-all-start.2 = ((f32[128,1,512]{2,1,0:T(1,128)}), f32[128,1,512]{2,1,0:T(1,128)S(1)}, u32[]{:S(2)}, u32[]{:S(2)}) async-start(f32[128,1,512]{2,1,0:T(1,128)} %broadcast_in_dim.10), calls=%async_computation.2 | async-start | bytes 524288 | tf_op jit(solution)/shard_map/while/body/eval_jaxpr/all_to_all | solution.py:93
  118.4 48.6 %copy-start.1 = (f32[256,256]{1,0:T(8,128)S(1)}, f32[256,256]{1,0:T(8,128)}, u32[]{:S(2)}) copy-start(f32[256,256]{1,0:T(8,128)} %copy-done) | copy-start | bytes 786436 | tf_op jit(solution)/shard_map/while
  212.4 6.8 %copy-start = (f32[256,256]{1,0:T(8,128)}, f32[256,256]{1,0:T(8,128)S(1)}, u32[]{:S(2)}) copy-start(f32[256,256]{1,0:T(8,128)S(1)} %broadcast_multiply_fusion.3) | copy-start | bytes 786436 | tf_op jit(solution)/shard_map/while
  213.9 16.8 %all-to-all-start.1 = ((f32[128,1,512]{2,1,0:T(1,128)}), f32[128,1,512]{2,1,0:T(1,128)S(1)}, u32[]{:S(2)}, u32[]{:S(2)}) async-start(f32[128,1,512]{2,1,0:T(1,128)} %all_to_all.23), calls=%async_computation.1 | async-start | bytes 524288 | tf_op jit(solution)/shard_map/while/body/eval_jaxpr/all_to_all | solution.py:92
  219.2 81.5 %all-gather.7.cloned.1.call-start = ((), (), s32[]{:S(2)}) async-start(), calls=%async_computation.4 | async-start | bytes 2359296 | tf_op jit(solution)/shard_map/while/body/eval_jaxpr/all_gather | solution.py:114
  231.8 18.3 %all-to-all-start.2 = ((f32[128,1,512]{2,1,0:T(1,128)}), f32[128,1,512]{2,1,0:T(1,128)S(1)}, u32[]{:S(2)}, u32[]{:S(2)}) async-start(f32[128,1,512]{2,1,0:T(1,128)} %broadcast_in_dim.10), calls=%async_computation.2 | async-start | bytes 524288 | tf_op jit(solution)/shard_map/while/body/eval_jaxpr/all_to_all | solution.py:93
  250.9 48.6 %copy-start.1 = (f32[256,256]{1,0:T(8,128)S(1)}, f32[256,256]{1,0:T(8,128)}, u32[]{:S(2)}) copy-start(f32[256,256]{1,0:T(8,128)} %copy-done) | copy-start | bytes 786436 | tf_op jit(solution)/shard_map/while
  344.0 0.7 copy-start.3
  344.8 6.8 %copy-start = (f32[256,256]{1,0:T(8,128)}, f32[256,256]{1,0:T(8,128)S(1)}, u32[]{:S(2)}) copy-start(f32[256,256]{1,0:T(8,128)S(1)} %broadcast_multiply_fusion.3) | copy-start | bytes 786436 | tf_op jit(solution)/shard_map/while
  346.4 16.8 %all-to-all-start.1 = ((f32[128,1,512]{2,1,0:T(1,128)}), f32[128,1,512]{2,1,0:T(1,128)S(1)}, u32[]{:S(2)}, u32[]{:S(2)}) async-start(f32[128,1,512]{2,1,0:T(1,128)} %all_to_all.23), calls=%async_computation.1 | async-start | bytes 524288 | tf_op jit(solution)/shard_map/while/body/eval_jaxpr/all_to_all | solution.py:92
  351.6 81.5 %all-gather.7.cloned.1.call-start = ((), (), s32[]{:S(2)}) async-start(), calls=%async_computation.4 | async-start | bytes 2359296 | tf_op jit(solution)/shard_map/while/body/eval_jaxpr/all_gather | solution.py:114
  364.2 18.3 %all-to-all-start.2 = ((f32[128,1,512]{2,1,0:T(1,128)}), f32[128,1,512]{2,1,0:T(1,128)S(1)}, u32[]{:S(2)}, u32[]{:S(2)}) async-start(f32[128,1,512]{2,1,0:T(1,128)} %broadcast_in_dim.10), calls=%async_computation.2 | async-start | bytes 524288 | tf_op jit(solution)/shard_map/while/body/eval_jaxpr/all_to_all | solution.py:93
  383.4 48.6 %copy-start.1 = (f32[256,256]{1,0:T(8,128)S(1)}, f32[256,256]{1,0:T(8,128)}, u32[]{:S(2)}) copy-start(f32[256,256]{1,0:T(8,128)} %copy-done) | copy-start | bytes 786436 | tf_op jit(solution)/shard_map/while
  476.5 0.7 copy-start.3
  477.3 6.9 %copy-start = (f32[256,256]{1,0:T(8,128)}, f32[256,256]{1,0:T(8,128)S(1)}, u32[]{:S(2)}) copy-start(f32[256,256]{1,0:T(8,128)S(1)} %broadcast_multiply_fusion.3) | copy-start | bytes 786436 | tf_op jit(solution)/shard_map/while
  478.8 16.8 %all-to-all-start.1 = ((f32[128,1,512]{2,1,0:T(1,128)}), f32[128,1,512]{2,1,0:T(1,128)S(1)}, u32[]{:S(2)}, u32[]{:S(2)}) async-start(f32[128,1,512]{2,1,0:T(1,128)} %all_to_all.23), calls=%async_computation.1 | async-start | bytes 524288 | tf_op jit(solution)/shard_map/while/body/eval_jaxpr/all_to_all | solution.py:92
  484.1 81.5 %all-gather.7.cloned.1.call-start = ((), (), s32[]{:S(2)}) async-start(), calls=%async_computation.4 | async-start | bytes 2359296 | tf_op jit(solution)/shard_map/while/body/eval_jaxpr/all_gather | solution.py:114
  496.7 18.3 %all-to-all-start.2 = ((f32[128,1,512]{2,1,0:T(1,128)}), f32[128,1,512]{2,1,0:T(1,128)S(1)}, u32[]{:S(2)}, u32[]{:S(2)}) async-start(f32[128,1,512]{2,1,0:T(1,128)} %broadcast_in_dim.10), calls=%async_computation.2 | async-start | bytes 524288 | tf_op jit(solution)/shard_map/while/body/eval_jaxpr/all_to_all | solution.py:93
  515.8 48.6 %copy-start.1 = (f32[256,256]{1,0:T(8,128)S(1)}, f32[256,256]{1,0:T(8,128)}, u32[]{:S(2)}) copy-start(f32[256,256]{1,0:T(8,128)} %copy-done) | copy-start | bytes 786436 | tf_op jit(solution)/shard_map/while
  (2 other events, 1.4 us)
Sparse Core Ops, SparseCore 0:
  10.3 26.7 all-gather.4
  89.9 28.6 all-gather.6
  222.3 28.8 all-gather.6
  354.4 28.6 all-gather.6
  486.9 28.6 all-gather.6

commit v6 on v5

--- a/solution.py
+++ b/solution.py
@@ -79,6 +79,12 @@
     )(index.reshape(-1), counts, tiles, basis)
 
 
+def gather_rows(x, axis):
+    n = lax.axis_size(axis)
+    got = lax.all_to_all(jnp.broadcast_to(x, (n,) + x.shape), axis, 0, 0, tiled=False)
+    return got.reshape((-1,) + x.shape[1:])
+
+
 def sum_scatter_rows(x, axis):
     n = lax.axis_size(axis)
     got = lax.all_to_all(x.reshape((n, -1) + x.shape[1:]), axis, 0, 0, tiled=False)
@@ -104,22 +110,23 @@
     scale = degree_scale[:, None]
     probe = (basis.astype(jnp.float32) * scale).astype(jnp.bfloat16)
     number = lax.axis_size("col") * rows_dev // tile
-    scale_block = lax.all_gather(scale, "row", axis=0, tiled=True)
+    scale_block = gather_rows(degree_scale, "row")[:, None]
 
     def loop_step(i, carry):
         block_probe = carry[0]
         result = apply_tiles(tiles, block_probe, index, counts)
         summed = sum_scatter_rows(result.reshape(number * tile, width), "col")
         image = summed * scale
-        image_block = lax.all_gather(image, "row", axis=0, tiled=True)
         gram = sum_all(gram_of(image, nodes), ("row", "col"))
+        image_late, gram = lax.optimization_barrier((image, gram))
+        image_block = lax.all_gather(image_late, "row", axis=0, tiled=True)
         gram = (gram + gram.T) * 0.5
         lower, inverse = cholesky_and_inverse(gram)
         embedding = dot_hi(image, inverse.T)
         next_probe = (dot_hi(image_block, inverse.T) * scale_block).astype(jnp.bfloat16)
         return (next_probe, embedding, lower.T)
 
-    start = (lax.all_gather(probe, "row", axis=0, tiled=True), jnp.zeros(basis.shape, jnp.float32), jnp.zeros((width, width), jnp.float32))
+    start = (gather_rows(probe, "row"), jnp.zeros(basis.shape, jnp.float32), jnp.zeros((width, width), jnp.float32))
     _, embedding, factor = lax.fori_loop(0, ITERS, loop_step, start)
     return (embedding, factor)
 

time: 580 us -> 555 us (0.957)
  blocking collectives: 140 us -> 255 us
  waiting for transfers between devices: 118 us -> 18.5 us
  starting transfers between devices: 37.1 us -> 10.1 us
    all_to_all x0 -> x8, blocking collectives: none -> 125 us  [the longest x4 64.5 us: sum_all(): lax.all_to_all(x.reshape(n, -1), axes, 0, 0, tiled=False)]
    all_to_all x8 -> x2, waiting for transfers between devices: 101 us -> 18.4 us  [gather_rows(): lax.all_to_all(jnp.broadcast_to(x, (n,) + x.shape), axis, 0, 0, tiled=False)]
    all_to_all x8 -> x2, starting transfers between devices: 36.9 us -> 9.95 us  [gather_rows(): lax.all_to_all(jnp.broadcast_to(x, (n,) + x.shape), axis, 0, 0, tiled=False)]
    all_gather x5 -> x4, waiting for transfers between devices: 15.2 us -> 0.01 us  [loop_step(): image_block = lax.all_gather(image_late, 'row', axis=0, tiled=True)]
    all_gather x1 -> x0, blocking collectives: 12.1 us -> none  [body(): scale_block = lax.all_gather(scale, 'row', axis=0, tiled=True)]
  transfers between devices with their start and end apart: 13 -> 6, of which waited for: 9 -> 2; matrix products, arithmetic and copies ran while one was open for 36% -> 36% of each run, Pallas kernels for 0% -> 0%
where the time goes in v6:
time: 555 us; the launch traced here: 554 us
  blocking collectives  255 us (46%)
  other arithmetic  192 us (35%)
  Pallas kernels  29.4 us (5%)
  matrix products  27 us (5%)
  waiting for transfers between devices  18.5 us (3%)
  between operations  13.7 us (2%)
  starting transfers between devices  10.1 us (2%)
  local copies, waits for them, and re-layouts  8.12 us (1%)
    all_to_all x4, blocking collectives, sum_scatter_rows(): lax.all_to_all(x.reshape((n, -1) + x.shape[1:]), axis, 0, 0, tiled=False)  129 us
    another operation x24, other arithmetic, cholesky_and_inverse(): lower = jnp.linalg.cholesky(g)  99.1 us
    another operation x16, other arithmetic, cholesky_and_inverse(): return (lower, jax.scipy.linalg.solve_triangular(lower, eye, lower=True))  83.7 us
    all_to_all x4, blocking collectives, sum_all(): lax.all_to_all(x.reshape(n, -1), axes, 0, 0, tiled=False)  64.5 us
    all_to_all x4, blocking collectives, sum_all(): lax.all_to_all(jnp.broadcast_to(piece, (n,) + piece.shape), axes, 0, 0, t...  60.9 us
    pallas_call x4, Pallas kernels, apply_tiles(): pl.pallas_call(kernel, grid_spec=spec, out_shape=jax.ShapeDtypeStruct((tr...  29.4 us
    dot_general x24, matrix products, dot_hi(): jnp.dot(a, b, precision=lax.Precision.HIGHEST, preferred_element_type=jnp...  22.4 us
    all_to_all x2, waiting for transfers between devices, gather_rows(): lax.all_to_all(jnp.broadcast_to(x, (n,) + x.shape), axis, 0, 0, tiled=False)  18.4 us
  transfers between devices with their start and end apart: 6, of which 2 were waited for; matrix products, arithmetic and copies ran while one was open for 36% of the time, Pallas kernels for 0%

profile of v6, /device:TPU:1, one launch (start us, length us, event | category | flops | bytes accessed | tf_op | source)
XLA Modules:
  0.0 554.4 jit_solution(17415569812790573561)
XLA Ops:
  24.3 14.8 %all-to-all-done.3 = bf16[8,256,256]{2,1,0:T(8,128)(2,1)S(1)} async-done(((bf16[8,256,256]{2,1,0:T(8,128)(2,1)}), bf16[8,256,256]{2,1,0:T(8,128)(2,1)S(1)}, u32[]{:S(2)}, u32[]{:S(2)}) %all-to-all-start.3) | async-done | bytes 1048608 | tf_op jit(solution)/shard_map/all_to_all | solution.py:84
  39.2 506.9 %while.15 = (s32[]{:T(128)}, bf16[2048,256]{1,0:T(8,128)(2,1)S(1)}, f32[256,256]{1,0:T(8,128)}, f32[256,256]{0,1:T(8,128)}, s32[32,1,8]{2,0,1:T(8,128)}, /*index...) while((s32[]{:T(128)}, bf16[2048,256]{1,0:T(8,128)(2,1)S(1)}, ...), condition=%wide.wide.region_5.8_spmd, body=%wide.wide.region_0.7_spmd.sunk | while | flops 2168848128 | bytes 28458212 | solution.py:130
  46.6 35.1 %all_to_all.40 = bf16[16,256,256]{2,1,0:T(8,128)(2,1)S(1)} all-to-all(bf16[16,256,256]{2,1,0:T(8,128)(2,1)} %bitcast.112), channel_id=1, replica_groups=mesh['row'=8,'col'=16] {'col'}, dimensions={0} | all-to-all | bytes 4194304 | tf_op jit(solution)/shard_map/while/body/eval_jaxpr/all_to_all | solution.py:90
  82.9 16.5 %all_to_all.41 = f32[128,1,512]{2,1,0:T(1,128)S(1)} all-to-all(f32[128,1,512]{2,1,0:T(1,128)S(1)} %all_to_all.32), channel_id=1, replica_groups=mesh['row'=8,'col'=16] {'row','col'}, dimensions={0} | all-to-all | bytes 524288 | tf_op jit(solution)/shard_map/while/body/eval_jaxpr/all_to_all | solution.py:98
  99.8 15.2 %all_to_all.42 = f32[128,1,512]{2,1,0:T(1,128)S(1)} all-to-all(f32[128,1,512]{2,1,0:T(1,128)S(1)} %broadcast_in_dim.18), channel_id=1, replica_groups=mesh['row'=8,'col'=16] {'row','col'}, dimensions={0} | all-to-all | bytes 524288 | tf_op jit(solution)/shard_map/while/body/eval_jaxpr/all_to_all | solution.py:99
  116.0 11.7 %cholesky.172 = f32[128,128]{1,0:T(8,128)S(1)} custom-call(f32[128,128]{1,0:T(8,128)S(1)} %fusion.107), custom_call_target="Cholesky" | custom-call | tf_op jit(solution)/shard_map/while/body/eval_jaxpr/jit(cholesky)/cholesky | solution.py:34
  129.1 9.8 %custom-call.14 = f32[1,128,128]{1,2,0:T(8,128)S(1)} custom-call(f32[1,128,128]{2,1,0:T(8,128)S(1)} %get-tuple-element.214), custom_call_target="InvertDiagBlocksLowerTriangular" | custom-call | tf_op jit(solution)/shard_map/while/body/eval_jaxpr/jit(_solve_triangular)/triangular_solve | solution.py:36
  139.9 11.7 %cholesky.173 = f32[128,128]{1,0:T(8,128)S(1)} custom-call(f32[128,128]{1,0:T(8,128)S(1)} %fusion.110), custom_call_target="Cholesky" | custom-call | tf_op jit(solution)/shard_map/while/body/eval_jaxpr/jit(cholesky)/cholesky | solution.py:34
  152.9 9.8 %custom-call.15 = f32[1,128,128]{1,2,0:T(8,128)S(1)} custom-call(f32[1,128,128]{2,1,0:T(8,128)S(1)} %get-tuple-element.215), custom_call_target="InvertDiagBlocksLowerTriangular" | custom-call | tf_op jit(solution)/shard_map/while/body/eval_jaxpr/jit(_solve_triangular)/triangular_solve | solution.py:36
  176.4 31.4 %all_to_all.40 = bf16[16,256,256]{2,1,0:T(8,128)(2,1)S(1)} all-to-all(bf16[16,256,256]{2,1,0:T(8,128)(2,1)} %bitcast.112), channel_id=1, replica_groups=mesh['row'=8,'col'=16] {'col'}, dimensions={0} | all-to-all | bytes 4194304 | tf_op jit(solution)/shard_map/while/body/eval_jaxpr/all_to_all | solution.py:90
  209.1 16.0 %all_to_all.41 = f32[128,1,512]{2,1,0:T(1,128)S(1)} all-to-all(f32[128,1,512]{2,1,0:T(1,128)S(1)} %all_to_all.32), channel_id=1, replica_groups=mesh['row'=8,'col'=16] {'row','col'}, dimensions={0} | all-to-all | bytes 524288 | tf_op jit(solution)/shard_map/while/body/eval_jaxpr/all_to_all | solution.py:98
  225.4 15.2 %all_to_all.42 = f32[128,1,512]{2,1,0:T(1,128)S(1)} all-to-all(f32[128,1,512]{2,1,0:T(1,128)S(1)} %broadcast_in_dim.18), channel_id=1, replica_groups=mesh['row'=8,'col'=16] {'row','col'}, dimensions={0} | all-to-all | bytes 524288 | tf_op jit(solution)/shard_map/while/body/eval_jaxpr/all_to_all | solution.py:99
  241.7 11.7 %cholesky.172 = f32[128,128]{1,0:T(8,128)S(1)} custom-call(f32[128,128]{1,0:T(8,128)S(1)} %fusion.107), custom_call_target="Cholesky" | custom-call | tf_op jit(solution)/shard_map/while/body/eval_jaxpr/jit(cholesky)/cholesky | solution.py:34
  265.6 11.7 %cholesky.173 = f32[128,128]{1,0:T(8,128)S(1)} custom-call(f32[128,128]{1,0:T(8,128)S(1)} %fusion.110), custom_call_target="Cholesky" | custom-call | tf_op jit(solution)/shard_map/while/body/eval_jaxpr/jit(cholesky)/cholesky | solution.py:34
  302.1 31.4 %all_to_all.40 = bf16[16,256,256]{2,1,0:T(8,128)(2,1)S(1)} all-to-all(bf16[16,256,256]{2,1,0:T(8,128)(2,1)} %bitcast.112), channel_id=1, replica_groups=mesh['row'=8,'col'=16] {'col'}, dimensions={0} | all-to-all | bytes 4194304 | tf_op jit(solution)/shard_map/while/body/eval_jaxpr/all_to_all | solution.py:90
  334.8 16.0 %all_to_all.41 = f32[128,1,512]{2,1,0:T(1,128)S(1)} all-to-all(f32[128,1,512]{2,1,0:T(1,128)S(1)} %all_to_all.32), channel_id=1, replica_groups=mesh['row'=8,'col'=16] {'row','col'}, dimensions={0} | all-to-all | bytes 524288 | tf_op jit(solution)/shard_map/while/body/eval_jaxpr/all_to_all | solution.py:98
  351.1 15.2 %all_to_all.42 = f32[128,1,512]{2,1,0:T(1,128)S(1)} all-to-all(f32[128,1,512]{2,1,0:T(1,128)S(1)} %broadcast_in_dim.18), channel_id=1, replica_groups=mesh['row'=8,'col'=16] {'row','col'}, dimensions={0} | all-to-all | bytes 524288 | tf_op jit(solution)/shard_map/while/body/eval_jaxpr/all_to_all | solution.py:99
  367.4 11.7 %cholesky.172 = f32[128,128]{1,0:T(8,128)S(1)} custom-call(f32[128,128]{1,0:T(8,128)S(1)} %fusion.107), custom_call_target="Cholesky" | custom-call | tf_op jit(solution)/shard_map/while/body/eval_jaxpr/jit(cholesky)/cholesky | solution.py:34
  391.3 11.7 %cholesky.173 = f32[128,128]{1,0:T(8,128)S(1)} custom-call(f32[128,128]{1,0:T(8,128)S(1)} %fusion.110), custom_call_target="Cholesky" | custom-call | tf_op jit(solution)/shard_map/while/body/eval_jaxpr/jit(cholesky)/cholesky | solution.py:34
  427.8 31.4 %all_to_all.40 = bf16[16,256,256]{2,1,0:T(8,128)(2,1)S(1)} all-to-all(bf16[16,256,256]{2,1,0:T(8,128)(2,1)} %bitcast.112), channel_id=1, replica_groups=mesh['row'=8,'col'=16] {'col'}, dimensions={0} | all-to-all | bytes 4194304 | tf_op jit(solution)/shard_map/while/body/eval_jaxpr/all_to_all | solution.py:90
  460.5 16.0 %all_to_all.41 = f32[128,1,512]{2,1,0:T(1,128)S(1)} all-to-all(f32[128,1,512]{2,1,0:T(1,128)S(1)} %all_to_all.32), channel_id=1, replica_groups=mesh['row'=8,'col'=16] {'row','col'}, dimensions={0} | all-to-all | bytes 524288 | tf_op jit(solution)/shard_map/while/body/eval_jaxpr/all_to_all | solution.py:98
  476.8 15.2 %all_to_all.42 = f32[128,1,512]{2,1,0:T(1,128)S(1)} all-to-all(f32[128,1,512]{2,1,0:T(1,128)S(1)} %broadcast_in_dim.18), channel_id=1, replica_groups=mesh['row'=8,'col'=16] {'row','col'}, dimensions={0} | all-to-all | bytes 524288 | tf_op jit(solution)/shard_map/while/body/eval_jaxpr/all_to_all | solution.py:99
  493.1 11.7 %cholesky.172 = f32[128,128]{1,0:T(8,128)S(1)} custom-call(f32[128,128]{1,0:T(8,128)S(1)} %fusion.107), custom_call_target="Cholesky" | custom-call | tf_op jit(solution)/shard_map/while/body/eval_jaxpr/jit(cholesky)/cholesky | solution.py:34
  516.9 11.7 %cholesky.173 = f32[128,128]{1,0:T(8,128)S(1)} custom-call(f32[128,128]{1,0:T(8,128)S(1)} %fusion.110), custom_call_target="Cholesky" | custom-call | tf_op jit(solution)/shard_map/while/body/eval_jaxpr/jit(cholesky)/cholesky | solution.py:34
  (185 shorter events, 157.0 us)
Async XLA Ops:
  7.2 32.0 %copy-start.3 = (f32[256]{0:T(256)S(1)}, f32[256]{0:T(256)}, u32[]{:S(2)}) copy-start(f32[256]{0:T(256)} %param.11) | copy-start | bytes 3076
  7.2 17.0 %copy-start.5 = (s32[32,1,8]{0,2,1:T(8,128)S(1)}, s32[32,1,8]{0,2,1:T(8,128)}, u32[]{:S(2)}) copy-start(s32[32,1,8]{0,2,1:T(8,128)} %param.13) | copy-start | bytes 3076
  7.2 32.0 %copy-start.4 = (s32[32,1]{0,1:T(1,128)S(1)}, s32[32,1]{0,1:T(1,128)}, u32[]{:S(2)}) copy-start(s32[32,1]{0,1:T(1,128)} %param.14) | copy-start | bytes 388
  8.5 10.4 %all-to-all-start.4 = ((f32[8,1,256]{2,1,0:T(1,128)}), f32[8,1,256]{2,1,0:T(1,128)S(1)}, u32[]{:S(2)}, u32[]{:S(2)}) async-start(f32[8,1,256]{2,1,0:T(1,128)} %broadcast_in_dim.15), calls=%async_computation.4 | async-start | bytes 16384 | tf_op jit(solution)/shard_map/all_to_all | solution.py:84
  20.0 19.2 %all-to-all-start.3 = ((bf16[8,256,256]{2,1,0:T(8,128)(2,1)}), bf16[8,256,256]{2,1,0:T(8,128)(2,1)S(1)}, u32[]{:S(2)}, u32[]{:S(2)}) async-start(bf16[8,256,256]{2,1,0:T(8,128)(2,1)} %broadcast_in_dim.13), calls=%async_computation.3 | async-start | bytes 2097152 | tf_op jit(solution)/shard_map/all_to_all | solution.py:84
  24.2 14.9 %copy-start.2 = (s32[32,1,8]{2,0,1:T(8,128)}, s32[32,1,8]{2,0,1:T(8,128)S(1)}, u32[]{:S(2)}) copy-start(s32[32,1,8]{2,0,1:T(8,128)S(1)} %copy.35) | copy-start | bytes 3076
  39.2 126.4 %all-gather.2.cloned.1.call-start = ((), (), s32[]{:S(2)}) async-start(), calls=%async_computation.5 | async-start | bytes 2359296 | tf_op jit(solution)/shard_map/while/body/eval_jaxpr/all_gather | solution.py:122
  82.0 33.6 %copy-start = (f32[256,256]{1,0:T(8,128)}, f32[256,256]{1,0:T(8,128)S(1)}, u32[]{:S(2)}) copy-start(f32[256,256]{1,0:T(8,128)S(1)} %broadcast_multiply_fusion.3) | copy-start | bytes 786436 | tf_op jit(solution)/shard_map/while
  115.8 48.6 %copy-start.1 = (f32[256,256]{1,0:T(8,128)S(1)}, f32[256,256]{1,0:T(8,128)}, u32[]{:S(2)}) copy-start(f32[256,256]{1,0:T(8,128)} %copy-done) | copy-start | bytes 786436 | tf_op jit(solution)/shard_map/while
  169.0 122.2 %all-gather.2.cloned.1.call-start = ((), (), s32[]{:S(2)}) async-start(), calls=%async_computation.5 | async-start | bytes 2359296 | tf_op jit(solution)/shard_map/while/body/eval_jaxpr/all_gather | solution.py:122
  208.2 33.1 %copy-start = (f32[256,256]{1,0:T(8,128)}, f32[256,256]{1,0:T(8,128)S(1)}, u32[]{:S(2)}) copy-start(f32[256,256]{1,0:T(8,128)S(1)} %broadcast_multiply_fusion.3) | copy-start | bytes 786436 | tf_op jit(solution)/shard_map/while
  241.5 48.6 %copy-start.1 = (f32[256,256]{1,0:T(8,128)S(1)}, f32[256,256]{1,0:T(8,128)}, u32[]{:S(2)}) copy-start(f32[256,256]{1,0:T(8,128)} %copy-done) | copy-start | bytes 786436 | tf_op jit(solution)/shard_map/while
  294.7 122.2 %all-gather.2.cloned.1.call-start = ((), (), s32[]{:S(2)}) async-start(), calls=%async_computation.5 | async-start | bytes 2359296 | tf_op jit(solution)/shard_map/while/body/eval_jaxpr/all_gather | solution.py:122
  333.9 33.1 %copy-start = (f32[256,256]{1,0:T(8,128)}, f32[256,256]{1,0:T(8,128)S(1)}, u32[]{:S(2)}) copy-start(f32[256,256]{1,0:T(8,128)S(1)} %broadcast_multiply_fusion.3) | copy-start | bytes 786436 | tf_op jit(solution)/shard_map/while
  367.2 48.6 %copy-start.1 = (f32[256,256]{1,0:T(8,128)S(1)}, f32[256,256]{1,0:T(8,128)}, u32[]{:S(2)}) copy-start(f32[256,256]{1,0:T(8,128)} %copy-done) | copy-start | bytes 786436 | tf_op jit(solution)/shard_map/while
  420.4 122.2 %all-gather.2.cloned.1.call-start = ((), (), s32[]{:S(2)}) async-start(), calls=%async_computation.5 | async-start | bytes 2359296 | tf_op jit(solution)/shard_map/while/body/eval_jaxpr/all_gather | solution.py:122
  459.6 33.1 %copy-start = (f32[256,256]{1,0:T(8,128)}, f32[256,256]{1,0:T(8,128)S(1)}, u32[]{:S(2)}) copy-start(f32[256,256]{1,0:T(8,128)S(1)} %broadcast_multiply_fusion.3) | copy-start | bytes 786436 | tf_op jit(solution)/shard_map/while
  492.9 48.6 %copy-start.1 = (f32[256,256]{1,0:T(8,128)S(1)}, f32[256,256]{1,0:T(8,128)}, u32[]{:S(2)}) copy-start(f32[256,256]{1,0:T(8,128)} %copy-done) | copy-start | bytes 786436 | tf_op jit(solution)/shard_map/while
Sparse Core Ops, SparseCore 0:
  115.8 21.4 all-gather.1
  241.5 21.4 all-gather.1
  367.2 21.4 all-gather.1
  492.9 21.4 all-gather.1

commit v7 on v6

--- a/solution.py
+++ b/solution.py
@@ -122,12 +122,14 @@
         image_block = lax.all_gather(image_late, "row", axis=0, tiled=True)
         gram = (gram + gram.T) * 0.5
         lower, inverse = cholesky_and_inverse(gram)
-        embedding = dot_hi(image, inverse.T)
         next_probe = (dot_hi(image_block, inverse.T) * scale_block).astype(jnp.bfloat16)
-        return (next_probe, embedding, lower.T)
+        return (next_probe, image, inverse, lower)
 
-    start = (gather_rows(probe, "row"), jnp.zeros(basis.shape, jnp.float32), jnp.zeros((width, width), jnp.float32))
-    _, embedding, factor = lax.fori_loop(0, ITERS, loop_step, start)
+    square = jnp.zeros((width, width), jnp.float32)
+    start = (gather_rows(probe, "row"), jnp.zeros(basis.shape, jnp.float32), square, square)
+    _, image, inverse, lower = lax.fori_loop(0, ITERS, loop_step, start)
+    embedding = dot_hi(image, inverse.T)
+    factor = lower.T
     return (embedding, factor)
 
 

time: 555 us -> 554 us (level)
    dot_general x24 -> x21, matrix products: 22.4 us -> 20.5 us  [dot_hi(): jnp.dot(a, b, precision=lax.Precision.HIGHEST, preferred_element_type=jnp...]
  transfers between devices with their start and end apart: 6 -> 6, of which waited for: 2 -> 2; matrix products, arithmetic and copies ran while one was open for 36% -> 35% of each run, Pallas kernels for 0% -> 0%
where the time goes in v7:
time: 554 us; the launch traced here: 552 us
  blocking collectives  255 us (46%)
  other arithmetic  192 us (35%)
  Pallas kernels  29.4 us (5%)
  matrix products  25.1 us (5%)
  waiting for transfers between devices  18.5 us (3%)
  between operations  13.8 us (2%)
  starting transfers between devices  10.1 us (2%)
  local copies, waits for them, and re-layouts  8.1 us (1%)
    all_to_all x4, blocking collectives, sum_scatter_rows(): lax.all_to_all(x.reshape((n, -1) + x.shape[1:]), axis, 0, 0, tiled=False)  129 us
    another operation x24, other arithmetic, cholesky_and_inverse(): lower = jnp.linalg.cholesky(g)  99.1 us
    another operation x16, other arithmetic, cholesky_and_inverse(): return (lower, jax.scipy.linalg.solve_triangular(lower, eye, lower=True))  83.7 us
    all_to_all x4, blocking collectives, sum_all(): lax.all_to_all(x.reshape(n, -1), axes, 0, 0, tiled=False)  64.5 us
    all_to_all x4, blocking collectives, sum_all(): lax.all_to_all(jnp.broadcast_to(piece, (n,) + piece.shape), axes, 0, 0, t...  60.9 us
    pallas_call x4, Pallas kernels, apply_tiles(): pl.pallas_call(kernel, grid_spec=spec, out_shape=jax.ShapeDtypeStruct((tr...  29.4 us
    dot_general x21, matrix products, dot_hi(): jnp.dot(a, b, precision=lax.Precision.HIGHEST, preferred_element_type=jnp...  20.5 us
    all_to_all x2, waiting for transfers between devices, gather_rows(): lax.all_to_all(jnp.broadcast_to(x, (n,) + x.shape), axis, 0, 0, tiled=False)  18.4 us
  transfers between devices with their start and end apart: 6, of which 2 were waited for; matrix products, arithmetic and copies ran while one was open for 35% of the time, Pallas kernels for 0%

profile of v7, /device:TPU:1, one launch (start us, length us, event | category | flops | bytes accessed | tf_op | source)
XLA Modules:
  0.0 552.4 jit_solution(4490421254883455321)
XLA Ops:
  24.3 14.8 %all-to-all-done.3 = bf16[8,256,256]{2,1,0:T(8,128)(2,1)S(1)} async-done(((bf16[8,256,256]{2,1,0:T(8,128)(2,1)}), bf16[8,256,256]{2,1,0:T(8,128)(2,1)S(1)}, u32[]{:S(2)}, u32[]{:S(2)}) %all-to-all-start.3) | async-done | bytes 1048608 | tf_op jit(solution)/shard_map/all_to_all | solution.py:84
  39.2 502.8 %while.17 = (s32[]{:T(128)}, bf16[2048,256]{1,0:T(8,128)(2,1)S(1)}, f32[256,256]{1,0:T(8,128)}, f32[256,256]{1,0:T(8,128)}, f32[256,256]{1,0:T(8,128)}, /*index=...) while((s32[]{:T(128)}, bf16[2048,256]{1,0:T(8,128)(2,1)S(1)}, ...), condition=%wide.wide.region_5.8_spmd, body=%wide.wide.region_0.7_spmd.sunk | while | flops 1967193856 | bytes 28261612 | solution.py:130
  46.6 35.1 %all_to_all.40 = bf16[16,256,256]{2,1,0:T(8,128)(2,1)S(1)} all-to-all(bf16[16,256,256]{2,1,0:T(8,128)(2,1)} %bitcast.110), channel_id=1, replica_groups=mesh['row'=8,'col'=16] {'col'}, dimensions={0} | all-to-all | bytes 4194304 | tf_op jit(solution)/shard_map/while/body/eval_jaxpr/all_to_all | solution.py:90
  82.9 16.5 %all_to_all.41 = f32[128,1,512]{2,1,0:T(1,128)S(1)} all-to-all(f32[128,1,512]{2,1,0:T(1,128)S(1)} %all_to_all.32), channel_id=1, replica_groups=mesh['row'=8,'col'=16] {'row','col'}, dimensions={0} | all-to-all | bytes 524288 | tf_op jit(solution)/shard_map/while/body/eval_jaxpr/all_to_all | solution.py:98
  99.8 15.2 %all_to_all.42 = f32[128,1,512]{2,1,0:T(1,128)S(1)} all-to-all(f32[128,1,512]{2,1,0:T(1,128)S(1)} %broadcast_in_dim.18), channel_id=1, replica_groups=mesh['row'=8,'col'=16] {'row','col'}, dimensions={0} | all-to-all | bytes 524288 | tf_op jit(solution)/shard_map/while/body/eval_jaxpr/all_to_all | solution.py:99
  116.0 11.7 %cholesky.172 = f32[128,128]{1,0:T(8,128)S(1)} custom-call(f32[128,128]{1,0:T(8,128)S(1)} %fusion.94), custom_call_target="Cholesky" | custom-call | tf_op jit(solution)/shard_map/while/body/eval_jaxpr/jit(cholesky)/cholesky | solution.py:34
  139.9 11.7 %cholesky.173 = f32[128,128]{1,0:T(8,128)S(1)} custom-call(f32[128,128]{1,0:T(8,128)S(1)} %fusion.97), custom_call_target="Cholesky" | custom-call | tf_op jit(solution)/shard_map/while/body/eval_jaxpr/jit(cholesky)/cholesky | solution.py:34
  175.4 31.4 %all_to_all.40 = bf16[16,256,256]{2,1,0:T(8,128)(2,1)S(1)} all-to-all(bf16[16,256,256]{2,1,0:T(8,128)(2,1)} %bitcast.110), channel_id=1, replica_groups=mesh['row'=8,'col'=16] {'col'}, dimensions={0} | all-to-all | bytes 4194304 | tf_op jit(solution)/shard_map/while/body/eval_jaxpr/all_to_all | solution.py:90
  208.0 16.0 %all_to_all.41 = f32[128,1,512]{2,1,0:T(1,128)S(1)} all-to-all(f32[128,1,512]{2,1,0:T(1,128)S(1)} %all_to_all.32), channel_id=1, replica_groups=mesh['row'=8,'col'=16] {'row','col'}, dimensions={0} | all-to-all | bytes 524288 | tf_op jit(solution)/shard_map/while/body/eval_jaxpr/all_to_all | solution.py:98
  224.4 15.2 %all_to_all.42 = f32[128,1,512]{2,1,0:T(1,128)S(1)} all-to-all(f32[128,1,512]{2,1,0:T(1,128)S(1)} %broadcast_in_dim.18), channel_id=1, replica_groups=mesh['row'=8,'col'=16] {'row','col'}, dimensions={0} | all-to-all | bytes 524288 | tf_op jit(solution)/shard_map/while/body/eval_jaxpr/all_to_all | solution.py:99
  240.7 11.7 %cholesky.172 = f32[128,128]{1,0:T(8,128)S(1)} custom-call(f32[128,128]{1,0:T(8,128)S(1)} %fusion.94), custom_call_target="Cholesky" | custom-call | tf_op jit(solution)/shard_map/while/body/eval_jaxpr/jit(cholesky)/cholesky | solution.py:34
  253.7 9.8 %custom-call.15 = f32[1,128,128]{1,2,0:T(8,128)S(1)} custom-call(f32[1,128,128]{2,1,0:T(8,128)S(1)} %get-tuple-element.223), custom_call_target="InvertDiagBlocksLowerTriangular" | custom-call | tf_op jit(solution)/shard_map/while/body/eval_jaxpr/jit(_solve_triangular)/triangular_solve | solution.py:36
  264.5 11.7 %cholesky.173 = f32[128,128]{1,0:T(8,128)S(1)} custom-call(f32[128,128]{1,0:T(8,128)S(1)} %fusion.97), custom_call_target="Cholesky" | custom-call | tf_op jit(solution)/shard_map/while/body/eval_jaxpr/jit(cholesky)/cholesky | solution.py:34
  300.1 31.4 %all_to_all.40 = bf16[16,256,256]{2,1,0:T(8,128)(2,1)S(1)} all-to-all(bf16[16,256,256]{2,1,0:T(8,128)(2,1)} %bitcast.110), channel_id=1, replica_groups=mesh['row'=8,'col'=16] {'col'}, dimensions={0} | all-to-all | bytes 4194304 | tf_op jit(solution)/shard_map/while/body/eval_jaxpr/all_to_all | solution.py:90
  332.7 16.0 %all_to_all.41 = f32[128,1,512]{2,1,0:T(1,128)S(1)} all-to-all(f32[128,1,512]{2,1,0:T(1,128)S(1)} %all_to_all.32), channel_id=1, replica_groups=mesh['row'=8,'col'=16] {'row','col'}, dimensions={0} | all-to-all | bytes 524288 | tf_op jit(solution)/shard_map/while/body/eval_jaxpr/all_to_all | solution.py:98
  349.1 15.2 %all_to_all.42 = f32[128,1,512]{2,1,0:T(1,128)S(1)} all-to-all(f32[128,1,512]{2,1,0:T(1,128)S(1)} %broadcast_in_dim.18), channel_id=1, replica_groups=mesh['row'=8,'col'=16] {'row','col'}, dimensions={0} | all-to-all | bytes 524288 | tf_op jit(solution)/shard_map/while/body/eval_jaxpr/all_to_all | solution.py:99
  365.3 11.7 %cholesky.172 = f32[128,128]{1,0:T(8,128)S(1)} custom-call(f32[128,128]{1,0:T(8,128)S(1)} %fusion.94), custom_call_target="Cholesky" | custom-call | tf_op jit(solution)/shard_map/while/body/eval_jaxpr/jit(cholesky)/cholesky | solution.py:34
  389.2 11.7 %cholesky.173 = f32[128,128]{1,0:T(8,128)S(1)} custom-call(f32[128,128]{1,0:T(8,128)S(1)} %fusion.97), custom_call_target="Cholesky" | custom-call | tf_op jit(solution)/shard_map/while/body/eval_jaxpr/jit(cholesky)/cholesky | solution.py:34
  402.2 9.8 %custom-call.16 = f32[1,128,128]{1,2,0:T(8,128)S(1)} custom-call(f32[1,128,128]{2,1,0:T(8,128)S(1)} %get-tuple-element.225), custom_call_target="InvertDiagBlocksLowerTriangular" | custom-call | tf_op jit(solution)/shard_map/while/body/eval_jaxpr/jit(_solve_triangular)/triangular_solve | solution.py:36
  424.7 31.4 %all_to_all.40 = bf16[16,256,256]{2,1,0:T(8,128)(2,1)S(1)} all-to-all(bf16[16,256,256]{2,1,0:T(8,128)(2,1)} %bitcast.110), channel_id=1, replica_groups=mesh['row'=8,'col'=16] {'col'}, dimensions={0} | all-to-all | bytes 4194304 | tf_op jit(solution)/shard_map/while/body/eval_jaxpr/all_to_all | solution.py:90
  457.4 16.0 %all_to_all.41 = f32[128,1,512]{2,1,0:T(1,128)S(1)} all-to-all(f32[128,1,512]{2,1,0:T(1,128)S(1)} %all_to_all.32), channel_id=1, replica_groups=mesh['row'=8,'col'=16] {'row','col'}, dimensions={0} | all-to-all | bytes 524288 | tf_op jit(solution)/shard_map/while/body/eval_jaxpr/all_to_all | solution.py:98
  473.7 15.2 %all_to_all.42 = f32[128,1,512]{2,1,0:T(1,128)S(1)} all-to-all(f32[128,1,512]{2,1,0:T(1,128)S(1)} %broadcast_in_dim.18), channel_id=1, replica_groups=mesh['row'=8,'col'=16] {'row','col'}, dimensions={0} | all-to-all | bytes 524288 | tf_op jit(solution)/shard_map/while/body/eval_jaxpr/all_to_all | solution.py:99
  490.0 11.7 %cholesky.172 = f32[128,128]{1,0:T(8,128)S(1)} custom-call(f32[128,128]{1,0:T(8,128)S(1)} %fusion.94), custom_call_target="Cholesky" | custom-call | tf_op jit(solution)/shard_map/while/body/eval_jaxpr/jit(cholesky)/cholesky | solution.py:34
  513.8 11.7 %cholesky.173 = f32[128,128]{1,0:T(8,128)S(1)} custom-call(f32[128,128]{1,0:T(8,128)S(1)} %fusion.97), custom_call_target="Cholesky" | custom-call | tf_op jit(solution)/shard_map/while/body/eval_jaxpr/jit(cholesky)/cholesky | solution.py:34
  (183 shorter events, 155.0 us)
Async XLA Ops:
  7.2 32.0 %copy-start.3 = (f32[256]{0:T(256)S(1)}, f32[256]{0:T(256)}, u32[]{:S(2)}) copy-start(f32[256]{0:T(256)} %param.11) | copy-start | bytes 3076
  7.2 17.0 %copy-start.5 = (s32[32,1,8]{0,2,1:T(8,128)S(1)}, s32[32,1,8]{0,2,1:T(8,128)}, u32[]{:S(2)}) copy-start(s32[32,1,8]{0,2,1:T(8,128)} %param.13) | copy-start | bytes 3076
  7.2 32.0 %copy-start.4 = (s32[32,1]{0,1:T(1,128)S(1)}, s32[32,1]{0,1:T(1,128)}, u32[]{:S(2)}) copy-start(s32[32,1]{0,1:T(1,128)} %param.14) | copy-start | bytes 388
  8.5 10.4 %all-to-all-start.4 = ((f32[8,1,256]{2,1,0:T(1,128)}), f32[8,1,256]{2,1,0:T(1,128)S(1)}, u32[]{:S(2)}, u32[]{:S(2)}) async-start(f32[8,1,256]{2,1,0:T(1,128)} %broadcast_in_dim.15), calls=%async_computation.4 | async-start | bytes 16384 | tf_op jit(solution)/shard_map/all_to_all | solution.py:84
  20.0 19.2 %all-to-all-start.3 = ((bf16[8,256,256]{2,1,0:T(8,128)(2,1)}), bf16[8,256,256]{2,1,0:T(8,128)(2,1)S(1)}, u32[]{:S(2)}, u32[]{:S(2)}) async-start(bf16[8,256,256]{2,1,0:T(8,128)(2,1)} %broadcast_in_dim.13), calls=%async_computation.3 | async-start | bytes 2097152 | tf_op jit(solution)/shard_map/all_to_all | solution.py:84
  24.2 14.9 %copy-start.2 = (s32[32,1,8]{2,0,1:T(8,128)}, s32[32,1,8]{2,0,1:T(8,128)S(1)}, u32[]{:S(2)}) copy-start(s32[32,1,8]{2,0,1:T(8,128)S(1)} %copy.32) | copy-start | bytes 3076
  39.2 125.3 %all-gather.2.cloned.1.call-start = ((), (), s32[]{:S(2)}) async-start(), calls=%async_computation.5 | async-start | bytes 2359296 | tf_op jit(solution)/shard_map/while/body/eval_jaxpr/all_gather | solution.py:122
  82.0 33.6 %copy-start = (f32[256,256]{1,0:T(8,128)}, f32[256,256]{1,0:T(8,128)S(1)}, u32[]{:S(2)}) copy-start(f32[256,256]{1,0:T(8,128)S(1)} %broadcast_multiply_fusion.3) | copy-start | bytes 786436 | tf_op jit(solution)/shard_map/while
  164.4 3.5 copy-start.1
  168.0 121.1 %all-gather.2.cloned.1.call-start = ((), (), s32[]{:S(2)}) async-start(), calls=%async_computation.5 | async-start | bytes 2359296 | tf_op jit(solution)/shard_map/while/body/eval_jaxpr/all_gather | solution.py:122
  207.2 33.2 %copy-start = (f32[256,256]{1,0:T(8,128)}, f32[256,256]{1,0:T(8,128)S(1)}, u32[]{:S(2)}) copy-start(f32[256,256]{1,0:T(8,128)S(1)} %broadcast_multiply_fusion.3) | copy-start | bytes 786436 | tf_op jit(solution)/shard_map/while
  289.1 3.5 copy-start.1
  292.7 121.1 %all-gather.2.cloned.1.call-start = ((), (), s32[]{:S(2)}) async-start(), calls=%async_computation.5 | async-start | bytes 2359296 | tf_op jit(solution)/shard_map/while/body/eval_jaxpr/all_gather | solution.py:122
  331.9 33.1 %copy-start = (f32[256,256]{1,0:T(8,128)}, f32[256,256]{1,0:T(8,128)S(1)}, u32[]{:S(2)}) copy-start(f32[256,256]{1,0:T(8,128)S(1)} %broadcast_multiply_fusion.3) | copy-start | bytes 786436 | tf_op jit(solution)/shard_map/while
  413.8 3.5 copy-start.1
  417.3 121.1 %all-gather.2.cloned.1.call-start = ((), (), s32[]{:S(2)}) async-start(), calls=%async_computation.5 | async-start | bytes 2359296 | tf_op jit(solution)/shard_map/while/body/eval_jaxpr/all_gather | solution.py:122
  456.5 33.1 %copy-start = (f32[256,256]{1,0:T(8,128)}, f32[256,256]{1,0:T(8,128)S(1)}, u32[]{:S(2)}) copy-start(f32[256,256]{1,0:T(8,128)S(1)} %broadcast_multiply_fusion.3) | copy-start | bytes 786436 | tf_op jit(solution)/shard_map/while
  538.4 3.5 copy-start.1
Sparse Core Ops, SparseCore 0:
  115.8 21.4 all-gather.1
  240.5 21.4 all-gather.1
  365.1 21.4 all-gather.1
  489.8 21.4 all-gather.1

commit v8 on v7

--- a/solution.py
+++ b/solution.py
@@ -58,7 +58,7 @@
         out_ref[r] = jnp.dot(lhs, gat_ref[...], preferred_element_type=jnp.float32).astype(out_ref.dtype)
 
 
-def apply_tiles(tiles, basis, index, counts, rows_per_block=8):
+def apply_tiles(tiles, basis, index, counts, rows_per_block=16):
     trows, slots, tile, _ = tiles.shape
     width = basis.shape[-1]
     kernel = functools.partial(_apply_kernel, rows_per_block=rows_per_block, slots=slots, tile=tile)
@@ -122,7 +122,8 @@
         image_block = lax.all_gather(image_late, "row", axis=0, tiled=True)
         gram = (gram + gram.T) * 0.5
         lower, inverse = cholesky_and_inverse(gram)
-        next_probe = (dot_hi(image_block, inverse.T) * scale_block).astype(jnp.bfloat16)
+        normalized = jnp.dot(image_block, inverse.T, precision=lax.Precision.HIGH, preferred_element_type=jnp.float32)
+        next_probe = (normalized * scale_block).astype(jnp.bfloat16)
         return (next_probe, image, inverse, lower)
 
     square = jnp.zeros((width, width), jnp.float32)

time: 554 us -> 548 us (0.989)
    dot_general x21 -> x17, matrix products: 20.5 us -> 6.43 us  [dot_hi(): jnp.dot(a, b, precision=lax.Precision.HIGHEST, preferred_element_type=jnp...]
    dot_general x0 -> x4, matrix products: none -> 10.9 us  [loop_step(): jnp.dot(image_block, inverse.T, precision=lax.Precision.HIGH, preferred_e...]
  transfers between devices with their start and end apart: 6 -> 6, of which waited for: 2 -> 2; matrix products, arithmetic and copies ran while one was open for 35% -> 36% of each run, Pallas kernels for 0% -> 0%
where the time goes in v8:
time: 548 us; the launch traced here: 547 us
  blocking collectives  255 us (47%)
  other arithmetic  192 us (35%)
  Pallas kernels  27.1 us (5%)
  matrix products  21.9 us (4%)
  waiting for transfers between devices  18.5 us (3%)
  between operations  13.8 us (3%)
  starting transfers between devices  10.1 us (2%)
  local copies, waits for them, and re-layouts  8.1 us (1%)
    all_to_all x4, blocking collectives, sum_scatter_rows(): lax.all_to_all(x.reshape((n, -1) + x.shape[1:]), axis, 0, 0, tiled=False)  129 us
    another operation x24, other arithmetic, cholesky_and_inverse(): lower = jnp.linalg.cholesky(g)  99.1 us
    another operation x16, other arithmetic, cholesky_and_inverse(): return (lower, jax.scipy.linalg.solve_triangular(lower, eye, lower=True))  83.7 us
    all_to_all x4, blocking collectives, sum_all(): lax.all_to_all(x.reshape(n, -1), axes, 0, 0, tiled=False)  64.6 us
    all_to_all x4, blocking collectives, sum_all(): lax.all_to_all(jnp.broadcast_to(piece, (n,) + piece.shape), axes, 0, 0, t...  60.9 us
    pallas_call x4, Pallas kernels, apply_tiles(): pl.pallas_call(kernel, grid_spec=spec, out_shape=jax.ShapeDtypeStruct((tr...  27.1 us
    all_to_all x2, waiting for transfers between devices, gather_rows(): lax.all_to_all(jnp.broadcast_to(x, (n,) + x.shape), axis, 0, 0, tiled=False)  18.4 us
  transfers between devices with their start and end apart: 6, of which 2 were waited for; matrix products, arithmetic and copies ran while one was open for 36% of the time, Pallas kernels for 0%

profile of v8, /device:TPU:1, one launch (start us, length us, event | category | flops | bytes accessed | tf_op | source)
XLA Modules:
  0.0 546.8 jit_solution(11889977232513612701)
XLA Ops:
  24.3 14.8 %all-to-all-done.3 = bf16[8,256,256]{2,1,0:T(8,128)(2,1)S(1)} async-done(((bf16[8,256,256]{2,1,0:T(8,128)(2,1)}), bf16[8,256,256]{2,1,0:T(8,128)(2,1)S(1)}, u32[]{:S(2)}, u32[]{:S(2)}) %all-to-all-start.3) | async-done | bytes 1048608 | tf_op jit(solution)/shard_map/all_to_all | solution.py:84
  39.2 497.2 %while.17 = (s32[]{:T(128)}, bf16[2048,256]{1,0:T(8,128)(2,1)S(1)}, f32[256,256]{1,0:T(8,128)}, f32[256,256]{1,0:T(8,128)}, f32[256,256]{1,0:T(8,128)}, /*index=...) while((s32[]{:T(128)}, bf16[2048,256]{1,0:T(8,128)(2,1)S(1)}, ...), condition=%wide.wide.region_5.8_spmd, body=%wide.wide.region_0.7_spmd.sunk | while | flops 1161887488 | bytes 28261612 | solution.py:131
  46.0 35.0 %all_to_all.40 = bf16[16,256,256]{2,1,0:T(8,128)(2,1)S(1)} all-to-all(bf16[16,256,256]{2,1,0:T(8,128)(2,1)} %bitcast.110), channel_id=1, replica_groups=mesh['row'=8,'col'=16] {'col'}, dimensions={0} | all-to-all | bytes 4194304 | tf_op jit(solution)/shard_map/while/body/eval_jaxpr/all_to_all | solution.py:90
  82.3 16.5 %all_to_all.41 = f32[128,1,512]{2,1,0:T(1,128)S(1)} all-to-all(f32[128,1,512]{2,1,0:T(1,128)S(1)} %all_to_all.32), channel_id=1, replica_groups=mesh['row'=8,'col'=16] {'row','col'}, dimensions={0} | all-to-all | bytes 524288 | tf_op jit(solution)/shard_map/while/body/eval_jaxpr/all_to_all | solution.py:98
  99.2 15.2 %all_to_all.42 = f32[128,1,512]{2,1,0:T(1,128)S(1)} all-to-all(f32[128,1,512]{2,1,0:T(1,128)S(1)} %broadcast_in_dim.18), channel_id=1, replica_groups=mesh['row'=8,'col'=16] {'row','col'}, dimensions={0} | all-to-all | bytes 524288 | tf_op jit(solution)/shard_map/while/body/eval_jaxpr/all_to_all | solution.py:99
  115.4 11.7 %cholesky.172 = f32[128,128]{1,0:T(8,128)S(1)} custom-call(f32[128,128]{1,0:T(8,128)S(1)} %fusion.94), custom_call_target="Cholesky" | custom-call | tf_op jit(solution)/shard_map/while/body/eval_jaxpr/jit(cholesky)/cholesky | solution.py:34
  139.3 11.7 %cholesky.173 = f32[128,128]{1,0:T(8,128)S(1)} custom-call(f32[128,128]{1,0:T(8,128)S(1)} %fusion.97), custom_call_target="Cholesky" | custom-call | tf_op jit(solution)/shard_map/while/body/eval_jaxpr/jit(cholesky)/cholesky | solution.py:34
  152.3 9.8 %custom-call.16 = f32[1,128,128]{1,2,0:T(8,128)S(1)} custom-call(f32[1,128,128]{2,1,0:T(8,128)S(1)} %get-tuple-element.225), custom_call_target="InvertDiagBlocksLowerTriangular" | custom-call | tf_op jit(solution)/shard_map/while/body/eval_jaxpr/jit(_solve_triangular)/triangular_solve | solution.py:36
  173.4 31.4 %all_to_all.40 = bf16[16,256,256]{2,1,0:T(8,128)(2,1)S(1)} all-to-all(bf16[16,256,256]{2,1,0:T(8,128)(2,1)} %bitcast.110), channel_id=1, replica_groups=mesh['row'=8,'col'=16] {'col'}, dimensions={0} | all-to-all | bytes 4194304 | tf_op jit(solution)/shard_map/while/body/eval_jaxpr/all_to_all | solution.py:90
  206.1 16.0 %all_to_all.41 = f32[128,1,512]{2,1,0:T(1,128)S(1)} all-to-all(f32[128,1,512]{2,1,0:T(1,128)S(1)} %all_to_all.32), channel_id=1, replica_groups=mesh['row'=8,'col'=16] {'row','col'}, dimensions={0} | all-to-all | bytes 524288 | tf_op jit(solution)/shard_map/while/body/eval_jaxpr/all_to_all | solution.py:98
  222.4 15.2 %all_to_all.42 = f32[128,1,512]{2,1,0:T(1,128)S(1)} all-to-all(f32[128,1,512]{2,1,0:T(1,128)S(1)} %broadcast_in_dim.18), channel_id=1, replica_groups=mesh['row'=8,'col'=16] {'row','col'}, dimensions={0} | all-to-all | bytes 524288 | tf_op jit(solution)/shard_map/while/body/eval_jaxpr/all_to_all | solution.py:99
  238.7 11.7 %cholesky.172 = f32[128,128]{1,0:T(8,128)S(1)} custom-call(f32[128,128]{1,0:T(8,128)S(1)} %fusion.94), custom_call_target="Cholesky" | custom-call | tf_op jit(solution)/shard_map/while/body/eval_jaxpr/jit(cholesky)/cholesky | solution.py:34
  262.5 11.7 %cholesky.173 = f32[128,128]{1,0:T(8,128)S(1)} custom-call(f32[128,128]{1,0:T(8,128)S(1)} %fusion.97), custom_call_target="Cholesky" | custom-call | tf_op jit(solution)/shard_map/while/body/eval_jaxpr/jit(cholesky)/cholesky | solution.py:34
  296.7 31.4 %all_to_all.40 = bf16[16,256,256]{2,1,0:T(8,128)(2,1)S(1)} all-to-all(bf16[16,256,256]{2,1,0:T(8,128)(2,1)} %bitcast.110), channel_id=1, replica_groups=mesh['row'=8,'col'=16] {'col'}, dimensions={0} | all-to-all | bytes 4194304 | tf_op jit(solution)/shard_map/while/body/eval_jaxpr/all_to_all | solution.py:90
  329.3 16.0 %all_to_all.41 = f32[128,1,512]{2,1,0:T(1,128)S(1)} all-to-all(f32[128,1,512]{2,1,0:T(1,128)S(1)} %all_to_all.32), channel_id=1, replica_groups=mesh['row'=8,'col'=16] {'row','col'}, dimensions={0} | all-to-all | bytes 524288 | tf_op jit(solution)/shard_map/while/body/eval_jaxpr/all_to_all | solution.py:98
  345.7 15.2 %all_to_all.42 = f32[128,1,512]{2,1,0:T(1,128)S(1)} all-to-all(f32[128,1,512]{2,1,0:T(1,128)S(1)} %broadcast_in_dim.18), channel_id=1, replica_groups=mesh['row'=8,'col'=16] {'row','col'}, dimensions={0} | all-to-all | bytes 524288 | tf_op jit(solution)/shard_map/while/body/eval_jaxpr/all_to_all | solution.py:99
  361.9 11.7 %cholesky.172 = f32[128,128]{1,0:T(8,128)S(1)} custom-call(f32[128,128]{1,0:T(8,128)S(1)} %fusion.94), custom_call_target="Cholesky" | custom-call | tf_op jit(solution)/shard_map/while/body/eval_jaxpr/jit(cholesky)/cholesky | solution.py:34
  385.8 11.7 %cholesky.173 = f32[128,128]{1,0:T(8,128)S(1)} custom-call(f32[128,128]{1,0:T(8,128)S(1)} %fusion.97), custom_call_target="Cholesky" | custom-call | tf_op jit(solution)/shard_map/while/body/eval_jaxpr/jit(cholesky)/cholesky | solution.py:34
  419.9 31.4 %all_to_all.40 = bf16[16,256,256]{2,1,0:T(8,128)(2,1)S(1)} all-to-all(bf16[16,256,256]{2,1,0:T(8,128)(2,1)} %bitcast.110), channel_id=1, replica_groups=mesh['row'=8,'col'=16] {'col'}, dimensions={0} | all-to-all | bytes 4194304 | tf_op jit(solution)/shard_map/while/body/eval_jaxpr/all_to_all | solution.py:90
  452.6 16.0 %all_to_all.41 = f32[128,1,512]{2,1,0:T(1,128)S(1)} all-to-all(f32[128,1,512]{2,1,0:T(1,128)S(1)} %all_to_all.32), channel_id=1, replica_groups=mesh['row'=8,'col'=16] {'row','col'}, dimensions={0} | all-to-all | bytes 524288 | tf_op jit(solution)/shard_map/while/body/eval_jaxpr/all_to_all | solution.py:98
  468.9 15.2 %all_to_all.42 = f32[128,1,512]{2,1,0:T(1,128)S(1)} all-to-all(f32[128,1,512]{2,1,0:T(1,128)S(1)} %broadcast_in_dim.18), channel_id=1, replica_groups=mesh['row'=8,'col'=16] {'row','col'}, dimensions={0} | all-to-all | bytes 524288 | tf_op jit(solution)/shard_map/while/body/eval_jaxpr/all_to_all | solution.py:99
  485.2 11.7 %cholesky.172 = f32[128,128]{1,0:T(8,128)S(1)} custom-call(f32[128,128]{1,0:T(8,128)S(1)} %fusion.94), custom_call_target="Cholesky" | custom-call | tf_op jit(solution)/shard_map/while/body/eval_jaxpr/jit(cholesky)/cholesky | solution.py:34
  509.1 11.7 %cholesky.173 = f32[128,128]{1,0:T(8,128)S(1)} custom-call(f32[128,128]{1,0:T(8,128)S(1)} %fusion.97), custom_call_target="Cholesky" | custom-call | tf_op jit(solution)/shard_map/while/body/eval_jaxpr/jit(cholesky)/cholesky | solution.py:34
  522.1 9.8 %custom-call.16 = f32[1,128,128]{1,2,0:T(8,128)S(1)} custom-call(f32[1,128,128]{2,1,0:T(8,128)S(1)} %get-tuple-element.225), custom_call_target="InvertDiagBlocksLowerTriangular" | custom-call | tf_op jit(solution)/shard_map/while/body/eval_jaxpr/jit(_solve_triangular)/triangular_solve | solution.py:36
  (183 shorter events, 149.4 us)
Async XLA Ops:
  7.2 32.0 %copy-start.3 = (f32[256]{0:T(256)S(1)}, f32[256]{0:T(256)}, u32[]{:S(2)}) copy-start(f32[256]{0:T(256)} %param.11) | copy-start | bytes 3076
  7.2 17.0 %copy-start.5 = (s32[32,1,8]{0,2,1:T(8,128)S(1)}, s32[32,1,8]{0,2,1:T(8,128)}, u32[]{:S(2)}) copy-start(s32[32,1,8]{0,2,1:T(8,128)} %param.13) | copy-start | bytes 3076
  7.2 32.0 %copy-start.4 = (s32[32,1]{0,1:T(1,128)S(1)}, s32[32,1]{0,1:T(1,128)}, u32[]{:S(2)}) copy-start(s32[32,1]{0,1:T(1,128)} %param.14) | copy-start | bytes 388
  8.5 10.4 %all-to-all-start.4 = ((f32[8,1,256]{2,1,0:T(1,128)}), f32[8,1,256]{2,1,0:T(1,128)S(1)}, u32[]{:S(2)}, u32[]{:S(2)}) async-start(f32[8,1,256]{2,1,0:T(1,128)} %broadcast_in_dim.15), calls=%async_computation.4 | async-start | bytes 16384 | tf_op jit(solution)/shard_map/all_to_all | solution.py:84
  20.0 19.2 %all-to-all-start.3 = ((bf16[8,256,256]{2,1,0:T(8,128)(2,1)}), bf16[8,256,256]{2,1,0:T(8,128)(2,1)S(1)}, u32[]{:S(2)}, u32[]{:S(2)}) async-start(bf16[8,256,256]{2,1,0:T(8,128)(2,1)} %broadcast_in_dim.13), calls=%async_computation.3 | async-start | bytes 2097152 | tf_op jit(solution)/shard_map/all_to_all | solution.py:84
  24.2 14.9 %copy-start.2 = (s32[32,1,8]{2,0,1:T(8,128)}, s32[32,1,8]{2,0,1:T(8,128)S(1)}, u32[]{:S(2)}) copy-start(s32[32,1,8]{2,0,1:T(8,128)S(1)} %copy.32) | copy-start | bytes 3076
  39.2 124.7 %all-gather.2.cloned.1.call-start = ((), (), s32[]{:S(2)}) async-start(), calls=%async_computation.5 | async-start | bytes 2359296 | tf_op jit(solution)/shard_map/while/body/eval_jaxpr/all_gather | solution.py:122
  81.4 33.6 %copy-start = (f32[256,256]{1,0:T(8,128)}, f32[256,256]{1,0:T(8,128)S(1)}, u32[]{:S(2)}) copy-start(f32[256,256]{1,0:T(8,128)S(1)} %broadcast_multiply_fusion.3) | copy-start | bytes 786436 | tf_op jit(solution)/shard_map/while
  163.9 2.7 copy-start.1
  166.6 120.5 %all-gather.2.cloned.1.call-start = ((), (), s32[]{:S(2)}) async-start(), calls=%async_computation.5 | async-start | bytes 2359296 | tf_op jit(solution)/shard_map/while/body/eval_jaxpr/all_gather | solution.py:122
  205.2 33.1 %copy-start = (f32[256,256]{1,0:T(8,128)}, f32[256,256]{1,0:T(8,128)S(1)}, u32[]{:S(2)}) copy-start(f32[256,256]{1,0:T(8,128)S(1)} %broadcast_multiply_fusion.3) | copy-start | bytes 786436 | tf_op jit(solution)/shard_map/while
  287.1 2.7 copy-start.1
  289.9 120.5 %all-gather.2.cloned.1.call-start = ((), (), s32[]{:S(2)}) async-start(), calls=%async_computation.5 | async-start | bytes 2359296 | tf_op jit(solution)/shard_map/while/body/eval_jaxpr/all_gather | solution.py:122
  328.4 33.1 %copy-start = (f32[256,256]{1,0:T(8,128)}, f32[256,256]{1,0:T(8,128)S(1)}, u32[]{:S(2)}) copy-start(f32[256,256]{1,0:T(8,128)S(1)} %broadcast_multiply_fusion.3) | copy-start | bytes 786436 | tf_op jit(solution)/shard_map/while
  410.4 2.7 copy-start.1
  413.1 120.5 %all-gather.2.cloned.1.call-start = ((), (), s32[]{:S(2)}) async-start(), calls=%async_computation.5 | async-start | bytes 2359296 | tf_op jit(solution)/shard_map/while/body/eval_jaxpr/all_gather | solution.py:122
  451.7 33.1 %copy-start = (f32[256,256]{1,0:T(8,128)}, f32[256,256]{1,0:T(8,128)S(1)}, u32[]{:S(2)}) copy-start(f32[256,256]{1,0:T(8,128)S(1)} %broadcast_multiply_fusion.3) | copy-start | bytes 786436 | tf_op jit(solution)/shard_map/while
  533.6 2.7 copy-start.1
Sparse Core Ops, SparseCore 0:
  115.2 21.4 all-gather.1
  238.5 21.4 all-gather.1
  361.7 21.4 all-gather.1
  485.0 21.4 all-gather.1

commit v9 on v8

--- a/solution.py
+++ b/solution.py
@@ -9,6 +9,7 @@
 
 
 ITERS = 4
+SC_ROWS = 64
 
 
 def gram_of(image, nodes):
@@ -105,17 +106,21 @@
     index = tile_index[:, 0]
     counts = tile_count[:, 0]
     rows_dev, width = basis.shape
-    tile = tiles.shape[-1]
     nodes = rows_dev * lax.axis_size("row") * lax.axis_size("col")
     scale = degree_scale[:, None]
     probe = (basis.astype(jnp.float32) * scale).astype(jnp.bfloat16)
-    number = lax.axis_size("col") * rows_dev // tile
-    scale_block = gather_rows(degree_scale, "row")[:, None]
+    n_col = lax.axis_size("col")
+    scale_block = lax.all_gather(degree_scale, "row", axis=0, tiled=True)[:, None]
 
     def loop_step(i, carry):
         block_probe = carry[0]
         result = apply_tiles(tiles, block_probe, index, counts)
-        summed = sum_scatter_rows(result.reshape(number * tile, width), "col")
+        parts = result.reshape(n_col, -1, width)
+        head = lax.psum_scatter(
+            parts[:, :SC_ROWS].reshape(-1, width), "col", scatter_dimension=0, tiled=True
+        ).astype(jnp.float32)
+        rest = sum_scatter_rows(parts[:, SC_ROWS:].reshape(-1, width), "col")
+        summed = jnp.concatenate([head, rest], axis=0)
         image = summed * scale
         gram = sum_all(gram_of(image, nodes), ("row", "col"))
         image_late, gram = lax.optimization_barrier((image, gram))

time: 548 us -> 774 us (1.41)
  waiting for transfers between devices: 18.5 us -> 302 us
  blocking collectives: 255 us -> 162 us
  local copies, waits for them, and re-layouts: 8.1 us -> 25.2 us
  starting transfers between devices: 10.1 us -> 25 us
    reduce_scatter x0 -> x4, waiting for transfers between devices: none -> 302 us  [loop_step(): lax.psum_scatter(parts[:, :SC_ROWS].reshape(-1, width), 'col', scatter_di...]
    all_to_all x4 -> x0, blocking collectives: 129 us -> none  [sum_scatter_rows(): lax.all_to_all(x.reshape((n, -1) + x.shape[1:]), axis, 0, 0, tiled=False)]
    all_to_all x0 -> x4, starting transfers between devices: none -> 18.9 us  [sum_scatter_rows(): lax.all_to_all(x.reshape((n, -1) + x.shape[1:]), axis, 0, 0, tiled=False)]
    all_gather x0 -> x1, blocking collectives: none -> 18.5 us  [body(): lax.all_gather(degree_scale, 'row', axis=0, tiled=True)[:, None]]
    all_to_all x2 -> x1, waiting for transfers between devices: 18.4 us -> 0.01 us  [gather_rows(): lax.all_to_all(jnp.broadcast_to(x, (n,) + x.shape), axis, 0, 0, tiled=False)]
    slice x0 -> x8, local copies, waits for them, and re-layouts: none -> 18.4 us  [the longest x4 10.8 us: loop_step(): rest = sum_scatter_rows(parts[:, SC_ROWS:].reshape(-1, width), 'col')]
    all_to_all x4, blocking collectives: 64.6 us -> 82.4 us  [sum_all(): lax.all_to_all(x.reshape(n, -1), axes, 0, 0, tiled=False)]
  transfers between devices with their start and end apart: 6 -> 13, of which waited for: 2 -> 4; matrix products, arithmetic and copies ran while one was open for 36% -> 27% of each run, Pallas kernels for 0% -> 0%
where the time goes in v9:
time: 774 us; the launch traced here: 773 us
  waiting for transfers between devices  302 us (39%)
  other arithmetic  195 us (25%)
  blocking collectives  162 us (21%)
  Pallas kernels  27 us (3%)
  local copies, waits for them, and re-layouts  25.2 us (3%)
  starting transfers between devices  25 us (3%)
  matrix products  21.9 us (3%)
  between operations  14.1 us (2%)
    reduce_scatter x4, waiting for transfers between devices, loop_step(): lax.psum_scatter(parts[:, :SC_ROWS].reshape(-1, width), 'col', scatter_di...  302 us
    another operation x24, other arithmetic, cholesky_and_inverse(): lower = jnp.linalg.cholesky(g)  99.1 us
    another operation x16, other arithmetic, cholesky_and_inverse(): return (lower, jax.scipy.linalg.solve_triangular(lower, eye, lower=True))  83.7 us
    all_to_all x4, blocking collectives, sum_all(): lax.all_to_all(x.reshape(n, -1), axes, 0, 0, tiled=False)  82.4 us
    all_to_all x4, blocking collectives, sum_all(): lax.all_to_all(jnp.broadcast_to(piece, (n,) + piece.shape), axes, 0, 0, t...  60.9 us
    pallas_call x4, Pallas kernels, apply_tiles(): pl.pallas_call(kernel, grid_spec=spec, out_shape=jax.ShapeDtypeStruct((tr...  27 us
    all_to_all x4, starting transfers between devices, sum_scatter_rows(): lax.all_to_all(x.reshape((n, -1) + x.shape[1:]), axis, 0, 0, tiled=False)  18.9 us
    all_gather x1, blocking collectives, body(): lax.all_gather(degree_scale, 'row', axis=0, tiled=True)[:, None]  18.5 us
  transfers between devices with their start and end apart: 13, of which 4 were waited for; matrix products, arithmetic and copies ran while one was open for 27% of the time, Pallas kernels for 0%

profile of v9, /device:TPU:1, one launch (start us, length us, event | category | flops | bytes accessed | tf_op | source)
XLA Modules:
  0.0 772.7 jit_solution(1887988343401558545)
XLA Ops:
  15.2 18.5 %all-gather = f32[8,1,256]{2,1,0:T(1,128)S(1)} all-gather(f32[1,1,256]{2,1,0:T(1,128)S(1)} %bitcast.122), channel_id=1, replica_groups=mesh['row'=8,'col'=16] {'row'}, dimensions={0}, use_global_device_ids=true | all-gather | bytes 9216 | tf_op jit(solution)/shard_map/all_gather | solution.py:113
  33.8 728.1 %while.17 = (s32[]{:T(128)}, bf16[2048,256]{1,0:T(8,128)(2,1)S(1)}, f32[256,256]{1,0:T(8,128)}, f32[256,256]{1,0:T(8,128)}, f32[256,256]{1,0:T(8,128)}, /*index=...) while((s32[]{:T(128)}, bf16[2048,256]{1,0:T(8,128)(2,1)S(1)}, ...), condition=%wide.wide.region_6.9_spmd, body=%wide.wide.region_0.8_spmd.sunk | while | flops 1161461504 | bytes 34159924 | solution.py:136
  53.1 75.6 %reduce-scatter.2.cloned.1.call-done = bf16[64,256]{1,0:T(8,128)(2,1)} async-done(((bf16[1024,256]{1,0:T(8,128)(2,1)}), bf16[64,256]{1,0:T(8,128)(2,1)}) %reduce-scatter.2.cloned.1.call-update) | async-done | bytes 32784 | tf_op jit(solution)/shard_map/while/body/eval_jaxpr/reduce_scatter | solution.py:119
  130.7 20.5 %all_to_all.34 = f32[128,1,512]{2,1,0:T(1,128)S(1)} all-to-all(f32[128,1,512]{2,1,0:T(1,128)S(1)} %all_to_all.27), channel_id=1, replica_groups=mesh['row'=8,'col'=16] {'row','col'}, dimensions={0} | all-to-all | bytes 524288 | tf_op jit(solution)/shard_map/while/body/eval_jaxpr/all_to_all | solution.py:99
  151.5 15.2 %all_to_all.35 = f32[128,1,512]{2,1,0:T(1,128)S(1)} all-to-all(f32[128,1,512]{2,1,0:T(1,128)S(1)} %broadcast_in_dim.18), channel_id=1, replica_groups=mesh['row'=8,'col'=16] {'row','col'}, dimensions={0} | all-to-all | bytes 524288 | tf_op jit(solution)/shard_map/while/body/eval_jaxpr/all_to_all | solution.py:100
  167.8 11.7 %cholesky.172 = f32[128,128]{1,0:T(8,128)S(1)} custom-call(f32[128,128]{1,0:T(8,128)S(1)} %fusion.94), custom_call_target="Cholesky" | custom-call | tf_op jit(solution)/shard_map/while/body/eval_jaxpr/jit(cholesky)/cholesky | solution.py:35
  180.8 9.8 %custom-call.15 = f32[1,128,128]{1,2,0:T(8,128)S(1)} custom-call(f32[1,128,128]{2,1,0:T(8,128)S(1)} %get-tuple-element.223), custom_call_target="InvertDiagBlocksLowerTriangular" | custom-call | tf_op jit(solution)/shard_map/while/body/eval_jaxpr/jit(_solve_triangular)/triangular_solve | solution.py:37
  191.6 11.7 %cholesky.173 = f32[128,128]{1,0:T(8,128)S(1)} custom-call(f32[128,128]{1,0:T(8,128)S(1)} %fusion.97), custom_call_target="Cholesky" | custom-call | tf_op jit(solution)/shard_map/while/body/eval_jaxpr/jit(cholesky)/cholesky | solution.py:35
  204.7 9.8 %custom-call.16 = f32[1,128,128]{1,2,0:T(8,128)S(1)} custom-call(f32[1,128,128]{2,1,0:T(8,128)S(1)} %get-tuple-element.225), custom_call_target="InvertDiagBlocksLowerTriangular" | custom-call | tf_op jit(solution)/shard_map/while/body/eval_jaxpr/jit(_solve_triangular)/triangular_solve | solution.py:37
  234.2 75.3 %reduce-scatter.2.cloned.1.call-done = bf16[64,256]{1,0:T(8,128)(2,1)} async-done(((bf16[1024,256]{1,0:T(8,128)(2,1)}), bf16[64,256]{1,0:T(8,128)(2,1)}) %reduce-scatter.2.cloned.1.call-update) | async-done | bytes 32784 | tf_op jit(solution)/shard_map/while/body/eval_jaxpr/reduce_scatter | solution.py:119
  311.4 20.7 %all_to_all.34 = f32[128,1,512]{2,1,0:T(1,128)S(1)} all-to-all(f32[128,1,512]{2,1,0:T(1,128)S(1)} %all_to_all.27), channel_id=1, replica_groups=mesh['row'=8,'col'=16] {'row','col'}, dimensions={0} | all-to-all | bytes 524288 | tf_op jit(solution)/shard_map/while/body/eval_jaxpr/all_to_all | solution.py:99
  332.5 15.2 %all_to_all.35 = f32[128,1,512]{2,1,0:T(1,128)S(1)} all-to-all(f32[128,1,512]{2,1,0:T(1,128)S(1)} %broadcast_in_dim.18), channel_id=1, replica_groups=mesh['row'=8,'col'=16] {'row','col'}, dimensions={0} | all-to-all | bytes 524288 | tf_op jit(solution)/shard_map/while/body/eval_jaxpr/all_to_all | solution.py:100
  348.7 11.7 %cholesky.172 = f32[128,128]{1,0:T(8,128)S(1)} custom-call(f32[128,128]{1,0:T(8,128)S(1)} %fusion.94), custom_call_target="Cholesky" | custom-call | tf_op jit(solution)/shard_map/while/body/eval_jaxpr/jit(cholesky)/cholesky | solution.py:35
  372.6 11.7 %cholesky.173 = f32[128,128]{1,0:T(8,128)S(1)} custom-call(f32[128,128]{1,0:T(8,128)S(1)} %fusion.97), custom_call_target="Cholesky" | custom-call | tf_op jit(solution)/shard_map/while/body/eval_jaxpr/jit(cholesky)/cholesky | solution.py:35
  415.1 75.5 %reduce-scatter.2.cloned.1.call-done = bf16[64,256]{1,0:T(8,128)(2,1)} async-done(((bf16[1024,256]{1,0:T(8,128)(2,1)}), bf16[64,256]{1,0:T(8,128)(2,1)}) %reduce-scatter.2.cloned.1.call-update) | async-done | bytes 32784 | tf_op jit(solution)/shard_map/while/body/eval_jaxpr/reduce_scatter | solution.py:119
  492.6 20.5 %all_to_all.34 = f32[128,1,512]{2,1,0:T(1,128)S(1)} all-to-all(f32[128,1,512]{2,1,0:T(1,128)S(1)} %all_to_all.27), channel_id=1, replica_groups=mesh['row'=8,'col'=16] {'row','col'}, dimensions={0} | all-to-all | bytes 524288 | tf_op jit(solution)/shard_map/while/body/eval_jaxpr/all_to_all | solution.py:99
  513.5 15.2 %all_to_all.35 = f32[128,1,512]{2,1,0:T(1,128)S(1)} all-to-all(f32[128,1,512]{2,1,0:T(1,128)S(1)} %broadcast_in_dim.18), channel_id=1, replica_groups=mesh['row'=8,'col'=16] {'row','col'}, dimensions={0} | all-to-all | bytes 524288 | tf_op jit(solution)/shard_map/while/body/eval_jaxpr/all_to_all | solution.py:100
  529.7 11.7 %cholesky.172 = f32[128,128]{1,0:T(8,128)S(1)} custom-call(f32[128,128]{1,0:T(8,128)S(1)} %fusion.94), custom_call_target="Cholesky" | custom-call | tf_op jit(solution)/shard_map/while/body/eval_jaxpr/jit(cholesky)/cholesky | solution.py:35
  553.6 11.7 %cholesky.173 = f32[128,128]{1,0:T(8,128)S(1)} custom-call(f32[128,128]{1,0:T(8,128)S(1)} %fusion.97), custom_call_target="Cholesky" | custom-call | tf_op jit(solution)/shard_map/while/body/eval_jaxpr/jit(cholesky)/cholesky | solution.py:35
  596.1 75.3 %reduce-scatter.2.cloned.1.call-done = bf16[64,256]{1,0:T(8,128)(2,1)} async-done(((bf16[1024,256]{1,0:T(8,128)(2,1)}), bf16[64,256]{1,0:T(8,128)(2,1)}) %reduce-scatter.2.cloned.1.call-update) | async-done | bytes 32784 | tf_op jit(solution)/shard_map/while/body/eval_jaxpr/reduce_scatter | solution.py:119
  673.4 20.7 %all_to_all.34 = f32[128,1,512]{2,1,0:T(1,128)S(1)} all-to-all(f32[128,1,512]{2,1,0:T(1,128)S(1)} %all_to_all.27), channel_id=1, replica_groups=mesh['row'=8,'col'=16] {'row','col'}, dimensions={0} | all-to-all | bytes 524288 | tf_op jit(solution)/shard_map/while/body/eval_jaxpr/all_to_all | solution.py:99
  694.5 15.2 %all_to_all.35 = f32[128,1,512]{2,1,0:T(1,128)S(1)} all-to-all(f32[128,1,512]{2,1,0:T(1,128)S(1)} %broadcast_in_dim.18), channel_id=1, replica_groups=mesh['row'=8,'col'=16] {'row','col'}, dimensions={0} | all-to-all | bytes 524288 | tf_op jit(solution)/shard_map/while/body/eval_jaxpr/all_to_all | solution.py:100
  710.7 11.7 %cholesky.172 = f32[128,128]{1,0:T(8,128)S(1)} custom-call(f32[128,128]{1,0:T(8,128)S(1)} %fusion.94), custom_call_target="Cholesky" | custom-call | tf_op jit(solution)/shard_map/while/body/eval_jaxpr/jit(cholesky)/cholesky | solution.py:35
  734.6 11.7 %cholesky.173 = f32[128,128]{1,0:T(8,128)S(1)} custom-call(f32[128,128]{1,0:T(8,128)S(1)} %fusion.97), custom_call_target="Cholesky" | custom-call | tf_op jit(solution)/shard_map/while/body/eval_jaxpr/jit(cholesky)/cholesky | solution.py:35
  (209 shorter events, 180.6 us)
Async XLA Ops:
  7.2 8.1 %copy-start.3 = (f32[256]{0:T(256)S(1)}, f32[256]{0:T(256)}, u32[]{:S(2)}) copy-start(f32[256]{0:T(256)} %param.11) | copy-start | bytes 3076
  7.2 7.9 %copy-start.5 = (s32[32,1,8]{0,2,1:T(8,128)S(1)}, s32[32,1,8]{0,2,1:T(8,128)}, u32[]{:S(2)}) copy-start(s32[32,1,8]{0,2,1:T(8,128)} %param.13) | copy-start | bytes 3076
  7.2 26.6 %copy-start.4 = (s32[32,1]{0,1:T(1,128)S(1)}, s32[32,1]{0,1:T(1,128)}, u32[]{:S(2)}) copy-start(s32[32,1]{0,1:T(1,128)} %param.14) | copy-start | bytes 388
  9.3 24.5 %all-to-all-start.3 = ((bf16[8,256,256]{2,1,0:T(8,128)(2,1)}), bf16[8,256,256]{2,1,0:T(8,128)(2,1)S(1)}, u32[]{:S(2)}, u32[]{:S(2)}) async-start(bf16[8,256,256]{2,1,0:T(8,128)(2,1)} %broadcast_in_dim.13), calls=%async_computation.4 | async-start | bytes 2097152 | tf_op jit(solution)/shard_map/all_to_all | solution.py:85
  15.1 18.6 %copy-start.2 = (s32[32,1,8]{2,0,1:T(8,128)}, s32[32,1,8]{2,0,1:T(8,128)S(1)}, u32[]{:S(2)}) copy-start(s32[32,1,8]{2,0,1:T(8,128)S(1)} %copy.32) | copy-start | bytes 3076
  43.3 86.2 %all-to-all-start = ((bf16[16,192,256]{2,1,0:T(8,128)(2,1)}), bf16[16,192,256]{2,1,0:T(8,128)(2,1)S(1)}, u32[]{:S(2)}, u32[]{:S(2)}) async-start(bf16[16,192,256]{2,1,0:T(8,128)(2,1)} %slice.47), calls=%async_computation | async-start | bytes 3145728 | tf_op jit(solution)/shard_map/while/body/eval_jaxpr/all_to_all | solution.py:91
  51.0 77.7 %reduce-scatter.2.cloned.1.call-start = ((), (), s32[]{:S(2)}) async-start(), calls=%async_computation.5 | async-start | bytes 557056 | tf_op jit(solution)/shard_map/while/body/eval_jaxpr/reduce_scatter | solution.py:119
  53.0 163.2 %all-gather.3.cloned.1.call-start = ((), (), s32[]{:S(2)}) async-start(), calls=%async_computation.6 | async-start | bytes 2359296 | tf_op jit(solution)/shard_map/while/body/eval_jaxpr/all_gather | solution.py:127
  129.8 37.6 %copy-start = (f32[256,256]{1,0:T(8,128)}, f32[256,256]{1,0:T(8,128)S(1)}, u32[]{:S(2)}) copy-start(f32[256,256]{1,0:T(8,128)S(1)} %maximum_multiply_fusion.3) | copy-start | bytes 786436 | tf_op jit(solution)/shard_map/while
  216.2 2.7 copy-start.1
  228.4 81.8 %all-to-all-start = ((bf16[16,192,256]{2,1,0:T(8,128)(2,1)}), bf16[16,192,256]{2,1,0:T(8,128)(2,1)S(1)}, u32[]{:S(2)}, u32[]{:S(2)}) async-start(bf16[16,192,256]{2,1,0:T(8,128)(2,1)} %slice.47), calls=%async_computation | async-start | bytes 3145728 | tf_op jit(solution)/shard_map/while/body/eval_jaxpr/all_to_all | solution.py:91
  232.1 77.3 %reduce-scatter.2.cloned.1.call-start = ((), (), s32[]{:S(2)}) async-start(), calls=%async_computation.5 | async-start | bytes 557056 | tf_op jit(solution)/shard_map/while/body/eval_jaxpr/reduce_scatter | solution.py:119
  234.1 163.1 %all-gather.3.cloned.1.call-start = ((), (), s32[]{:S(2)}) async-start(), calls=%async_computation.6 | async-start | bytes 2359296 | tf_op jit(solution)/shard_map/while/body/eval_jaxpr/all_gather | solution.py:127
  310.5 37.8 %copy-start = (f32[256,256]{1,0:T(8,128)}, f32[256,256]{1,0:T(8,128)S(1)}, u32[]{:S(2)}) copy-start(f32[256,256]{1,0:T(8,128)S(1)} %maximum_multiply_fusion.3) | copy-start | bytes 786436 | tf_op jit(solution)/shard_map/while
  397.2 2.7 copy-start.1
  409.4 82.0 %all-to-all-start = ((bf16[16,192,256]{2,1,0:T(8,128)(2,1)}), bf16[16,192,256]{2,1,0:T(8,128)(2,1)S(1)}, u32[]{:S(2)}, u32[]{:S(2)}) async-start(bf16[16,192,256]{2,1,0:T(8,128)(2,1)} %slice.47), calls=%async_computation | async-start | bytes 3145728 | tf_op jit(solution)/shard_map/while/body/eval_jaxpr/all_to_all | solution.py:91
  413.1 77.6 %reduce-scatter.2.cloned.1.call-start = ((), (), s32[]{:S(2)}) async-start(), calls=%async_computation.5 | async-start | bytes 557056 | tf_op jit(solution)/shard_map/while/body/eval_jaxpr/reduce_scatter | solution.py:119
  415.1 163.1 %all-gather.3.cloned.1.call-start = ((), (), s32[]{:S(2)}) async-start(), calls=%async_computation.6 | async-start | bytes 2359296 | tf_op jit(solution)/shard_map/while/body/eval_jaxpr/all_gather | solution.py:127
  491.7 37.6 %copy-start = (f32[256,256]{1,0:T(8,128)}, f32[256,256]{1,0:T(8,128)S(1)}, u32[]{:S(2)}) copy-start(f32[256,256]{1,0:T(8,128)S(1)} %maximum_multiply_fusion.3) | copy-start | bytes 786436 | tf_op jit(solution)/shard_map/while
  578.1 2.7 copy-start.1
  590.3 81.8 %all-to-all-start = ((bf16[16,192,256]{2,1,0:T(8,128)(2,1)}), bf16[16,192,256]{2,1,0:T(8,128)(2,1)S(1)}, u32[]{:S(2)}, u32[]{:S(2)}) async-start(bf16[16,192,256]{2,1,0:T(8,128)(2,1)} %slice.47), calls=%async_computation | async-start | bytes 3145728 | tf_op jit(solution)/shard_map/while/body/eval_jaxpr/all_to_all | solution.py:91
  594.1 77.4 %reduce-scatter.2.cloned.1.call-start = ((), (), s32[]{:S(2)}) async-start(), calls=%async_computation.5 | async-start | bytes 557056 | tf_op jit(solution)/shard_map/while/body/eval_jaxpr/reduce_scatter | solution.py:119
  596.0 163.1 %all-gather.3.cloned.1.call-start = ((), (), s32[]{:S(2)}) async-start(), calls=%async_computation.6 | async-start | bytes 2359296 | tf_op jit(solution)/shard_map/while/body/eval_jaxpr/all_gather | solution.py:127
  672.5 37.8 %copy-start = (f32[256,256]{1,0:T(8,128)}, f32[256,256]{1,0:T(8,128)S(1)}, u32[]{:S(2)}) copy-start(f32[256,256]{1,0:T(8,128)S(1)} %maximum_multiply_fusion.3) | copy-start | bytes 786436 | tf_op jit(solution)/shard_map/while
  (1 other events, 2.7 us)
Sparse Core Ops, SparseCore 0:
  55.0 73.6 reduce-scatter.1
  167.6 21.4 all-gather.2
  236.1 73.2 reduce-scatter.1
  348.5 21.4 all-gather.2
  416.8 73.8 reduce-scatter.1
  529.5 21.4 all-gather.2
  598.1 73.3 reduce-scatter.1
  710.5 21.4 all-gather.2

commit v10 on v8

--- a/solution.py
+++ b/solution.py
@@ -54,19 +54,22 @@
             start = pl.multiple_of(index_ref[t * slots + s] * tile, tile)
             rows = basis_ref[pl.ds(start, tile), :]
             gat_ref[s * tile:(s + 1) * tile, :] = jnp.where(s < live, rows, jnp.zeros_like(rows))
-        lhs = jnp.concatenate([tiles_ref[r, s] for s in range(slots)], axis=1)
+        lhs = jnp.concatenate([tiles_ref[r, 0, s] for s in range(slots)], axis=1)
         out_ref[r] = jnp.dot(lhs, gat_ref[...], preferred_element_type=jnp.float32).astype(out_ref.dtype)
 
 
-def apply_tiles(tiles, basis, index, counts, rows_per_block=16):
+def apply_tiles(tiles, basis, index, counts, half, rows_per_block=8):
     trows, slots, tile, _ = tiles.shape
     width = basis.shape[-1]
+    pairs = tiles.reshape(trows // 2, 2, slots, tile, tile)
+    index = index.reshape(trows // 2, 2, slots)[:, half].reshape(-1)
+    counts = counts.reshape(trows // 2, 2)[:, half]
     kernel = functools.partial(_apply_kernel, rows_per_block=rows_per_block, slots=slots, tile=tile)
     spec = pltpu.PrefetchScalarGridSpec(
         num_scalar_prefetch=2,
-        grid=(trows // rows_per_block,),
+        grid=(trows // 2 // rows_per_block,),
         in_specs=[
-            pl.BlockSpec((rows_per_block, slots, tile, tile), lambda i, idx, cnt: (i, 0, 0, 0)),
+            pl.BlockSpec((rows_per_block, 1, slots, tile, tile), lambda i, idx, cnt: (i, half, 0, 0, 0)),
             pl.BlockSpec(basis.shape, lambda i, idx, cnt: (0, 0)),
         ],
         out_specs=pl.BlockSpec((rows_per_block, tile, width), lambda i, idx, cnt: (i, 0, 0)),
@@ -75,8 +78,8 @@
     return pl.pallas_call(
         kernel,
         grid_spec=spec,
-        out_shape=jax.ShapeDtypeStruct((trows, tile, width), jnp.bfloat16),
-    )(index.reshape(-1), counts, tiles, basis)
+        out_shape=jax.ShapeDtypeStruct((trows // 2, tile, width), jnp.bfloat16),
+    )(index, counts, pairs, basis)
 
 
 def gather_rows(x, axis):
@@ -105,17 +108,16 @@
     index = tile_index[:, 0]
     counts = tile_count[:, 0]
     rows_dev, width = basis.shape
-    tile = tiles.shape[-1]
     nodes = rows_dev * lax.axis_size("row") * lax.axis_size("col")
     scale = degree_scale[:, None]
     probe = (basis.astype(jnp.float32) * scale).astype(jnp.bfloat16)
-    number = lax.axis_size("col") * rows_dev // tile
-    scale_block = gather_rows(degree_scale, "row")[:, None]
+    scale_block = lax.all_gather(degree_scale, "row", axis=0, tiled=True)[:, None]
 
     def loop_step(i, carry):
         block_probe = carry[0]
-        result = apply_tiles(tiles, block_probe, index, counts)
-        summed = sum_scatter_rows(result.reshape(number * tile, width), "col")
+        first = sum_scatter_rows(apply_tiles(tiles, block_probe, index, counts, 0).reshape(-1, width), "col")
+        second = sum_scatter_rows(apply_tiles(tiles, block_probe, index, counts, 1).reshape(-1, width), "col")
+        summed = jnp.concatenate([first, second], axis=0)
         image = summed * scale
         gram = sum_all(gram_of(image, nodes), ("row", "col"))
         image_late, gram = lax.optimization_barrier((image, gram))

time: 548 us -> 585 us (1.068)
  blocking collectives: 255 us -> 148 us
  waiting for transfers between devices: 18.5 us -> 108 us
  starting transfers between devices: 10.1 us -> 42.4 us
  Pallas kernels: 27.1 us -> 37.7 us
  local copies, waits for them, and re-layouts: 8.1 us -> 17.2 us
    all_to_all x4 -> x0, blocking collectives: 129 us -> none  [sum_scatter_rows(): lax.all_to_all(x.reshape((n, -1) + x.shape[1:]), axis, 0, 0, tiled=False)]
    all_to_all x0 -> x8, waiting for transfers between devices: none -> 108 us  [sum_scatter_rows(): lax.all_to_all(x.reshape((n, -1) + x.shape[1:]), axis, 0, 0, tiled=False)]
    all_to_all x0 -> x8, starting transfers between devices: none -> 36.5 us  [sum_scatter_rows(): lax.all_to_all(x.reshape((n, -1) + x.shape[1:]), axis, 0, 0, tiled=False)]
    all_gather x0 -> x1, blocking collectives: none -> 18.6 us  [body(): lax.all_gather(degree_scale, 'row', axis=0, tiled=True)[:, None]]
    all_to_all x2 -> x1, waiting for transfers between devices: 18.4 us -> 0.01 us  [gather_rows(): lax.all_to_all(jnp.broadcast_to(x, (n,) + x.shape), axis, 0, 0, tiled=False)]
    pallas_call x4 -> x8, Pallas kernels: 27.1 us -> 37.7 us  [apply_tiles(): pl.pallas_call(kernel, grid_spec=spec, out_shape=jax.ShapeDtypeStruct((tr...]
  transfers between devices with their start and end apart: 6 -> 13, of which waited for: 2 -> 8; matrix products, arithmetic and copies ran while one was open for 36% -> 34% of each run, Pallas kernels for 0% -> 3%
where the time goes in v10:
time: 585 us; the launch traced here: 584 us
  other arithmetic  194 us (33%)
  blocking collectives  148 us (25%)
  waiting for transfers between devices  108 us (18%)
  starting transfers between devices  42.4 us (7%)
  Pallas kernels  37.7 us (6%)
  matrix products  21.9 us (4%)
  local copies, waits for them, and re-layouts  17.2 us (3%)
  between operations  13.7 us (2%)
    all_to_all x8, waiting for transfers between devices, sum_scatter_rows(): lax.all_to_all(x.reshape((n, -1) + x.shape[1:]), axis, 0, 0, tiled=False)  108 us
    another operation x24, other arithmetic, cholesky_and_inverse(): lower = jnp.linalg.cholesky(g)  99.1 us
    another operation x16, other arithmetic, cholesky_and_inverse(): return (lower, jax.scipy.linalg.solve_triangular(lower, eye, lower=True))  83.7 us
    all_to_all x4, blocking collectives, sum_all(): lax.all_to_all(x.reshape(n, -1), axes, 0, 0, tiled=False)  68.2 us
    all_to_all x4, blocking collectives, sum_all(): lax.all_to_all(jnp.broadcast_to(piece, (n,) + piece.shape), axes, 0, 0, t...  60.9 us
    pallas_call x8, Pallas kernels, apply_tiles(): pl.pallas_call(kernel, grid_spec=spec, out_shape=jax.ShapeDtypeStruct((tr...  37.7 us
    all_to_all x8, starting transfers between devices, sum_scatter_rows(): lax.all_to_all(x.reshape((n, -1) + x.shape[1:]), axis, 0, 0, tiled=False)  36.5 us
    all_gather x1, blocking collectives, body(): lax.all_gather(degree_scale, 'row', axis=0, tiled=True)[:, None]  18.6 us
  transfers between devices with their start and end apart: 13, of which 8 were waited for; matrix products, arithmetic and copies ran while one was open for 34% of the time, Pallas kernels for 3%

profile of v10, /device:TPU:1, one launch (start us, length us, event | category | flops | bytes accessed | tf_op | source)
XLA Modules:
  0.0 584.1 jit_solution(9562163470705619736)
XLA Ops:
  15.1 18.6 %all-gather = f32[8,1,256]{2,1,0:T(1,128)S(1)} all-gather(f32[1,1,256]{2,1,0:T(1,128)S(1)} %bitcast.98), channel_id=1, replica_groups=mesh['row'=8,'col'=16] {'row'}, dimensions={0}, use_global_device_ids=true | all-gather | bytes 9216 | tf_op jit(solution)/shard_map/all_gather | solution.py:114
  33.8 539.8 %while.16 = (s32[]{:T(128)}, bf16[2048,256]{1,0:T(8,128)(2,1)S(1)}, f32[256,256]{1,0:T(8,128)}, f32[256,256]{1,0:T(8,128)}, f32[256,256]{1,0:T(8,128)}, /*index=...) while((s32[]{:T(128)}, bf16[2048,256]{1,0:T(8,128)(2,1)S(1)}, ...), condition=%wide.region_6.9_spmd, body=%wide.region_0.8_spmd.sunk | while | flops 1161953024 | bytes 30363704 | solution.py:133
  54.3 11.3 %all-to-all-done.1 = bf16[16,128,256]{2,1,0:T(8,128)(2,1)S(1)} async-done(((bf16[16,128,256]{2,1,0:T(8,128)(2,1)}), bf16[16,128,256]{2,1,0:T(8,128)(2,1)S(1)}, u32[]{:S(2)}, u32[]{:S(2)}) %all-to-all-start.1) | async-done | bytes 1048608 | tf_op jit(solution)/shard_map/while/body/eval_jaxpr/all_to_all | solution.py:93
  70.3 15.7 %all-to-all-done = bf16[16,128,256]{2,1,0:T(8,128)(2,1)S(1)} async-done(((bf16[16,128,256]{2,1,0:T(8,128)(2,1)}), bf16[16,128,256]{2,1,0:T(8,128)(2,1)S(1)}, u32[]{:S(2)}, u32[]{:S(2)}) %all-to-all-start) | async-done | bytes 1048608 | tf_op jit(solution)/shard_map/while/body/eval_jaxpr/all_to_all | solution.py:93
  87.1 17.1 %all_to_all.36 = f32[128,1,512]{2,1,0:T(1,128)S(1)} all-to-all(f32[128,1,512]{2,1,0:T(1,128)S(1)} %all_to_all.28), channel_id=1, replica_groups=mesh['row'=8,'col'=16] {'row','col'}, dimensions={0} | all-to-all | bytes 524288 | tf_op jit(solution)/shard_map/while/body/eval_jaxpr/all_to_all | solution.py:101
  104.5 15.2 %all_to_all.37 = f32[128,1,512]{2,1,0:T(1,128)S(1)} all-to-all(f32[128,1,512]{2,1,0:T(1,128)S(1)} %broadcast_in_dim.17), channel_id=1, replica_groups=mesh['row'=8,'col'=16] {'row','col'}, dimensions={0} | all-to-all | bytes 524288 | tf_op jit(solution)/shard_map/while/body/eval_jaxpr/all_to_all | solution.py:102
  120.7 11.7 %cholesky.152 = f32[128,128]{1,0:T(8,128)S(1)} custom-call(f32[128,128]{1,0:T(8,128)S(1)} %fusion.70), custom_call_target="Cholesky" | custom-call | tf_op jit(solution)/shard_map/while/body/eval_jaxpr/jit(cholesky)/cholesky | solution.py:34
  144.6 11.7 %cholesky.153 = f32[128,128]{1,0:T(8,128)S(1)} custom-call(f32[128,128]{1,0:T(8,128)S(1)} %fusion.73), custom_call_target="Cholesky" | custom-call | tf_op jit(solution)/shard_map/while/body/eval_jaxpr/jit(cholesky)/cholesky | solution.py:34
  204.1 15.7 %all-to-all-done = bf16[16,128,256]{2,1,0:T(8,128)(2,1)S(1)} async-done(((bf16[16,128,256]{2,1,0:T(8,128)(2,1)}), bf16[16,128,256]{2,1,0:T(8,128)(2,1)S(1)}, u32[]{:S(2)}, u32[]{:S(2)}) %all-to-all-start) | async-done | bytes 1048608 | tf_op jit(solution)/shard_map/while/body/eval_jaxpr/all_to_all | solution.py:93
  221.0 17.0 %all_to_all.36 = f32[128,1,512]{2,1,0:T(1,128)S(1)} all-to-all(f32[128,1,512]{2,1,0:T(1,128)S(1)} %all_to_all.28), channel_id=1, replica_groups=mesh['row'=8,'col'=16] {'row','col'}, dimensions={0} | all-to-all | bytes 524288 | tf_op jit(solution)/shard_map/while/body/eval_jaxpr/all_to_all | solution.py:101
  238.4 15.2 %all_to_all.37 = f32[128,1,512]{2,1,0:T(1,128)S(1)} all-to-all(f32[128,1,512]{2,1,0:T(1,128)S(1)} %broadcast_in_dim.17), channel_id=1, replica_groups=mesh['row'=8,'col'=16] {'row','col'}, dimensions={0} | all-to-all | bytes 524288 | tf_op jit(solution)/shard_map/while/body/eval_jaxpr/all_to_all | solution.py:102
  254.6 11.7 %cholesky.152 = f32[128,128]{1,0:T(8,128)S(1)} custom-call(f32[128,128]{1,0:T(8,128)S(1)} %fusion.70), custom_call_target="Cholesky" | custom-call | tf_op jit(solution)/shard_map/while/body/eval_jaxpr/jit(cholesky)/cholesky | solution.py:34
  278.5 11.7 %cholesky.153 = f32[128,128]{1,0:T(8,128)S(1)} custom-call(f32[128,128]{1,0:T(8,128)S(1)} %fusion.73), custom_call_target="Cholesky" | custom-call | tf_op jit(solution)/shard_map/while/body/eval_jaxpr/jit(cholesky)/cholesky | solution.py:34
  338.0 15.7 %all-to-all-done = bf16[16,128,256]{2,1,0:T(8,128)(2,1)S(1)} async-done(((bf16[16,128,256]{2,1,0:T(8,128)(2,1)}), bf16[16,128,256]{2,1,0:T(8,128)(2,1)S(1)}, u32[]{:S(2)}, u32[]{:S(2)}) %all-to-all-start) | async-done | bytes 1048608 | tf_op jit(solution)/shard_map/while/body/eval_jaxpr/all_to_all | solution.py:93
  354.9 17.0 %all_to_all.36 = f32[128,1,512]{2,1,0:T(1,128)S(1)} all-to-all(f32[128,1,512]{2,1,0:T(1,128)S(1)} %all_to_all.28), channel_id=1, replica_groups=mesh['row'=8,'col'=16] {'row','col'}, dimensions={0} | all-to-all | bytes 524288 | tf_op jit(solution)/shard_map/while/body/eval_jaxpr/all_to_all | solution.py:101
  372.2 15.2 %all_to_all.37 = f32[128,1,512]{2,1,0:T(1,128)S(1)} all-to-all(f32[128,1,512]{2,1,0:T(1,128)S(1)} %broadcast_in_dim.17), channel_id=1, replica_groups=mesh['row'=8,'col'=16] {'row','col'}, dimensions={0} | all-to-all | bytes 524288 | tf_op jit(solution)/shard_map/while/body/eval_jaxpr/all_to_all | solution.py:102
  388.5 11.7 %cholesky.152 = f32[128,128]{1,0:T(8,128)S(1)} custom-call(f32[128,128]{1,0:T(8,128)S(1)} %fusion.70), custom_call_target="Cholesky" | custom-call | tf_op jit(solution)/shard_map/while/body/eval_jaxpr/jit(cholesky)/cholesky | solution.py:34
  412.4 11.7 %cholesky.153 = f32[128,128]{1,0:T(8,128)S(1)} custom-call(f32[128,128]{1,0:T(8,128)S(1)} %fusion.73), custom_call_target="Cholesky" | custom-call | tf_op jit(solution)/shard_map/while/body/eval_jaxpr/jit(cholesky)/cholesky | solution.py:34
  456.1 11.2 %all-to-all-done.1 = bf16[16,128,256]{2,1,0:T(8,128)(2,1)S(1)} async-done(((bf16[16,128,256]{2,1,0:T(8,128)(2,1)}), bf16[16,128,256]{2,1,0:T(8,128)(2,1)S(1)}, u32[]{:S(2)}, u32[]{:S(2)}) %all-to-all-start.1) | async-done | bytes 1048608 | tf_op jit(solution)/shard_map/while/body/eval_jaxpr/all_to_all | solution.py:93
  471.9 15.7 %all-to-all-done = bf16[16,128,256]{2,1,0:T(8,128)(2,1)S(1)} async-done(((bf16[16,128,256]{2,1,0:T(8,128)(2,1)}), bf16[16,128,256]{2,1,0:T(8,128)(2,1)S(1)}, u32[]{:S(2)}, u32[]{:S(2)}) %all-to-all-start) | async-done | bytes 1048608 | tf_op jit(solution)/shard_map/while/body/eval_jaxpr/all_to_all | solution.py:93
  488.8 17.0 %all_to_all.36 = f32[128,1,512]{2,1,0:T(1,128)S(1)} all-to-all(f32[128,1,512]{2,1,0:T(1,128)S(1)} %all_to_all.28), channel_id=1, replica_groups=mesh['row'=8,'col'=16] {'row','col'}, dimensions={0} | all-to-all | bytes 524288 | tf_op jit(solution)/shard_map/while/body/eval_jaxpr/all_to_all | solution.py:101
  506.2 15.2 %all_to_all.37 = f32[128,1,512]{2,1,0:T(1,128)S(1)} all-to-all(f32[128,1,512]{2,1,0:T(1,128)S(1)} %broadcast_in_dim.17), channel_id=1, replica_groups=mesh['row'=8,'col'=16] {'row','col'}, dimensions={0} | all-to-all | bytes 524288 | tf_op jit(solution)/shard_map/while/body/eval_jaxpr/all_to_all | solution.py:102
  522.4 11.7 %cholesky.152 = f32[128,128]{1,0:T(8,128)S(1)} custom-call(f32[128,128]{1,0:T(8,128)S(1)} %fusion.70), custom_call_target="Cholesky" | custom-call | tf_op jit(solution)/shard_map/while/body/eval_jaxpr/jit(cholesky)/cholesky | solution.py:34
  546.3 11.7 %cholesky.153 = f32[128,128]{1,0:T(8,128)S(1)} custom-call(f32[128,128]{1,0:T(8,128)S(1)} %fusion.73), custom_call_target="Cholesky" | custom-call | tf_op jit(solution)/shard_map/while/body/eval_jaxpr/jit(cholesky)/cholesky | solution.py:34
  (226 shorter events, 242.4 us)
Async XLA Ops:
  7.2 8.0 %copy-start.2 = (f32[256]{0:T(256)S(1)}, f32[256]{0:T(256)}, u32[]{:S(2)}) copy-start(f32[256]{0:T(256)} %param.11) | copy-start | bytes 3076
  7.2 7.9 %copy-start.3 = (s32[32,1,8]{0,2,1:T(8,128)S(1)}, s32[32,1,8]{0,2,1:T(8,128)}, u32[]{:S(2)}) copy-start(s32[32,1,8]{0,2,1:T(8,128)} %param.13) | copy-start | bytes 3076
  7.2 26.6 %copy-start.4 = (s32[32,1]{0,1:T(1,128)S(1)}, s32[32,1]{0,1:T(1,128)}, u32[]{:S(2)}) copy-start(s32[32,1]{0,1:T(1,128)} %param.14) | copy-start | bytes 388
  9.3 24.5 %all-to-all-start.4 = ((bf16[8,256,256]{2,1,0:T(8,128)(2,1)}), bf16[8,256,256]{2,1,0:T(8,128)(2,1)S(1)}, u32[]{:S(2)}, u32[]{:S(2)}) async-start(bf16[8,256,256]{2,1,0:T(8,128)(2,1)} %broadcast_in_dim.13), calls=%async_computation.4 | async-start | bytes 2097152 | tf_op jit(solution)/shard_map/all_to_all | solution.py:87
  41.2 24.4 %all-to-all-start.1 = ((bf16[16,128,256]{2,1,0:T(8,128)(2,1)}), bf16[16,128,256]{2,1,0:T(8,128)(2,1)S(1)}, u32[]{:S(2)}, u32[]{:S(2)}) async-start(bf16[16,128,256]{2,1,0:T(8,128)(2,1)} %eval_jaxpr.3), calls=%async_computation.1 | async-start | bytes 2097152 | tf_op jit(solution)/shard_map/while/body/eval_jaxpr/all_to_all | solution.py:93
  65.7 20.3 %all-to-all-start = ((bf16[16,128,256]{2,1,0:T(8,128)(2,1)}), bf16[16,128,256]{2,1,0:T(8,128)(2,1)S(1)}, u32[]{:S(2)}, u32[]{:S(2)}) async-start(bf16[16,128,256]{2,1,0:T(8,128)(2,1)} %eval_jaxpr.2), calls=%async_computation | async-start | bytes 2097152 | tf_op jit(solution)/shard_map/while/body/eval_jaxpr/all_to_all | solution.py:93
  70.1 99.1 %all-gather.3.cloned.1.call-start = ((), (), s32[]{:S(2)}) async-start(), calls=%async_computation.5 | async-start | bytes 2359296 | tf_op jit(solution)/shard_map/while/body/eval_jaxpr/all_gather | solution.py:124
  86.2 34.2 %copy-start = (f32[256,256]{1,0:T(8,128)}, f32[256,256]{1,0:T(8,128)S(1)}, u32[]{:S(2)}) copy-start(f32[256,256]{1,0:T(8,128)S(1)} %maximum_multiply_fusion.2) | copy-start | bytes 786436 | tf_op jit(solution)/shard_map/while
  169.2 2.7 copy-start.1
  179.3 20.1 %all-to-all-start.1 = ((bf16[16,128,256]{2,1,0:T(8,128)(2,1)}), bf16[16,128,256]{2,1,0:T(8,128)(2,1)S(1)}, u32[]{:S(2)}, u32[]{:S(2)}) async-start(bf16[16,128,256]{2,1,0:T(8,128)(2,1)} %eval_jaxpr.3), calls=%async_computation.1 | async-start | bytes 2097152 | tf_op jit(solution)/shard_map/while/body/eval_jaxpr/all_to_all | solution.py:93
  199.5 20.4 %all-to-all-start = ((bf16[16,128,256]{2,1,0:T(8,128)(2,1)}), bf16[16,128,256]{2,1,0:T(8,128)(2,1)S(1)}, u32[]{:S(2)}, u32[]{:S(2)}) async-start(bf16[16,128,256]{2,1,0:T(8,128)(2,1)} %eval_jaxpr.2), calls=%async_computation | async-start | bytes 2097152 | tf_op jit(solution)/shard_map/while/body/eval_jaxpr/all_to_all | solution.py:93
  203.9 99.1 %all-gather.3.cloned.1.call-start = ((), (), s32[]{:S(2)}) async-start(), calls=%async_computation.5 | async-start | bytes 2359296 | tf_op jit(solution)/shard_map/while/body/eval_jaxpr/all_gather | solution.py:124
  220.1 34.2 %copy-start = (f32[256,256]{1,0:T(8,128)}, f32[256,256]{1,0:T(8,128)S(1)}, u32[]{:S(2)}) copy-start(f32[256,256]{1,0:T(8,128)S(1)} %maximum_multiply_fusion.2) | copy-start | bytes 786436 | tf_op jit(solution)/shard_map/while
  303.1 2.7 copy-start.1
  313.2 20.1 %all-to-all-start.1 = ((bf16[16,128,256]{2,1,0:T(8,128)(2,1)}), bf16[16,128,256]{2,1,0:T(8,128)(2,1)S(1)}, u32[]{:S(2)}, u32[]{:S(2)}) async-start(bf16[16,128,256]{2,1,0:T(8,128)(2,1)} %eval_jaxpr.3), calls=%async_computation.1 | async-start | bytes 2097152 | tf_op jit(solution)/shard_map/while/body/eval_jaxpr/all_to_all | solution.py:93
  333.4 20.4 %all-to-all-start = ((bf16[16,128,256]{2,1,0:T(8,128)(2,1)}), bf16[16,128,256]{2,1,0:T(8,128)(2,1)S(1)}, u32[]{:S(2)}, u32[]{:S(2)}) async-start(bf16[16,128,256]{2,1,0:T(8,128)(2,1)} %eval_jaxpr.2), calls=%async_computation | async-start | bytes 2097152 | tf_op jit(solution)/shard_map/while/body/eval_jaxpr/all_to_all | solution.py:93
  337.8 99.1 %all-gather.3.cloned.1.call-start = ((), (), s32[]{:S(2)}) async-start(), calls=%async_computation.5 | async-start | bytes 2359296 | tf_op jit(solution)/shard_map/while/body/eval_jaxpr/all_gather | solution.py:124
  354.0 34.2 %copy-start = (f32[256,256]{1,0:T(8,128)}, f32[256,256]{1,0:T(8,128)S(1)}, u32[]{:S(2)}) copy-start(f32[256,256]{1,0:T(8,128)S(1)} %maximum_multiply_fusion.2) | copy-start | bytes 786436 | tf_op jit(solution)/shard_map/while
  436.9 2.7 copy-start.1
  447.1 20.1 %all-to-all-start.1 = ((bf16[16,128,256]{2,1,0:T(8,128)(2,1)}), bf16[16,128,256]{2,1,0:T(8,128)(2,1)S(1)}, u32[]{:S(2)}, u32[]{:S(2)}) async-start(bf16[16,128,256]{2,1,0:T(8,128)(2,1)} %eval_jaxpr.3), calls=%async_computation.1 | async-start | bytes 2097152 | tf_op jit(solution)/shard_map/while/body/eval_jaxpr/all_to_all | solution.py:93
  467.3 20.4 %all-to-all-start = ((bf16[16,128,256]{2,1,0:T(8,128)(2,1)}), bf16[16,128,256]{2,1,0:T(8,128)(2,1)S(1)}, u32[]{:S(2)}, u32[]{:S(2)}) async-start(bf16[16,128,256]{2,1,0:T(8,128)(2,1)} %eval_jaxpr.2), calls=%async_computation | async-start | bytes 2097152 | tf_op jit(solution)/shard_map/while/body/eval_jaxpr/all_to_all | solution.py:93
  471.7 99.1 %all-gather.3.cloned.1.call-start = ((), (), s32[]{:S(2)}) async-start(), calls=%async_computation.5 | async-start | bytes 2359296 | tf_op jit(solution)/shard_map/while/body/eval_jaxpr/all_gather | solution.py:124
  487.9 34.2 %copy-start = (f32[256,256]{1,0:T(8,128)}, f32[256,256]{1,0:T(8,128)S(1)}, u32[]{:S(2)}) copy-start(f32[256,256]{1,0:T(8,128)S(1)} %maximum_multiply_fusion.2) | copy-start | bytes 786436 | tf_op jit(solution)/shard_map/while
  570.8 2.7 copy-start.1
Sparse Core Ops, SparseCore 0:
  120.5 21.4 all-gather.2
  254.4 21.4 all-gather.2
  388.3 21.4 all-gather.2
  522.2 21.4 all-gather.2

commit v11 on v8

--- a/solution.py
+++ b/solution.py
@@ -31,7 +31,7 @@
 def cholesky_and_inverse(g, leaf=128):
     n = g.shape[0]
     if n <= leaf:
-        lower = jnp.linalg.cholesky(g)
+        lower = jnp.linalg.cholesky(g, symmetrize_input=False)
         eye = jnp.eye(n, dtype=jnp.float32)
         return lower, jax.scipy.linalg.solve_triangular(lower, eye, lower=True)
     h = n // 2
@@ -110,7 +110,7 @@
     scale = degree_scale[:, None]
     probe = (basis.astype(jnp.float32) * scale).astype(jnp.bfloat16)
     number = lax.axis_size("col") * rows_dev // tile
-    scale_block = gather_rows(degree_scale, "row")[:, None]
+    scale_block = lax.all_gather(degree_scale, "row", axis=0, tiled=True)[:, None]
 
     def loop_step(i, carry):
         block_probe = carry[0]
@@ -122,8 +122,14 @@
         image_block = lax.all_gather(image_late, "row", axis=0, tiled=True)
         gram = (gram + gram.T) * 0.5
         lower, inverse = cholesky_and_inverse(gram)
-        normalized = jnp.dot(image_block, inverse.T, precision=lax.Precision.HIGH, preferred_element_type=jnp.float32)
-        next_probe = (normalized * scale_block).astype(jnp.bfloat16)
+
+        def probe_of(block, inv):
+            normalized = jnp.dot(block, inv.T, precision=lax.Precision.HIGH, preferred_element_type=jnp.float32)
+            return (normalized * scale_block).astype(jnp.bfloat16)
+
+        next_probe = lax.cond(
+            i < ITERS - 1, probe_of, lambda block, inv: jnp.zeros(block.shape, jnp.bfloat16), image_block, inverse
+        )
         return (next_probe, image, inverse, lower)
 
     square = jnp.zeros((width, width), jnp.float32)

time: 548 us -> 544 us (level)
  waiting for transfers between devices: 18.5 us -> 0.08 us
  blocking collectives: 255 us -> 273 us
    all_gather x0 -> x1, blocking collectives: none -> 18.5 us  [body(): lax.all_gather(degree_scale, 'row', axis=0, tiled=True)[:, None]]
    all_to_all x2 -> x1, waiting for transfers between devices: 18.4 us -> 0.01 us  [gather_rows(): lax.all_to_all(jnp.broadcast_to(x, (n,) + x.shape), axis, 0, 0, tiled=False)]
  transfers between devices with their start and end apart: 6 -> 5, of which waited for: 2 -> 0; matrix products, arithmetic and copies ran while one was open for 36% -> 36% of each run, Pallas kernels for 0% -> 0%
where the time goes in v11:
time: 544 us; the launch traced here: 543 us
  blocking collectives  273 us (50%)
  other arithmetic  192 us (35%)
  Pallas kernels  28.1 us (5%)
  matrix products  22.1 us (4%)
  between operations  13.8 us (3%)
  local copies, waits for them, and re-layouts  7.13 us (1%)
  starting transfers between devices  5.84 us (1%)
    all_to_all x4, blocking collectives, sum_scatter_rows(): lax.all_to_all(x.reshape((n, -1) + x.shape[1:]), axis, 0, 0, tiled=False)  130 us
    another operation x24, other arithmetic, cholesky_and_inverse(): lower = jnp.linalg.cholesky(g, symmetrize_input=False)  99.1 us
    another operation x16, other arithmetic, cholesky_and_inverse(): return (lower, jax.scipy.linalg.solve_triangular(lower, eye, lower=True))  83.7 us
    all_to_all x4, blocking collectives, sum_all(): lax.all_to_all(x.reshape(n, -1), axes, 0, 0, tiled=False)  64 us
    all_to_all x4, blocking collectives, sum_all(): lax.all_to_all(jnp.broadcast_to(piece, (n,) + piece.shape), axes, 0, 0, t...  60.9 us
    pallas_call x4, Pallas kernels, apply_tiles(): pl.pallas_call(kernel, grid_spec=spec, out_shape=jax.ShapeDtypeStruct((tr...  28.1 us
    all_gather x1, blocking collectives, body(): lax.all_gather(degree_scale, 'row', axis=0, tiled=True)[:, None]  18.5 us
  transfers between devices with their start and end apart: 5, of which 0 were waited for; matrix products, arithmetic and copies ran while one was open for 36% of the time, Pallas kernels for 0%

profile of v11, /device:TPU:1, one launch (start us, length us, event | category | flops | bytes accessed | tf_op | source)
XLA Modules:
  0.0 542.9 jit_solution(4855669684486800872)
XLA Ops:
  15.2 18.5 %all-gather = f32[8,1,256]{2,1,0:T(1,128)S(1)} all-gather(f32[1,1,256]{2,1,0:T(1,128)S(1)} %bitcast.92), channel_id=1, replica_groups=mesh['row'=8,'col'=16] {'row'}, dimensions={0}, use_global_device_ids=true | all-gather | bytes 9216 | tf_op jit(solution)/shard_map/all_gather | solution.py:113
  33.8 498.7 %while.20 = (s32[]{:T(128)}, bf16[2048,256]{1,0:T(8,128)(2,1)}, f32[256,256]{1,0:T(8,128)}, f32[256,256]{1,0:T(8,128)}, f32[256,256]{1,0:T(8,128)}, /*index=5*/s...) while((s32[]{:T(128)}, bf16[2048,256]{1,0:T(8,128)(2,1)}, ...), condition=%wide.wide.region_7.10_spmd, body=%wide.wide.region_0.9_spmd.sunk | while | flops 1161821952 | bytes 26557704 | solution.py:137
  40.9 35.5 %all_to_all.46 = bf16[16,256,256]{2,1,0:T(8,128)(2,1)S(1)} all-to-all(bf16[16,256,256]{2,1,0:T(8,128)(2,1)} %bitcast.88), channel_id=1, replica_groups=mesh['row'=8,'col'=16] {'col'}, dimensions={0} | all-to-all | bytes 4194304 | tf_op jit(solution)/shard_map/while/body/eval_jaxpr/all_to_all | solution.py:90
  77.7 16.0 %all_to_all.47 = f32[128,1,512]{2,1,0:T(1,128)S(1)} all-to-all(f32[128,1,512]{2,1,0:T(1,128)S(1)} %all_to_all.39), channel_id=1, replica_groups=mesh['row'=8,'col'=16] {'row','col'}, dimensions={0} | all-to-all | bytes 524288 | tf_op jit(solution)/shard_map/while/body/eval_jaxpr/all_to_all | solution.py:98
  94.0 15.2 %all_to_all.48 = f32[128,1,512]{2,1,0:T(1,128)S(1)} all-to-all(f32[128,1,512]{2,1,0:T(1,128)S(1)} %broadcast_in_dim.20), channel_id=1, replica_groups=mesh['row'=8,'col'=16] {'row','col'}, dimensions={0} | all-to-all | bytes 524288 | tf_op jit(solution)/shard_map/while/body/eval_jaxpr/all_to_all | solution.py:99
  110.1 11.7 %cholesky.173 = f32[128,128]{1,0:T(8,128)S(1)} custom-call(f32[128,128]{1,0:T(8,128)S(1)} %slice.43), custom_call_target="Cholesky" | custom-call | tf_op jit(solution)/shard_map/while/body/eval_jaxpr/jit(cholesky)/cholesky | solution.py:34
  134.0 11.7 %cholesky.174 = f32[128,128]{1,0:T(8,128)S(1)} custom-call(f32[128,128]{1,0:T(8,128)S(1)} %convolution_subtract_fusion.3), custom_call_target="Cholesky" | custom-call | tf_op jit(solution)/shard_map/while/body/eval_jaxpr/jit(cholesky)/cholesky | solution.py:34
  147.0 9.8 %custom-call.16 = f32[1,128,128]{1,2,0:T(8,128)S(1)} custom-call(f32[1,128,128]{2,1,0:T(8,128)S(1)} %get-tuple-element.339), custom_call_target="InvertDiagBlocksLowerTriangular" | custom-call | tf_op jit(solution)/shard_map/while/body/eval_jaxpr/jit(_solve_triangular)/triangular_solve | solution.py:36
  169.3 31.4 %all_to_all.46 = bf16[16,256,256]{2,1,0:T(8,128)(2,1)S(1)} all-to-all(bf16[16,256,256]{2,1,0:T(8,128)(2,1)} %bitcast.88), channel_id=1, replica_groups=mesh['row'=8,'col'=16] {'col'}, dimensions={0} | all-to-all | bytes 4194304 | tf_op jit(solution)/shard_map/while/body/eval_jaxpr/all_to_all | solution.py:90
  201.9 16.0 %all_to_all.47 = f32[128,1,512]{2,1,0:T(1,128)S(1)} all-to-all(f32[128,1,512]{2,1,0:T(1,128)S(1)} %all_to_all.39), channel_id=1, replica_groups=mesh['row'=8,'col'=16] {'row','col'}, dimensions={0} | all-to-all | bytes 524288 | tf_op jit(solution)/shard_map/while/body/eval_jaxpr/all_to_all | solution.py:98
  218.3 15.2 %all_to_all.48 = f32[128,1,512]{2,1,0:T(1,128)S(1)} all-to-all(f32[128,1,512]{2,1,0:T(1,128)S(1)} %broadcast_in_dim.20), channel_id=1, replica_groups=mesh['row'=8,'col'=16] {'row','col'}, dimensions={0} | all-to-all | bytes 524288 | tf_op jit(solution)/shard_map/while/body/eval_jaxpr/all_to_all | solution.py:99
  234.4 11.7 %cholesky.173 = f32[128,128]{1,0:T(8,128)S(1)} custom-call(f32[128,128]{1,0:T(8,128)S(1)} %slice.43), custom_call_target="Cholesky" | custom-call | tf_op jit(solution)/shard_map/while/body/eval_jaxpr/jit(cholesky)/cholesky | solution.py:34
  258.2 11.7 %cholesky.174 = f32[128,128]{1,0:T(8,128)S(1)} custom-call(f32[128,128]{1,0:T(8,128)S(1)} %convolution_subtract_fusion.3), custom_call_target="Cholesky" | custom-call | tf_op jit(solution)/shard_map/while/body/eval_jaxpr/jit(cholesky)/cholesky | solution.py:34
  293.5 31.4 %all_to_all.46 = bf16[16,256,256]{2,1,0:T(8,128)(2,1)S(1)} all-to-all(bf16[16,256,256]{2,1,0:T(8,128)(2,1)} %bitcast.88), channel_id=1, replica_groups=mesh['row'=8,'col'=16] {'col'}, dimensions={0} | all-to-all | bytes 4194304 | tf_op jit(solution)/shard_map/while/body/eval_jaxpr/all_to_all | solution.py:90
  326.1 16.0 %all_to_all.47 = f32[128,1,512]{2,1,0:T(1,128)S(1)} all-to-all(f32[128,1,512]{2,1,0:T(1,128)S(1)} %all_to_all.39), channel_id=1, replica_groups=mesh['row'=8,'col'=16] {'row','col'}, dimensions={0} | all-to-all | bytes 524288 | tf_op jit(solution)/shard_map/while/body/eval_jaxpr/all_to_all | solution.py:98
  342.5 15.2 %all_to_all.48 = f32[128,1,512]{2,1,0:T(1,128)S(1)} all-to-all(f32[128,1,512]{2,1,0:T(1,128)S(1)} %broadcast_in_dim.20), channel_id=1, replica_groups=mesh['row'=8,'col'=16] {'row','col'}, dimensions={0} | all-to-all | bytes 524288 | tf_op jit(solution)/shard_map/while/body/eval_jaxpr/all_to_all | solution.py:99
  358.6 11.7 %cholesky.173 = f32[128,128]{1,0:T(8,128)S(1)} custom-call(f32[128,128]{1,0:T(8,128)S(1)} %slice.43), custom_call_target="Cholesky" | custom-call | tf_op jit(solution)/shard_map/while/body/eval_jaxpr/jit(cholesky)/cholesky | solution.py:34
  382.5 11.7 %cholesky.174 = f32[128,128]{1,0:T(8,128)S(1)} custom-call(f32[128,128]{1,0:T(8,128)S(1)} %convolution_subtract_fusion.3), custom_call_target="Cholesky" | custom-call | tf_op jit(solution)/shard_map/while/body/eval_jaxpr/jit(cholesky)/cholesky | solution.py:34
  395.5 9.8 %custom-call.16 = f32[1,128,128]{1,2,0:T(8,128)S(1)} custom-call(f32[1,128,128]{2,1,0:T(8,128)S(1)} %get-tuple-element.339), custom_call_target="InvertDiagBlocksLowerTriangular" | custom-call | tf_op jit(solution)/shard_map/while/body/eval_jaxpr/jit(_solve_triangular)/triangular_solve | solution.py:36
  417.8 31.4 %all_to_all.46 = bf16[16,256,256]{2,1,0:T(8,128)(2,1)S(1)} all-to-all(bf16[16,256,256]{2,1,0:T(8,128)(2,1)} %bitcast.88), channel_id=1, replica_groups=mesh['row'=8,'col'=16] {'col'}, dimensions={0} | all-to-all | bytes 4194304 | tf_op jit(solution)/shard_map/while/body/eval_jaxpr/all_to_all | solution.py:90
  450.4 16.0 %all_to_all.47 = f32[128,1,512]{2,1,0:T(1,128)S(1)} all-to-all(f32[128,1,512]{2,1,0:T(1,128)S(1)} %all_to_all.39), channel_id=1, replica_groups=mesh['row'=8,'col'=16] {'row','col'}, dimensions={0} | all-to-all | bytes 524288 | tf_op jit(solution)/shard_map/while/body/eval_jaxpr/all_to_all | solution.py:98
  466.8 15.2 %all_to_all.48 = f32[128,1,512]{2,1,0:T(1,128)S(1)} all-to-all(f32[128,1,512]{2,1,0:T(1,128)S(1)} %broadcast_in_dim.20), channel_id=1, replica_groups=mesh['row'=8,'col'=16] {'row','col'}, dimensions={0} | all-to-all | bytes 524288 | tf_op jit(solution)/shard_map/while/body/eval_jaxpr/all_to_all | solution.py:99
  482.9 11.7 %cholesky.173 = f32[128,128]{1,0:T(8,128)S(1)} custom-call(f32[128,128]{1,0:T(8,128)S(1)} %slice.43), custom_call_target="Cholesky" | custom-call | tf_op jit(solution)/shard_map/while/body/eval_jaxpr/jit(cholesky)/cholesky | solution.py:34
  506.7 11.7 %cholesky.174 = f32[128,128]{1,0:T(8,128)S(1)} custom-call(f32[128,128]{1,0:T(8,128)S(1)} %convolution_subtract_fusion.3), custom_call_target="Cholesky" | custom-call | tf_op jit(solution)/shard_map/while/body/eval_jaxpr/jit(cholesky)/cholesky | solution.py:34
  (161 shorter events, 154.0 us)
Async XLA Ops:
  7.2 8.1 %copy-start.2 = (f32[256]{0:T(256)S(1)}, f32[256]{0:T(256)}, u32[]{:S(2)}) copy-start(f32[256]{0:T(256)} %param.13) | copy-start | bytes 3076
  7.2 7.9 %copy-start.4 = (s32[32,1,8]{0,2,1:T(8,128)S(1)}, s32[32,1,8]{0,2,1:T(8,128)}, u32[]{:S(2)}) copy-start(s32[32,1,8]{0,2,1:T(8,128)} %param.15) | copy-start | bytes 3076
  7.2 26.6 %copy-start.3 = (s32[32,1]{0,1:T(1,128)S(1)}, s32[32,1]{0,1:T(1,128)}, u32[]{:S(2)}) copy-start(s32[32,1]{0,1:T(1,128)} %param.16) | copy-start | bytes 388
  9.3 24.5 %all-to-all-start.3 = ((bf16[8,256,256]{2,1,0:T(8,128)(2,1)}), bf16[8,256,256]{2,1,0:T(8,128)(2,1)}, u32[]{:S(2)}, u32[]{:S(2)}) async-start(bf16[8,256,256]{2,1,0:T(8,128)(2,1)} %broadcast_in_dim.15), calls=%async_computation.3 | async-start | bytes 2097152 | tf_op jit(solution)/shard_map/all_to_all | solution.py:84
  15.1 18.6 %copy-start.1 = (s32[32,1,8]{2,0,1:T(8,128)}, s32[32,1,8]{2,0,1:T(8,128)S(1)}, u32[]{:S(2)}) copy-start(s32[32,1,8]{2,0,1:T(8,128)S(1)} %copy.23) | copy-start | bytes 3076
  33.8 124.8 %all-gather.3.cloned.1.call-start = ((), (), s32[]{:S(2)}) async-start(), calls=%async_computation.4 | async-start | bytes 2359296 | tf_op jit(solution)/shard_map/while/body/eval_jaxpr/all_gather | solution.py:122
  76.8 33.1 %copy-start = (f32[256,256]{1,0:T(8,128)}, f32[256,256]{1,0:T(8,128)S(1)}, u32[]{:S(2)}) copy-start(f32[256,256]{1,0:T(8,128)S(1)} %broadcast_multiply_fusion.3) | copy-start | bytes 786436 | tf_op jit(solution)/shard_map/while
  162.2 120.6 %all-gather.3.cloned.1.call-start = ((), (), s32[]{:S(2)}) async-start(), calls=%async_computation.4 | async-start | bytes 2359296 | tf_op jit(solution)/shard_map/while/body/eval_jaxpr/all_gather | solution.py:122
  201.0 33.1 %copy-start = (f32[256,256]{1,0:T(8,128)}, f32[256,256]{1,0:T(8,128)S(1)}, u32[]{:S(2)}) copy-start(f32[256,256]{1,0:T(8,128)S(1)} %broadcast_multiply_fusion.3) | copy-start | bytes 786436 | tf_op jit(solution)/shard_map/while
  286.5 120.6 %all-gather.3.cloned.1.call-start = ((), (), s32[]{:S(2)}) async-start(), calls=%async_computation.4 | async-start | bytes 2359296 | tf_op jit(solution)/shard_map/while/body/eval_jaxpr/all_gather | solution.py:122
  325.3 33.1 %copy-start = (f32[256,256]{1,0:T(8,128)}, f32[256,256]{1,0:T(8,128)S(1)}, u32[]{:S(2)}) copy-start(f32[256,256]{1,0:T(8,128)S(1)} %broadcast_multiply_fusion.3) | copy-start | bytes 786436 | tf_op jit(solution)/shard_map/while
  410.8 120.7 %all-gather.3.cloned.1.call-start = ((), (), s32[]{:S(2)}) async-start(), calls=%async_computation.4 | async-start | bytes 2359296 | tf_op jit(solution)/shard_map/while/body/eval_jaxpr/all_gather | solution.py:122
  449.5 33.2 %copy-start = (f32[256,256]{1,0:T(8,128)}, f32[256,256]{1,0:T(8,128)S(1)}, u32[]{:S(2)}) copy-start(f32[256,256]{1,0:T(8,128)S(1)} %broadcast_multiply_fusion.3) | copy-start | bytes 786436 | tf_op jit(solution)/shard_map/while
Sparse Core Ops, SparseCore 0:
  110.0 21.4 all-gather.2
  234.3 21.4 all-gather.2
  358.6 21.4 all-gather.2
  482.8 21.4 all-gather.2

commit v12 on v8

--- a/solution.py
+++ b/solution.py
@@ -31,7 +31,7 @@
 def cholesky_and_inverse(g, leaf=128):
     n = g.shape[0]
     if n <= leaf:
-        lower = jnp.linalg.cholesky(g)
+        lower = jnp.linalg.cholesky(g, symmetrize_input=False)
         eye = jnp.eye(n, dtype=jnp.float32)
         return lower, jax.scipy.linalg.solve_triangular(lower, eye, lower=True)
     h = n // 2
@@ -110,7 +110,7 @@
     scale = degree_scale[:, None]
     probe = (basis.astype(jnp.float32) * scale).astype(jnp.bfloat16)
     number = lax.axis_size("col") * rows_dev // tile
-    scale_block = gather_rows(degree_scale, "row")[:, None]
+    scale_block = lax.all_gather(degree_scale, "row", axis=0, tiled=True)[:, None]
 
     def loop_step(i, carry):
         block_probe = carry[0]
@@ -120,7 +120,6 @@
         gram = sum_all(gram_of(image, nodes), ("row", "col"))
         image_late, gram = lax.optimization_barrier((image, gram))
         image_block = lax.all_gather(image_late, "row", axis=0, tiled=True)
-        gram = (gram + gram.T) * 0.5
         lower, inverse = cholesky_and_inverse(gram)
         normalized = jnp.dot(image_block, inverse.T, precision=lax.Precision.HIGH, preferred_element_type=jnp.float32)
         next_probe = (normalized * scale_block).astype(jnp.bfloat16)

time: 548 us -> 541 us (0.987)
  waiting for transfers between devices: 18.5 us -> 0.08 us
  blocking collectives: 255 us -> 273 us
    all_gather x0 -> x1, blocking collectives: none -> 18.5 us  [body(): lax.all_gather(degree_scale, 'row', axis=0, tiled=True)[:, None]]
    all_to_all x2 -> x1, waiting for transfers between devices: 18.4 us -> 0.01 us  [gather_rows(): lax.all_to_all(jnp.broadcast_to(x, (n,) + x.shape), axis, 0, 0, tiled=False)]
  transfers between devices with their start and end apart: 6 -> 5, of which waited for: 2 -> 0; matrix products, arithmetic and copies ran while one was open for 36% -> 36% of each run, Pallas kernels for 0% -> 0%
where the time goes in v12:
time: 541 us; the launch traced here: 540 us
  blocking collectives  273 us (50%)
  other arithmetic  192 us (35%)
  Pallas kernels  27 us (5%)
  matrix products  22.1 us (4%)
  between operations  13.8 us (3%)
  starting transfers between devices  5.95 us (1%)
  local copies, waits for them, and re-layouts  5.58 us (1%)
    all_to_all x4, blocking collectives, sum_scatter_rows(): lax.all_to_all(x.reshape((n, -1) + x.shape[1:]), axis, 0, 0, tiled=False)  130 us
    another operation x24, other arithmetic, cholesky_and_inverse(): lower = jnp.linalg.cholesky(g, symmetrize_input=False)  99.1 us
    another operation x16, other arithmetic, cholesky_and_inverse(): return (lower, jax.scipy.linalg.solve_triangular(lower, eye, lower=True))  83.8 us
    all_to_all x4, blocking collectives, sum_all(): lax.all_to_all(x.reshape(n, -1), axes, 0, 0, tiled=False)  63.9 us
    all_to_all x4, blocking collectives, sum_all(): lax.all_to_all(jnp.broadcast_to(piece, (n,) + piece.shape), axes, 0, 0, t...  60.9 us
    pallas_call x4, Pallas kernels, apply_tiles(): pl.pallas_call(kernel, grid_spec=spec, out_shape=jax.ShapeDtypeStruct((tr...  27 us
    all_gather x1, blocking collectives, body(): lax.all_gather(degree_scale, 'row', axis=0, tiled=True)[:, None]  18.5 us
    dot_general x4, matrix products, loop_step(): jnp.dot(image_block, inverse.T, precision=lax.Precision.HIGH, preferred_e...  10.8 us
  transfers between devices with their start and end apart: 5, of which 0 were waited for; matrix products, arithmetic and copies ran while one was open for 36% of the time, Pallas kernels for 0%

profile of v12, /device:TPU:1, one launch (start us, length us, event | category | flops | bytes accessed | tf_op | source)
XLA Modules:
  0.0 539.9 jit_solution(7817459836968721012)
XLA Ops:
  15.2 18.5 %all-gather = f32[8,1,256]{2,1,0:T(1,128)S(1)} all-gather(f32[1,1,256]{2,1,0:T(1,128)S(1)} %bitcast.95), channel_id=1, replica_groups=mesh['row'=8,'col'=16] {'row'}, dimensions={0}, use_global_device_ids=true | all-gather | bytes 9216 | tf_op jit(solution)/shard_map/all_gather | solution.py:113
  33.8 495.7 %while.17 = (s32[]{:T(128)}, bf16[2048,256]{1,0:T(8,128)(2,1)S(1)}, f32[256,256]{1,0:T(8,128)}, f32[256,256]{1,0:T(8,128)}, f32[256,256]{1,0:T(8,128)}, /*index=...) while((s32[]{:T(128)}, bf16[2048,256]{1,0:T(8,128)(2,1)S(1)}, ...), condition=%wide.wide.region_5.8_spmd, body=%wide.wide.region_0.7_spmd.sunk | while | flops 1161690880 | bytes 26295532 | solution.py:130
  40.6 35.5 %all_to_all.34 = bf16[16,256,256]{2,1,0:T(8,128)(2,1)S(1)} all-to-all(bf16[16,256,256]{2,1,0:T(8,128)(2,1)} %bitcast.90), channel_id=1, replica_groups=mesh['row'=8,'col'=16] {'col'}, dimensions={0} | all-to-all | bytes 4194304 | tf_op jit(solution)/shard_map/while/body/eval_jaxpr/all_to_all | solution.py:90
  77.4 16.0 %all_to_all.35 = f32[128,1,512]{2,1,0:T(1,128)S(1)} all-to-all(f32[128,1,512]{2,1,0:T(1,128)S(1)} %all_to_all.27), channel_id=1, replica_groups=mesh['row'=8,'col'=16] {'row','col'}, dimensions={0} | all-to-all | bytes 524288 | tf_op jit(solution)/shard_map/while/body/eval_jaxpr/all_to_all | solution.py:98
  93.7 15.2 %all_to_all.36 = f32[128,1,512]{2,1,0:T(1,128)S(1)} all-to-all(f32[128,1,512]{2,1,0:T(1,128)S(1)} %broadcast_in_dim.18), channel_id=1, replica_groups=mesh['row'=8,'col'=16] {'row','col'}, dimensions={0} | all-to-all | bytes 524288 | tf_op jit(solution)/shard_map/while/body/eval_jaxpr/all_to_all | solution.py:99
  109.7 11.7 %cholesky.173 = f32[128,128]{1,0:T(8,128)S(1)} custom-call(f32[128,128]{1,0:T(8,128)S(1)} %slice.28), custom_call_target="Cholesky" | custom-call | tf_op jit(solution)/shard_map/while/body/eval_jaxpr/jit(cholesky)/cholesky | solution.py:34
  122.7 9.8 %custom-call.15 = f32[1,128,128]{1,2,0:T(8,128)S(1)} custom-call(f32[1,128,128]{2,1,0:T(8,128)S(1)} %get-tuple-element.223), custom_call_target="InvertDiagBlocksLowerTriangular" | custom-call | tf_op jit(solution)/shard_map/while/body/eval_jaxpr/jit(_solve_triangular)/triangular_solve | solution.py:36
  133.5 11.7 %cholesky.174 = f32[128,128]{1,0:T(8,128)S(1)} custom-call(f32[128,128]{1,0:T(8,128)S(1)} %convolution_subtract_fusion.3), custom_call_target="Cholesky" | custom-call | tf_op jit(solution)/shard_map/while/body/eval_jaxpr/jit(cholesky)/cholesky | solution.py:34
  167.6 31.4 %all_to_all.34 = bf16[16,256,256]{2,1,0:T(8,128)(2,1)S(1)} all-to-all(bf16[16,256,256]{2,1,0:T(8,128)(2,1)} %bitcast.90), channel_id=1, replica_groups=mesh['row'=8,'col'=16] {'col'}, dimensions={0} | all-to-all | bytes 4194304 | tf_op jit(solution)/shard_map/while/body/eval_jaxpr/all_to_all | solution.py:90
  200.3 16.0 %all_to_all.35 = f32[128,1,512]{2,1,0:T(1,128)S(1)} all-to-all(f32[128,1,512]{2,1,0:T(1,128)S(1)} %all_to_all.27), channel_id=1, replica_groups=mesh['row'=8,'col'=16] {'row','col'}, dimensions={0} | all-to-all | bytes 524288 | tf_op jit(solution)/shard_map/while/body/eval_jaxpr/all_to_all | solution.py:98
  216.6 15.2 %all_to_all.36 = f32[128,1,512]{2,1,0:T(1,128)S(1)} all-to-all(f32[128,1,512]{2,1,0:T(1,128)S(1)} %broadcast_in_dim.18), channel_id=1, replica_groups=mesh['row'=8,'col'=16] {'row','col'}, dimensions={0} | all-to-all | bytes 524288 | tf_op jit(solution)/shard_map/while/body/eval_jaxpr/all_to_all | solution.py:99
  232.5 11.7 %cholesky.173 = f32[128,128]{1,0:T(8,128)S(1)} custom-call(f32[128,128]{1,0:T(8,128)S(1)} %slice.28), custom_call_target="Cholesky" | custom-call | tf_op jit(solution)/shard_map/while/body/eval_jaxpr/jit(cholesky)/cholesky | solution.py:34
  256.4 11.7 %cholesky.174 = f32[128,128]{1,0:T(8,128)S(1)} custom-call(f32[128,128]{1,0:T(8,128)S(1)} %convolution_subtract_fusion.3), custom_call_target="Cholesky" | custom-call | tf_op jit(solution)/shard_map/while/body/eval_jaxpr/jit(cholesky)/cholesky | solution.py:34
  269.4 9.8 %custom-call.16 = f32[1,128,128]{1,2,0:T(8,128)S(1)} custom-call(f32[1,128,128]{2,1,0:T(8,128)S(1)} %get-tuple-element.225), custom_call_target="InvertDiagBlocksLowerTriangular" | custom-call | tf_op jit(solution)/shard_map/while/body/eval_jaxpr/jit(_solve_triangular)/triangular_solve | solution.py:36
  290.5 31.4 %all_to_all.34 = bf16[16,256,256]{2,1,0:T(8,128)(2,1)S(1)} all-to-all(bf16[16,256,256]{2,1,0:T(8,128)(2,1)} %bitcast.90), channel_id=1, replica_groups=mesh['row'=8,'col'=16] {'col'}, dimensions={0} | all-to-all | bytes 4194304 | tf_op jit(solution)/shard_map/while/body/eval_jaxpr/all_to_all | solution.py:90
  323.1 16.0 %all_to_all.35 = f32[128,1,512]{2,1,0:T(1,128)S(1)} all-to-all(f32[128,1,512]{2,1,0:T(1,128)S(1)} %all_to_all.27), channel_id=1, replica_groups=mesh['row'=8,'col'=16] {'row','col'}, dimensions={0} | all-to-all | bytes 524288 | tf_op jit(solution)/shard_map/while/body/eval_jaxpr/all_to_all | solution.py:98
  339.5 15.2 %all_to_all.36 = f32[128,1,512]{2,1,0:T(1,128)S(1)} all-to-all(f32[128,1,512]{2,1,0:T(1,128)S(1)} %broadcast_in_dim.18), channel_id=1, replica_groups=mesh['row'=8,'col'=16] {'row','col'}, dimensions={0} | all-to-all | bytes 524288 | tf_op jit(solution)/shard_map/while/body/eval_jaxpr/all_to_all | solution.py:99
  355.4 11.7 %cholesky.173 = f32[128,128]{1,0:T(8,128)S(1)} custom-call(f32[128,128]{1,0:T(8,128)S(1)} %slice.28), custom_call_target="Cholesky" | custom-call | tf_op jit(solution)/shard_map/while/body/eval_jaxpr/jit(cholesky)/cholesky | solution.py:34
  379.3 11.7 %cholesky.174 = f32[128,128]{1,0:T(8,128)S(1)} custom-call(f32[128,128]{1,0:T(8,128)S(1)} %convolution_subtract_fusion.3), custom_call_target="Cholesky" | custom-call | tf_op jit(solution)/shard_map/while/body/eval_jaxpr/jit(cholesky)/cholesky | solution.py:34
  413.4 31.4 %all_to_all.34 = bf16[16,256,256]{2,1,0:T(8,128)(2,1)S(1)} all-to-all(bf16[16,256,256]{2,1,0:T(8,128)(2,1)} %bitcast.90), channel_id=1, replica_groups=mesh['row'=8,'col'=16] {'col'}, dimensions={0} | all-to-all | bytes 4194304 | tf_op jit(solution)/shard_map/while/body/eval_jaxpr/all_to_all | solution.py:90
  446.0 16.0 %all_to_all.35 = f32[128,1,512]{2,1,0:T(1,128)S(1)} all-to-all(f32[128,1,512]{2,1,0:T(1,128)S(1)} %all_to_all.27), channel_id=1, replica_groups=mesh['row'=8,'col'=16] {'row','col'}, dimensions={0} | all-to-all | bytes 524288 | tf_op jit(solution)/shard_map/while/body/eval_jaxpr/all_to_all | solution.py:98
  462.4 15.2 %all_to_all.36 = f32[128,1,512]{2,1,0:T(1,128)S(1)} all-to-all(f32[128,1,512]{2,1,0:T(1,128)S(1)} %broadcast_in_dim.18), channel_id=1, replica_groups=mesh['row'=8,'col'=16] {'row','col'}, dimensions={0} | all-to-all | bytes 524288 | tf_op jit(solution)/shard_map/while/body/eval_jaxpr/all_to_all | solution.py:99
  478.3 11.7 %cholesky.173 = f32[128,128]{1,0:T(8,128)S(1)} custom-call(f32[128,128]{1,0:T(8,128)S(1)} %slice.28), custom_call_target="Cholesky" | custom-call | tf_op jit(solution)/shard_map/while/body/eval_jaxpr/jit(cholesky)/cholesky | solution.py:34
  502.2 11.7 %cholesky.174 = f32[128,128]{1,0:T(8,128)S(1)} custom-call(f32[128,128]{1,0:T(8,128)S(1)} %convolution_subtract_fusion.3), custom_call_target="Cholesky" | custom-call | tf_op jit(solution)/shard_map/while/body/eval_jaxpr/jit(cholesky)/cholesky | solution.py:34
  (157 shorter events, 139.1 us)
Async XLA Ops:
  7.2 8.1 %copy-start.3 = (f32[256]{0:T(256)S(1)}, f32[256]{0:T(256)}, u32[]{:S(2)}) copy-start(f32[256]{0:T(256)} %param.11) | copy-start | bytes 3076
  7.2 7.9 %copy-start.5 = (s32[32,1,8]{0,2,1:T(8,128)S(1)}, s32[32,1,8]{0,2,1:T(8,128)}, u32[]{:S(2)}) copy-start(s32[32,1,8]{0,2,1:T(8,128)} %param.13) | copy-start | bytes 3076
  7.2 26.6 %copy-start.4 = (s32[32,1]{0,1:T(1,128)S(1)}, s32[32,1]{0,1:T(1,128)}, u32[]{:S(2)}) copy-start(s32[32,1]{0,1:T(1,128)} %param.14) | copy-start | bytes 388
  9.3 24.5 %all-to-all-start.3 = ((bf16[8,256,256]{2,1,0:T(8,128)(2,1)}), bf16[8,256,256]{2,1,0:T(8,128)(2,1)S(1)}, u32[]{:S(2)}, u32[]{:S(2)}) async-start(bf16[8,256,256]{2,1,0:T(8,128)(2,1)} %broadcast_in_dim.13), calls=%async_computation.3 | async-start | bytes 2097152 | tf_op jit(solution)/shard_map/all_to_all | solution.py:84
  15.1 18.6 %copy-start.2 = (s32[32,1,8]{2,0,1:T(8,128)}, s32[32,1,8]{2,0,1:T(8,128)S(1)}, u32[]{:S(2)}) copy-start(s32[32,1,8]{2,0,1:T(8,128)S(1)} %copy.20) | copy-start | bytes 3076
  33.8 124.3 %all-gather.3.cloned.1.call-start = ((), (), s32[]{:S(2)}) async-start(), calls=%async_computation.4 | async-start | bytes 2359296 | tf_op jit(solution)/shard_map/while/body/eval_jaxpr/all_gather | solution.py:122
  76.5 33.1 %copy-start = (f32[256,256]{1,0:T(8,128)}, f32[256,256]{1,0:T(8,128)S(1)}, u32[]{:S(2)}) copy-start(f32[256,256]{1,0:T(8,128)S(1)} %broadcast_multiply_fusion.3) | copy-start | bytes 786436 | tf_op jit(solution)/shard_map/while
  158.1 2.7 copy-start.1
  160.8 120.1 %all-gather.3.cloned.1.call-start = ((), (), s32[]{:S(2)}) async-start(), calls=%async_computation.4 | async-start | bytes 2359296 | tf_op jit(solution)/shard_map/while/body/eval_jaxpr/all_gather | solution.py:122
  199.4 33.1 %copy-start = (f32[256,256]{1,0:T(8,128)}, f32[256,256]{1,0:T(8,128)S(1)}, u32[]{:S(2)}) copy-start(f32[256,256]{1,0:T(8,128)S(1)} %broadcast_multiply_fusion.3) | copy-start | bytes 786436 | tf_op jit(solution)/shard_map/while
  280.9 2.7 copy-start.1
  283.7 120.1 %all-gather.3.cloned.1.call-start = ((), (), s32[]{:S(2)}) async-start(), calls=%async_computation.4 | async-start | bytes 2359296 | tf_op jit(solution)/shard_map/while/body/eval_jaxpr/all_gather | solution.py:122
  322.3 33.1 %copy-start = (f32[256,256]{1,0:T(8,128)}, f32[256,256]{1,0:T(8,128)S(1)}, u32[]{:S(2)}) copy-start(f32[256,256]{1,0:T(8,128)S(1)} %broadcast_multiply_fusion.3) | copy-start | bytes 786436 | tf_op jit(solution)/shard_map/while
  403.8 2.7 copy-start.1
  406.6 120.1 %all-gather.3.cloned.1.call-start = ((), (), s32[]{:S(2)}) async-start(), calls=%async_computation.4 | async-start | bytes 2359296 | tf_op jit(solution)/shard_map/while/body/eval_jaxpr/all_gather | solution.py:122
  445.1 33.1 %copy-start = (f32[256,256]{1,0:T(8,128)}, f32[256,256]{1,0:T(8,128)S(1)}, u32[]{:S(2)}) copy-start(f32[256,256]{1,0:T(8,128)S(1)} %broadcast_multiply_fusion.3) | copy-start | bytes 786436 | tf_op jit(solution)/shard_map/while
  526.7 2.7 copy-start.1
Sparse Core Ops, SparseCore 0:
  109.8 21.4 all-gather.2
  232.7 21.4 all-gather.2
  355.5 21.4 all-gather.2
  478.4 21.4 all-gather.2

commit v13 on v12

--- a/solution.py
+++ b/solution.py
@@ -79,12 +79,6 @@
     )(index.reshape(-1), counts, tiles, basis)
 
 
-def gather_rows(x, axis):
-    n = lax.axis_size(axis)
-    got = lax.all_to_all(jnp.broadcast_to(x, (n,) + x.shape), axis, 0, 0, tiled=False)
-    return got.reshape((-1,) + x.shape[1:])
-
-
 def sum_scatter_rows(x, axis):
     n = lax.axis_size(axis)
     got = lax.all_to_all(x.reshape((n, -1) + x.shape[1:]), axis, 0, 0, tiled=False)
@@ -126,7 +120,7 @@
         return (next_probe, image, inverse, lower)
 
     square = jnp.zeros((width, width), jnp.float32)
-    start = (gather_rows(probe, "row"), jnp.zeros(basis.shape, jnp.float32), square, square)
+    start = (lax.all_gather(probe, "row", axis=0, tiled=True), jnp.zeros(basis.shape, jnp.float32), square, square)
     _, image, inverse, lower = lax.fori_loop(0, ITERS, loop_step, start)
     embedding = dot_hi(image, inverse.T)
     factor = lower.T

time: 541 us -> 550 us (1.017)
  waiting for transfers between devices: 0.08 us -> 15.3 us
  blocking collectives: 273 us -> 266 us
  starting transfers between devices: 5.95 us -> 0.05 us
    all_gather x0 -> x1, waiting for transfers between devices: none -> 15.2 us  [body(): lax.all_gather(probe, 'row', axis=0, tiled=True)]
    all_gather x1, blocking collectives: 18.5 us -> 12.1 us  [body(): lax.all_gather(degree_scale, 'row', axis=0, tiled=True)[:, None]]
    all_to_all x1 -> x0, starting transfers between devices: 5.79 us -> none  [gather_rows(): lax.all_to_all(jnp.broadcast_to(x, (n,) + x.shape), axis, 0, 0, tiled=False)]
  transfers between devices with their start and end apart: 5 -> 5, of which waited for: 0 -> 1; matrix products, arithmetic and copies ran while one was open for 36% -> 35% of each run, Pallas kernels for 0% -> 0%
where the time goes in v13:
time: 550 us; the launch traced here: 549 us
  blocking collectives  266 us (48%)
  other arithmetic  192 us (35%)
  Pallas kernels  28.6 us (5%)
  matrix products  26 us (5%)
  waiting for transfers between devices  15.3 us (3%)
  between operations  13.7 us (2%)
  local copies, waits for them, and re-layouts  6.75 us (1%)
    all_to_all x4, blocking collectives, sum_scatter_rows(): lax.all_to_all(x.reshape((n, -1) + x.shape[1:]), axis, 0, 0, tiled=False)  128 us
    another operation x24, other arithmetic, cholesky_and_inverse(): lower = jnp.linalg.cholesky(g, symmetrize_input=False)  99.1 us
    another operation x16, other arithmetic, cholesky_and_inverse(): return (lower, jax.scipy.linalg.solve_triangular(lower, eye, lower=True))  83.8 us
    all_to_all x4, blocking collectives, sum_all(): lax.all_to_all(x.reshape(n, -1), axes, 0, 0, tiled=False)  64.5 us
    all_to_all x4, blocking collectives, sum_all(): lax.all_to_all(jnp.broadcast_to(piece, (n,) + piece.shape), axes, 0, 0, t...  60.9 us
    pallas_call x4, Pallas kernels, apply_tiles(): pl.pallas_call(kernel, grid_spec=spec, out_shape=jax.ShapeDtypeStruct((tr...  28.6 us
    all_gather x1, waiting for transfers between devices, body(): lax.all_gather(probe, 'row', axis=0, tiled=True)  15.2 us
    dot_general x4, matrix products, loop_step(): jnp.dot(image_block, inverse.T, precision=lax.Precision.HIGH, preferred_e...  14.8 us
  transfers between devices with their start and end apart: 5, of which 1 were waited for; matrix products, arithmetic and copies ran while one was open for 35% of the time, Pallas kernels for 0%

profile of v13, /device:TPU:1, one launch (start us, length us, event | category | flops | bytes accessed | tf_op | source)
XLA Modules:
  0.0 549.4 jit_solution(7975940940703486242)
XLA Ops:
  9.8 12.1 %all-gather = f32[8,1,256]{2,1,0:T(1,128)S(1)} all-gather(f32[1,1,256]{2,1,0:T(1,128)} %bitcast.93), channel_id=1, replica_groups=mesh['row'=8,'col'=16] {'row'}, dimensions={0}, use_global_device_ids=true | all-gather | bytes 9216 | tf_op jit(solution)/shard_map/all_gather | solution.py:107
  21.9 15.2 %all-gather.4.cloned.1.call-done = bf16[2048,256]{1,0:T(8,128)(2,1)} async-done(((bf16[256,256]{1,0:T(8,128)(2,1)}), bf16[2048,256]{1,0:T(8,128)(2,1)}) %all-gather.4.cloned.1.call-update) | async-done | bytes 1048592 | tf_op jit(solution)/shard_map/all_gather | solution.py:123
  37.1 501.9 %while.17 = (s32[]{:T(128)}, bf16[2048,256]{1,0:T(8,128)(2,1)}, f32[256,256]{1,0:T(8,128)}, f32[256,256]{1,0:T(8,128)}, f32[256,256]{1,0:T(8,128)}, /*index=5*/s...) while((s32[]{:T(128)}, bf16[2048,256]{1,0:T(8,128)(2,1)}, ...), condition=%wide.wide.region_5.8_spmd, body=%wide.wide.region_0.7_spmd.sunk | while | flops 1161690880 | bytes 26299656 | solution.py:124
  44.3 34.4 %all_to_all.29 = bf16[16,256,256]{2,1,0:T(8,128)(2,1)S(1)} all-to-all(bf16[16,256,256]{2,1,0:T(8,128)(2,1)} %bitcast.89), channel_id=1, replica_groups=mesh['row'=8,'col'=16] {'col'}, dimensions={0} | all-to-all | bytes 4194304 | tf_op jit(solution)/shard_map/while/body/eval_jaxpr/all_to_all | solution.py:84
  80.3 16.5 %all_to_all.30 = f32[128,1,512]{2,1,0:T(1,128)S(1)} all-to-all(f32[128,1,512]{2,1,0:T(1,128)S(1)} %all_to_all.23), channel_id=1, replica_groups=mesh['row'=8,'col'=16] {'row','col'}, dimensions={0} | all-to-all | bytes 524288 | tf_op jit(solution)/shard_map/while/body/eval_jaxpr/all_to_all | solution.py:92
  97.1 15.2 %all_to_all.31 = f32[128,1,512]{2,1,0:T(1,128)S(1)} all-to-all(f32[128,1,512]{2,1,0:T(1,128)S(1)} %broadcast_in_dim.14), channel_id=1, replica_groups=mesh['row'=8,'col'=16] {'row','col'}, dimensions={0} | all-to-all | bytes 524288 | tf_op jit(solution)/shard_map/while/body/eval_jaxpr/all_to_all | solution.py:93
  113.1 11.7 %cholesky.173 = f32[128,128]{1,0:T(8,128)S(1)} custom-call(f32[128,128]{1,0:T(8,128)S(1)} %slice.28), custom_call_target="Cholesky" | custom-call | tf_op jit(solution)/shard_map/while/body/eval_jaxpr/jit(cholesky)/cholesky | solution.py:34
  126.1 9.8 %custom-call.15 = f32[1,128,128]{1,2,0:T(8,128)S(1)} custom-call(f32[1,128,128]{2,1,0:T(8,128)S(1)} %get-tuple-element.223), custom_call_target="InvertDiagBlocksLowerTriangular" | custom-call | tf_op jit(solution)/shard_map/while/body/eval_jaxpr/jit(_solve_triangular)/triangular_solve | solution.py:36
  136.9 11.7 %cholesky.174 = f32[128,128]{1,0:T(8,128)S(1)} custom-call(f32[128,128]{1,0:T(8,128)S(1)} %convolution_subtract_fusion.3), custom_call_target="Cholesky" | custom-call | tf_op jit(solution)/shard_map/while/body/eval_jaxpr/jit(cholesky)/cholesky | solution.py:34
  172.4 31.4 %all_to_all.29 = bf16[16,256,256]{2,1,0:T(8,128)(2,1)S(1)} all-to-all(bf16[16,256,256]{2,1,0:T(8,128)(2,1)} %bitcast.89), channel_id=1, replica_groups=mesh['row'=8,'col'=16] {'col'}, dimensions={0} | all-to-all | bytes 4194304 | tf_op jit(solution)/shard_map/while/body/eval_jaxpr/all_to_all | solution.py:84
  205.4 16.0 %all_to_all.30 = f32[128,1,512]{2,1,0:T(1,128)S(1)} all-to-all(f32[128,1,512]{2,1,0:T(1,128)S(1)} %all_to_all.23), channel_id=1, replica_groups=mesh['row'=8,'col'=16] {'row','col'}, dimensions={0} | all-to-all | bytes 524288 | tf_op jit(solution)/shard_map/while/body/eval_jaxpr/all_to_all | solution.py:92
  221.7 15.2 %all_to_all.31 = f32[128,1,512]{2,1,0:T(1,128)S(1)} all-to-all(f32[128,1,512]{2,1,0:T(1,128)S(1)} %broadcast_in_dim.14), channel_id=1, replica_groups=mesh['row'=8,'col'=16] {'row','col'}, dimensions={0} | all-to-all | bytes 524288 | tf_op jit(solution)/shard_map/while/body/eval_jaxpr/all_to_all | solution.py:93
  237.7 11.7 %cholesky.173 = f32[128,128]{1,0:T(8,128)S(1)} custom-call(f32[128,128]{1,0:T(8,128)S(1)} %slice.28), custom_call_target="Cholesky" | custom-call | tf_op jit(solution)/shard_map/while/body/eval_jaxpr/jit(cholesky)/cholesky | solution.py:34
  261.5 11.7 %cholesky.174 = f32[128,128]{1,0:T(8,128)S(1)} custom-call(f32[128,128]{1,0:T(8,128)S(1)} %convolution_subtract_fusion.3), custom_call_target="Cholesky" | custom-call | tf_op jit(solution)/shard_map/while/body/eval_jaxpr/jit(cholesky)/cholesky | solution.py:34
  296.9 31.4 %all_to_all.29 = bf16[16,256,256]{2,1,0:T(8,128)(2,1)S(1)} all-to-all(bf16[16,256,256]{2,1,0:T(8,128)(2,1)} %bitcast.89), channel_id=1, replica_groups=mesh['row'=8,'col'=16] {'col'}, dimensions={0} | all-to-all | bytes 4194304 | tf_op jit(solution)/shard_map/while/body/eval_jaxpr/all_to_all | solution.py:84
  330.0 16.0 %all_to_all.30 = f32[128,1,512]{2,1,0:T(1,128)S(1)} all-to-all(f32[128,1,512]{2,1,0:T(1,128)S(1)} %all_to_all.23), channel_id=1, replica_groups=mesh['row'=8,'col'=16] {'row','col'}, dimensions={0} | all-to-all | bytes 524288 | tf_op jit(solution)/shard_map/while/body/eval_jaxpr/all_to_all | solution.py:92
  346.3 15.2 %all_to_all.31 = f32[128,1,512]{2,1,0:T(1,128)S(1)} all-to-all(f32[128,1,512]{2,1,0:T(1,128)S(1)} %broadcast_in_dim.14), channel_id=1, replica_groups=mesh['row'=8,'col'=16] {'row','col'}, dimensions={0} | all-to-all | bytes 524288 | tf_op jit(solution)/shard_map/while/body/eval_jaxpr/all_to_all | solution.py:93
  362.3 11.7 %cholesky.173 = f32[128,128]{1,0:T(8,128)S(1)} custom-call(f32[128,128]{1,0:T(8,128)S(1)} %slice.28), custom_call_target="Cholesky" | custom-call | tf_op jit(solution)/shard_map/while/body/eval_jaxpr/jit(cholesky)/cholesky | solution.py:34
  386.1 11.7 %cholesky.174 = f32[128,128]{1,0:T(8,128)S(1)} custom-call(f32[128,128]{1,0:T(8,128)S(1)} %convolution_subtract_fusion.3), custom_call_target="Cholesky" | custom-call | tf_op jit(solution)/shard_map/while/body/eval_jaxpr/jit(cholesky)/cholesky | solution.py:34
  421.5 31.4 %all_to_all.29 = bf16[16,256,256]{2,1,0:T(8,128)(2,1)S(1)} all-to-all(bf16[16,256,256]{2,1,0:T(8,128)(2,1)} %bitcast.89), channel_id=1, replica_groups=mesh['row'=8,'col'=16] {'col'}, dimensions={0} | all-to-all | bytes 4194304 | tf_op jit(solution)/shard_map/while/body/eval_jaxpr/all_to_all | solution.py:84
  454.6 16.0 %all_to_all.30 = f32[128,1,512]{2,1,0:T(1,128)S(1)} all-to-all(f32[128,1,512]{2,1,0:T(1,128)S(1)} %all_to_all.23), channel_id=1, replica_groups=mesh['row'=8,'col'=16] {'row','col'}, dimensions={0} | all-to-all | bytes 524288 | tf_op jit(solution)/shard_map/while/body/eval_jaxpr/all_to_all | solution.py:92
  470.9 15.2 %all_to_all.31 = f32[128,1,512]{2,1,0:T(1,128)S(1)} all-to-all(f32[128,1,512]{2,1,0:T(1,128)S(1)} %broadcast_in_dim.14), channel_id=1, replica_groups=mesh['row'=8,'col'=16] {'row','col'}, dimensions={0} | all-to-all | bytes 524288 | tf_op jit(solution)/shard_map/while/body/eval_jaxpr/all_to_all | solution.py:93
  486.9 11.7 %cholesky.173 = f32[128,128]{1,0:T(8,128)S(1)} custom-call(f32[128,128]{1,0:T(8,128)S(1)} %slice.28), custom_call_target="Cholesky" | custom-call | tf_op jit(solution)/shard_map/while/body/eval_jaxpr/jit(cholesky)/cholesky | solution.py:34
  510.7 11.7 %cholesky.174 = f32[128,128]{1,0:T(8,128)S(1)} custom-call(f32[128,128]{1,0:T(8,128)S(1)} %convolution_subtract_fusion.3), custom_call_target="Cholesky" | custom-call | tf_op jit(solution)/shard_map/while/body/eval_jaxpr/jit(cholesky)/cholesky | solution.py:34
  (159 shorter events, 150.4 us)
Async XLA Ops:
  7.2 29.9 %all-gather.4.cloned.1.call-start = ((), (), s32[]{:S(2)}) async-start(), calls=%async_computation.3 | async-start | bytes 1179648 | tf_op jit(solution)/shard_map/all_gather | solution.py:123
  9.7 27.4 %copy-start.2 = (s32[32,1,8]{2,0,1:T(8,128)}, s32[32,1,8]{2,0,1:T(8,128)S(1)}, u32[]{:S(2)}) copy-start(s32[32,1,8]{2,0,1:T(8,128)S(1)} %copy.20) | copy-start | bytes 3076
  37.1 124.4 %all-gather.6.cloned.1.call-start = ((), (), s32[]{:S(2)}) async-start(), calls=%async_computation.4 | async-start | bytes 2359296 | tf_op jit(solution)/shard_map/while/body/eval_jaxpr/all_gather | solution.py:116
  78.6 0.7 copy-start.3
  79.4 33.6 %copy-start = (f32[256,256]{1,0:T(8,128)}, f32[256,256]{1,0:T(8,128)S(1)}, u32[]{:S(2)}) copy-start(f32[256,256]{1,0:T(8,128)S(1)} %broadcast_multiply_fusion.3) | copy-start | bytes 786436 | tf_op jit(solution)/shard_map/while
  161.5 3.7 copy-start.1
  165.2 120.9 %all-gather.6.cloned.1.call-start = ((), (), s32[]{:S(2)}) async-start(), calls=%async_computation.4 | async-start | bytes 2359296 | tf_op jit(solution)/shard_map/while/body/eval_jaxpr/all_gather | solution.py:116
  203.7 0.7 copy-start.3
  204.5 33.1 %copy-start = (f32[256,256]{1,0:T(8,128)}, f32[256,256]{1,0:T(8,128)S(1)}, u32[]{:S(2)}) copy-start(f32[256,256]{1,0:T(8,128)S(1)} %broadcast_multiply_fusion.3) | copy-start | bytes 786436 | tf_op jit(solution)/shard_map/while
  286.1 3.7 copy-start.1
  289.8 120.9 %all-gather.6.cloned.1.call-start = ((), (), s32[]{:S(2)}) async-start(), calls=%async_computation.4 | async-start | bytes 2359296 | tf_op jit(solution)/shard_map/while/body/eval_jaxpr/all_gather | solution.py:116
  328.3 0.7 copy-start.3
  329.1 33.1 %copy-start = (f32[256,256]{1,0:T(8,128)}, f32[256,256]{1,0:T(8,128)S(1)}, u32[]{:S(2)}) copy-start(f32[256,256]{1,0:T(8,128)S(1)} %broadcast_multiply_fusion.3) | copy-start | bytes 786436 | tf_op jit(solution)/shard_map/while
  410.7 3.7 copy-start.1
  414.4 120.9 %all-gather.6.cloned.1.call-start = ((), (), s32[]{:S(2)}) async-start(), calls=%async_computation.4 | async-start | bytes 2359296 | tf_op jit(solution)/shard_map/while/body/eval_jaxpr/all_gather | solution.py:116
  452.9 0.7 copy-start.3
  453.7 33.1 %copy-start = (f32[256,256]{1,0:T(8,128)}, f32[256,256]{1,0:T(8,128)S(1)}, u32[]{:S(2)}) copy-start(f32[256,256]{1,0:T(8,128)S(1)} %broadcast_multiply_fusion.3) | copy-start | bytes 786436 | tf_op jit(solution)/shard_map/while
  535.3 3.7 copy-start.1
Sparse Core Ops, SparseCore 0:
  10.3 26.7 all-gather.3
  113.2 21.4 all-gather.5
  237.8 21.4 all-gather.5
  362.4 21.4 all-gather.5
  487.0 21.4 all-gather.5
